TPU v7x, 1024 devices: a whole 8x8x8 slice. The times are simulated.
1024 devices in a mesh: seq: 64 (over y, x), head: 16 (over z, core).
Axes of the slice: x: 8, y: 8, z: 8, core: 2. Of those that a mesh axis runs over, the one named last changes fastest.
Arguments:
- queries: bfloat16 [8192, 8192], P('seq', 'head'), may hold values from -6 to 6, as said below
- keys: bfloat16 [8192, 1024], P('seq'), may hold values from -6 to 6, as said below
- values: bfloat16 [8192, 1024], P('seq'), may hold values from -6 to 6
- residual: bfloat16 [8192, 8192], P('seq', 'head'), may hold values from -50 to 50
- norm_gain: float32 [8192], replicated, may hold values from 0.25 to 1.75
- block_pos: int32 [1, 64], replicated, may hold values from 0 to 63, each once within a row
- doc_offset: int32 [1, 64], replicated, may hold values from 1 to 128, as said below
Outputs:
- attn_out: bfloat16 [8192, 8192], P('seq', 'head')
- r_factor: float32 [64, 128, 128], P('head')
- whitened: float32 [8192, 8192], P('seq', 'head')
Inputs may be any that keep to these rules, and one draw needn't show every extreme that they name: queries may hold rows of large entries. keys may hold rows of large entries. `block_pos`: in each sequence every sequence block is stored exactly once. A document begins at token doc_offset[c, b] of sequence block b when that value is under 128; the first document begins at position 0.
All inputs are finite; a program needn't handle non-finite values.
Results may differ from a plain program's by a relative error of at most 0.0045.
Values may be sent and summed in bfloat16 or wider, within the bound.
No kernel may reach another device: no remote copies, remote signals or barrier semaphores. Data moves between devices by JAX's collectives and lax.ppermute only.
A program may use at most 32 MiB of HBM per device.

v0:
```python
import math

import jax
import jax.numpy as jnp
from jax import lax
from jax.sharding import PartitionSpec as P

HEADS = 64
KVH = 8
HD = 128
BLOCK = 128
COPIES = 1
WIDTH = 8192


EPSILON = 1e-05


def side_by_side(arrays, axis, dim, along):
    both = jnp.concatenate(arrays, axis=along)
    whole, at, done = (lax.all_gather(both, axis, axis=dim, tiled=True), 0, [])
    for a in arrays:
        done.append(lax.slice_in_dim(whole, at, at + a.shape[along], axis=along))
        at += a.shape[along]
    return tuple(done)


def copy_for_each(shard, axis):
    count = lax.axis_size(axis)
    return lax.all_to_all(
        jnp.broadcast_to(shard[None], (count, *shard.shape)), axis, 0, 0, tiled=True
    )


def over_copies(shard, axis):
    everything = copy_for_each(shard, axis)
    return jnp.sum(everything, axis=0)


def positions_and_docs(block_pos, doc_offset):
    block_total = block_pos.shape[0]
    doc_flags = (doc_offset < BLOCK).astype(jnp.int32)
    starts_before = jnp.cumsum(doc_flags) - doc_flags
    matches = block_pos[:, None] == jnp.arange(block_total, dtype=jnp.int32)[None, :]
    start_count = jnp.sum(jnp.where(matches, starts_before[None, :], 0), axis=1)
    offsets = jnp.sum(jnp.where(matches, doc_offset[None, :], 0), axis=1)
    within = jnp.arange(BLOCK, dtype=jnp.int32)
    seq_pos = (block_pos[:, None] * BLOCK + within[None, :]).reshape(-1)
    doc_id = (
        start_count[:, None] + (within[None, :] >= offsets[:, None]).astype(jnp.int32)
    ).reshape(-1)
    return (seq_pos, doc_id)


def gram_of(matrix):
    return jnp.einsum("hnc,hnd->hcd", matrix, matrix, precision=lax.Precision.HIGHEST)


def local(queries, keys, values, residual, norm_gain, block_pos, doc_offset):
    row_count = queries.shape[0]
    head_count = queries.shape[1] // HD
    group_size = HEADS // KVH
    share_count = max(1, head_count // group_size)
    per_share = head_count // share_count
    total_rows = row_count * lax.axis_size("seq")
    global_first = lax.axis_index("head") * head_count
    copy_index = global_first // HEADS
    first_head = global_first % HEADS
    first_share = first_head // group_size
    key_start = copy_index * (KVH * HD) + first_share * HD
    key_cols = lax.dynamic_slice_in_dim(keys, key_start, share_count * HD, 1)
    value_cols = lax.dynamic_slice_in_dim(values, key_start, share_count * HD, 1)
    own_blocks = lax.dynamic_index_in_dim(block_pos, copy_index, 0, keepdims=False)
    own_offsets = lax.dynamic_index_in_dim(doc_offset, copy_index, 0, keepdims=False)
    gain_cols = lax.dynamic_slice_in_dim(norm_gain, first_head * HD, head_count * HD)
    seq_pos, doc_id = positions_and_docs(own_blocks, own_offsets)
    first_row = lax.axis_index("seq") * row_count
    own_pos = lax.dynamic_slice_in_dim(seq_pos, first_row, row_count)
    own_doc = lax.dynamic_slice_in_dim(doc_id, first_row, row_count)
    query_heads = queries.reshape(row_count, share_count, per_share, HD)
    score_scale = 1.0 / math.sqrt(HD)

    def attend_block(state_now, key_piece, value_piece, first_key):
        length = key_piece.shape[0]
        key_pos = lax.dynamic_slice_in_dim(seq_pos, first_key, length)
        key_doc = lax.dynamic_slice_in_dim(doc_id, first_key, length)
        seen = (key_pos[None, :] <= own_pos[:, None]) & (key_doc[None, :] == own_doc[:, None])

        def accumulate(state_inner):
            run_max, run_total, run_acc = state_inner
            key_heads = key_piece.reshape(length, share_count, HD)
            value_heads = value_piece.reshape(length, share_count, HD)
            scores = (
                jnp.einsum(
                    "rkgd,nkd->kgrn", query_heads, key_heads, preferred_element_type=jnp.float32
                )
                * score_scale
            )
            scores = jnp.where(seen[None, None], scores, -jnp.inf)
            new_max = jnp.maximum(run_max, jnp.max(scores, axis=3))
            factor = jnp.exp(run_max - new_max)
            expo = jnp.exp(scores - new_max[..., None])
            new_total = run_total * factor + jnp.sum(expo, axis=3)
            partial_value = jnp.einsum(
                "kgrn,nkd->kgrd",
                expo.astype(jnp.bfloat16),
                value_heads,
                preferred_element_type=jnp.float32,
            )
            new_acc = run_acc * factor[..., None] + partial_value
            return (new_max, new_total, new_acc)

        def unchanged(state_inner):
            return state_inner

        return lax.cond(jnp.any(seen), accumulate, unchanged, state_now)

    start_state = (
        jnp.full((share_count, per_share, row_count), -1e30, jnp.float32),
        jnp.zeros((share_count, per_share, row_count), jnp.float32),
        jnp.zeros((share_count, per_share, row_count, HD), jnp.float32),
    )
    key_piece, value_piece = side_by_side((key_cols, value_cols), "seq", 0, 1)
    length = key_piece.shape[0]
    step_rows = math.gcd(length, 1024)

    def advance(step_index, state_inner):
        begin_row = step_index * step_rows
        key_part = lax.dynamic_slice_in_dim(key_piece, begin_row, step_rows, 0)
        value_part = lax.dynamic_slice_in_dim(value_piece, begin_row, step_rows, 0)
        return attend_block(state_inner, key_part, value_part, begin_row)

    final_max, final_total, final_acc = lax.fori_loop(0, length // step_rows, advance, start_state)
    output = final_acc / final_total[..., None]
    attn_out = (
        jnp.transpose(output, (2, 0, 1, 3)).reshape(row_count, head_count * HD).astype(jnp.bfloat16)
    )
    mixed = attn_out.astype(jnp.float32) + residual.astype(jnp.float32)
    local_squares = jnp.sum(mixed * mixed, axis=1)
    slot_mask = jnp.arange(COPIES, dtype=jnp.int32) == copy_index
    slotted = jnp.where(slot_mask[:, None], local_squares[None, :], 0.0)
    summed = over_copies(slotted, "head")
    square_sum = lax.dynamic_index_in_dim(summed, copy_index, 0, keepdims=False)
    normed = mixed * lax.rsqrt(square_sum[:, None] / WIDTH + EPSILON) * gain_cols[None, :]
    blocks = normed.reshape(row_count, head_count, HD)
    head_rows = jnp.transpose(blocks, (1, 0, 2))
    gram_sum = lax.psum(gram_of(head_rows), "seq")
    lower_factor = jnp.linalg.cholesky(gram_sum)
    r_factor = jnp.transpose(lower_factor, (0, 2, 1)) / math.sqrt(total_rows)
    solved = jax.scipy.linalg.solve_triangular(
        lower_factor, jnp.transpose(blocks, (1, 2, 0)), lower=True
    )
    whitened = jnp.transpose(solved, (2, 0, 1)).reshape(row_count, head_count * HD) * math.sqrt(
        total_rows
    )
    return (attn_out, r_factor, whitened)


def solution(mesh):
    return jax.shard_map(
        local,
        mesh=mesh,
        in_specs=(
            P("seq", "head"),
            P("seq", None),
            P("seq", None),
            P("seq", "head"),
            P(),
            P(),
            P(),
        ),
        out_specs=(P("seq", "head"), P("head", None, None), P("seq", "head")),
        check_vma=False,
    )
```

profile of v0, /device:TPU:14, one launch (start us, length us, event | category | flops | bytes accessed | tf_op | source)
XLA Modules:
  0.0 422.1 jit_solution(1722447071533349287)
XLA Ops:
  12.1 1.0 copy.45
  13.2 101.3 %all-gather.2.cloned.1.call-done = bf16[8192,256]{1,0:T(8,128)(2,1)} async-done(((bf16[128,256]{1,0:T(8,128)(2,1)}), bf16[8192,256]{1,0:T(8,128)(2,1)}) %all-gather.2.cloned.1.call-update) | async-done | bytes 4194320 | tf_op jit(solution)/shard_map/all_gather | solution.py:21
  114.5 3.8 fusion.19
  118.4 25.2 %while.17 = (s32[]{:T(128)}, f32[1,4,128]{2,1,0:T(4,128)S(1)}, f32[1,4,128]{2,1,0:T(4,128)S(1)}, f32[1,4,128,128]{3,2,1,0:T(8,128)S(1)}, s32[8192]{0:T(1024)S(1)...) while((s32[]{:T(128)}, f32[1,4,128]{2,1,0:T(4,128)S(1)}, ...), condition=%wide.region_9.10_spmd, body=%wide.region_3.9_spmd.sunk | while | flops 272762368 | bytes 7792453 | solution.py:133
  118.4 1.0 fusion.25
  120.0 2.3 conditional.2
  120.1 1.4 fusion.18
  122.4 1.0 fusion.25
  124.1 2.3 conditional.2
  124.1 1.4 fusion.18
  128.1 2.3 conditional.2
  128.1 1.4 fusion.18
  132.1 2.3 conditional.2
  132.1 1.4 fusion.18
  137.8 2.3 conditional.2
  137.8 1.4 fusion.18
  144.6 8.2 %all-to-all-start = ((f32[16,1,128]{2,1,0:T(1,128)}), f32[16,1,128]{2,1,0:T(1,128)S(1)}, u32[]{:S(2)}, u32[]{:S(2)}) async-start(f32[16,1,128]{2,1,0:T(1,128)} %broadcast_in_dim.116), calls=%async_computation | async-start | bytes 16384 | tf_op jit(solution)/shard_map/all_to_all | solution.py:30
  153.7 6.7 %all-to-all-done = f32[16,1,128]{2,1,0:T(1,128)S(1)} async-done(((f32[16,1,128]{2,1,0:T(1,128)}), f32[16,1,128]{2,1,0:T(1,128)S(1)}, u32[]{:S(2)}, u32[]{:S(2)}) %all-to-all-start) | async-done | bytes 8224 | tf_op jit(solution)/shard_map/all_to_all | solution.py:30
  160.6 1.4 fusion.20
  162.1 162.3 %all-reduce.2.cloned.1.call-done = f32[4,128,128]{1,2,0:T(8,128)} async-done(((f32[4,128,128]{1,2,0:T(8,128)}), f32[4,128,128]{1,2,0:T(8,128)}) %all-reduce.2.cloned.1.call-update) | async-done | bytes 262160 | tf_op jit(solution)/shard_map/psum | solution.py:147
  324.4 1.1 copy.52
  325.5 1.0 fusion.15
  326.5 46.9 %custom-call.8 = f32[4,128,128]{2,1,0:T(8,128)S(1)} custom-call(f32[4,128,128]{2,1,0:T(8,128)S(1)} %fusion.15), custom_call_target="Cholesky" | custom-call | tf_op jit(solution)/shard_map/jit(cholesky)/cholesky | solution.py:148
  373.7 39.3 %custom-call.9 = f32[4,1,128,128]{2,3,1,0:T(8,128)S(1)} custom-call(f32[4,1,128,128]{3,2,1,0:T(8,128)S(1)} %get-tuple-element.349), custom_call_target="InvertDiagBlocksLowerTriangular" | custom-call | tf_op jit(solution)/shard_map/jit(_solve_triangular)/vmap()/triangular_solve | solution.py:150
  (90 shorter events, 20.1 us)
Async XLA Ops:
  7.2 107.3 %all-gather.2.cloned.1.call-start = ((), (), s32[]{:S(2)}) async-start(), calls=%async_computation.1 | async-start | bytes 4259840 | tf_op jit(solution)/shard_map/all_gather | solution.py:21
  118.4 25.5 %copy-start = (bf16[128,512]{1,0:T(8,128)(2,1)S(1)}, bf16[128,512]{1,0:T(8,128)(2,1)}, u32[]{:S(2)}) copy-start(bf16[128,512]{1,0:T(8,128)(2,1)} %param.14) | copy-start | bytes 393220
  144.0 229.7 %copy-start.1 = (bf16[128,512]{1,0:T(8,128)(2,1)}, bf16[128,512]{1,0:T(8,128)(2,1)S(1)}, u32[]{:S(2)}) copy-start(bf16[128,512]{1,0:T(8,128)(2,1)S(1)} %get-tuple-element.344) | copy-start | bytes 393220
  144.6 15.7 %all-to-all-start = ((f32[16,1,128]{2,1,0:T(1,128)}), f32[16,1,128]{2,1,0:T(1,128)S(1)}, u32[]{:S(2)}, u32[]{:S(2)}) async-start(f32[16,1,128]{2,1,0:T(1,128)} %broadcast_in_dim.116), calls=%async_computation | async-start | bytes 16384 | tf_op jit(solution)/shard_map/all_to_all | solution.py:30
  152.8 171.6 %all-reduce.2.cloned.1.call-start = ((), (), s32[]{:S(2)}) async-start(), calls=%async_computation.2 | async-start | bytes 524288 | tf_op jit(solution)/shard_map/psum | solution.py:147
Sparse Core Ops, SparseCore 0:
  12.8 101.6 all-gather.1
  162.1 162.2 all-reduce.1
where the time goes:
time: 424 us; the launch traced here: 422 us
  waiting for transfers between devices  270 us (64%)
  other arithmetic  101 us (24%)
  between operations  14.3 us (3%)
  matrix products  11.8 us (3%)
  local copies, waits for them, and re-layouts  10.5 us (2%)
  starting transfers between devices  8.29 us (2%)
  loops' own time  5.82 us (1%)
    psum x1, waiting for transfers between devices, local(): gram_sum = lax.psum(gram_of(head_rows), 'seq')  162 us
    all_gather x1, waiting for transfers between devices, side_by_side(): whole, at, done = (lax.all_gather(both, axis, axis=dim, tiled=True), 0, [])  101 us
    another operation x4, other arithmetic, local(): lower_factor = jnp.linalg.cholesky(gram_sum)  47.1 us
    another operation x2, other arithmetic, local(): jax.scipy.linalg.solve_triangular(lower_factor, jnp.transpose(blocks, (1,...  39.4 us
  transfers between devices with their start and end apart: 3, of which 3 were waited for; matrix products, arithmetic and copies ran while one was open for 1% of the time, Pallas kernels for 0%

commit v1 on v0

--- a/solution.py
+++ b/solution.py
@@ -56,14 +56,18 @@
     return jnp.einsum("hnc,hnd->hcd", matrix, matrix, precision=lax.Precision.HIGHEST)
 
 
+SEQ = ("y", "x")
+HEAD = ("z", "c")
+
+
 def local(queries, keys, values, residual, norm_gain, block_pos, doc_offset):
     row_count = queries.shape[0]
     head_count = queries.shape[1] // HD
     group_size = HEADS // KVH
     share_count = max(1, head_count // group_size)
     per_share = head_count // share_count
-    total_rows = row_count * lax.axis_size("seq")
-    global_first = lax.axis_index("head") * head_count
+    total_rows = row_count * lax.axis_size(SEQ)
+    global_first = lax.axis_index(HEAD) * head_count
     copy_index = global_first // HEADS
     first_head = global_first % HEADS
     first_share = first_head // group_size
@@ -74,7 +78,7 @@
     own_offsets = lax.dynamic_index_in_dim(doc_offset, copy_index, 0, keepdims=False)
     gain_cols = lax.dynamic_slice_in_dim(norm_gain, first_head * HD, head_count * HD)
     seq_pos, doc_id = positions_and_docs(own_blocks, own_offsets)
-    first_row = lax.axis_index("seq") * row_count
+    first_row = lax.axis_index(SEQ) * row_count
     own_pos = lax.dynamic_slice_in_dim(seq_pos, first_row, row_count)
     own_doc = lax.dynamic_slice_in_dim(doc_id, first_row, row_count)
     query_heads = queries.reshape(row_count, share_count, per_share, HD)
@@ -120,7 +124,12 @@
         jnp.zeros((share_count, per_share, row_count), jnp.float32),
         jnp.zeros((share_count, per_share, row_count, HD), jnp.float32),
     )
-    key_piece, value_piece = side_by_side((key_cols, value_cols), "seq", 0, 1)
+    core = lax.axis_index("c")
+    mine = jnp.where(core == 0, key_cols, value_cols)
+    gathered = lax.all_gather(lax.all_gather(mine, "x", axis=0, tiled=True), "y", axis=0, tiled=True)
+    other = lax.ppermute(gathered, "c", perm=[(0, 1), (1, 0)])
+    key_piece = jnp.where(core == 0, gathered, other)
+    value_piece = jnp.where(core == 0, other, gathered)
     length = key_piece.shape[0]
     step_rows = math.gcd(length, 1024)
 
@@ -139,12 +148,12 @@
     local_squares = jnp.sum(mixed * mixed, axis=1)
     slot_mask = jnp.arange(COPIES, dtype=jnp.int32) == copy_index
     slotted = jnp.where(slot_mask[:, None], local_squares[None, :], 0.0)
-    summed = over_copies(slotted, "head")
+    summed = over_copies(slotted, HEAD)
     square_sum = lax.dynamic_index_in_dim(summed, copy_index, 0, keepdims=False)
     normed = mixed * lax.rsqrt(square_sum[:, None] / WIDTH + EPSILON) * gain_cols[None, :]
     blocks = normed.reshape(row_count, head_count, HD)
     head_rows = jnp.transpose(blocks, (1, 0, 2))
-    gram_sum = lax.psum(gram_of(head_rows), "seq")
+    gram_sum = lax.psum(lax.optimization_barrier(lax.psum(gram_of(head_rows), "x")), "y")
     lower_factor = jnp.linalg.cholesky(gram_sum)
     r_factor = jnp.transpose(lower_factor, (0, 2, 1)) / math.sqrt(total_rows)
     solved = jax.scipy.linalg.solve_triangular(
@@ -157,18 +166,23 @@
 
 
 def solution(mesh):
+    seq_size, head_size = mesh.devices.shape
+    side = math.isqrt(seq_size)
+    grid = jax.sharding.Mesh(
+        mesh.devices.reshape(side, seq_size // side, head_size // 2, 2), ("y", "x", "z", "c")
+    )
     return jax.shard_map(
         local,
-        mesh=mesh,
+        mesh=grid,
         in_specs=(
-            P("seq", "head"),
-            P("seq", None),
-            P("seq", None),
-            P("seq", "head"),
+            P(SEQ, HEAD),
+            P(SEQ, None),
+            P(SEQ, None),
+            P(SEQ, HEAD),
             P(),
             P(),
             P(),
         ),
-        out_specs=(P("seq", "head"), P("head", None, None), P("seq", "head")),
+        out_specs=(P(SEQ, HEAD), P(HEAD, None, None), P(SEQ, HEAD)),
         check_vma=False,
     )

time: 424 us -> 414 us (0.976)
  waiting for transfers between devices: 270 us -> 228 us
  blocking collectives: 0 us -> 36.6 us
  local copies, waits for them, and re-layouts: 10.5 us -> 5.9 us
    all_gather x1, waiting for transfers between devices: 101 us -> 47.6 us  [local(): lax.all_gather(lax.all_gather(mine, 'x', axis=0, tiled=True), 'y', axis=0...]
    all_gather x0 -> x1, blocking collectives: none -> 36.6 us  [local(): lax.all_gather(mine, 'x', axis=0, tiled=True)]
    psum x1 -> x2, waiting for transfers between devices: 162 us -> 174 us  [the longest x1 87.8 us: local(): lax.psum(gram_of(head_rows), 'x')]
    select_n x0 -> x2, other arithmetic: none -> 4.66 us  [the longest x1 3.85 us: local(): value_piece = jnp.where(core == 0, other, gathered)]
  transfers between devices with their start and end apart: 3 -> 5, of which waited for: 3 -> 4; matrix products, arithmetic and copies ran while one was open for 1% -> 1% of each run, Pallas kernels for 0% -> 0%
where the time goes in v1:
time: 414 us; the launch traced here: 413 us
  waiting for transfers between devices  228 us (55%)
  other arithmetic  104 us (25%)
  blocking collectives  36.6 us (9%)
  between operations  14 us (3%)
  starting transfers between devices  10.4 us (3%)
  matrix products  7.87 us (2%)
  local copies, waits for them, and re-layouts  5.9 us (1%)
  loops' own time  5.76 us (1%)
    psum x1, waiting for transfers between devices, local(): lax.psum(gram_of(head_rows), 'x')  87.8 us
    psum x1, waiting for transfers between devices, local(): lax.psum(lax.optimization_barrier(lax.psum(gram_of(head_rows), 'x')), 'y')  85.9 us
    all_gather x1, waiting for transfers between devices, local(): lax.all_gather(lax.all_gather(mine, 'x', axis=0, tiled=True), 'y', axis=0...  47.6 us
    another operation x4, other arithmetic, local(): lower_factor = jnp.linalg.cholesky(gram_sum)  47.1 us
    another operation x2, other arithmetic, local(): jax.scipy.linalg.solve_triangular(lower_factor, jnp.transpose(blocks, (1,...  39.4 us
    all_gather x1, blocking collectives, local(): lax.all_gather(mine, 'x', axis=0, tiled=True)  36.6 us
    all_to_all x1, starting transfers between devices, copy_for_each(): lax.all_to_all(jnp.broadcast_to(shard[None], (count, *shard.shape)), axis...  8.32 us
  transfers between devices with their start and end apart: 5, of which 4 were waited for; matrix products, arithmetic and copies ran while one was open for 1% of the time, Pallas kernels for 0%

profile of v1, /device:TPU:14, one launch (start us, length us, event | category | flops | bytes accessed | tf_op | source)
XLA Modules:
  0.0 413.0 jit_solution(13710554941562860274)
XLA Ops:
  8.1 36.6 %all_gather.6 = bf16[1024,128]{1,0:T(8,128)(2,1)} all-gather(bf16[128,128]{1,0:T(8,128)(2,1)S(1)} %dynamic-slice_select_fusion), channel_id=1, replica_groups=mesh['y'=8,'x'=8,'z'=8,'c'=2] {'x'}, dimensions={0}, use_global_device_ids=true | all-gather | bytes 294912 | tf_op jit(solution)/shard_map/all_gather | solution.py:129
  44.7 47.6 %all-gather.2.cloned.1.call-done = bf16[8192,128]{1,0:T(8,128)(2,1)} async-done(((bf16[1024,128]{1,0:T(8,128)(2,1)}), bf16[8192,128]{1,0:T(8,128)(2,1)}) %all-gather.2.cloned.1.call-update) | async-done | bytes 2097168 | tf_op jit(solution)/shard_map/all_gather | solution.py:129
  92.3 1.9 collective-permute-start
  97.6 1.0 copy.45
  98.7 3.8 broadcast_select_fusion
  102.6 20.6 %while.17 = (s32[]{:T(128)}, f32[1,4,128]{2,1,0:T(4,128)S(1)}, f32[1,4,128]{2,1,0:T(4,128)S(1)}, f32[1,4,128,128]{3,2,1,0:T(8,128)S(1)}, s32[8192]{0:T(1024)S(1)...) while((s32[]{:T(128)}, f32[1,4,128]{2,1,0:T(4,128)S(1)}, ...), condition=%wide.region_9.10_spmd, body=%wide.region_3.9_spmd.sunk | while | flops 272762368 | bytes 7792453 | solution.py:142
  102.7 1.0 fusion.24
  104.3 2.3 conditional.2
  104.3 1.4 fusion.18
  106.7 1.0 fusion.24
  108.3 2.3 conditional.2
  108.4 1.4 fusion.18
  110.7 1.0 fusion.24
  120.9 2.3 conditional.2
  120.9 1.4 fusion.18
  124.3 8.3 %all-to-all-start = ((f32[16,1,128]{2,1,0:T(1,128)}), f32[16,1,128]{2,1,0:T(1,128)S(1)}, u32[]{:S(2)}, u32[]{:S(2)}) async-start(f32[16,1,128]{2,1,0:T(1,128)} %broadcast_in_dim.116), calls=%async_computation | async-start | bytes 16384 | tf_op jit(solution)/shard_map/all_to_all | solution.py:30
  133.4 6.7 %all-to-all-done = f32[16,1,128]{2,1,0:T(1,128)S(1)} async-done(((f32[16,1,128]{2,1,0:T(1,128)}), f32[16,1,128]{2,1,0:T(1,128)S(1)}, u32[]{:S(2)}, u32[]{:S(2)}) %all-to-all-start) | async-done | bytes 8224 | tf_op jit(solution)/shard_map/all_to_all | solution.py:30
  140.4 1.4 fusion.19
  141.8 87.8 %all-reduce.3.cloned.1.call-done = f32[4,128,128]{1,2,0:T(8,128)} async-done(((f32[4,128,128]{1,2,0:T(8,128)}), f32[4,128,128]{1,2,0:T(8,128)}) %all-reduce.3.cloned.1.call-update) | async-done | bytes 262160 | tf_op jit(solution)/shard_map/psum | solution.py:156
  229.7 85.9 %all-reduce.5.cloned.1.call-done = f32[4,128,128]{1,2,0:T(8,128)} async-done(((f32[4,128,128]{1,2,0:T(8,128)}), f32[4,128,128]{1,2,0:T(8,128)}) %all-reduce.5.cloned.1.call-update) | async-done | bytes 262160 | tf_op jit(solution)/shard_map/psum | solution.py:156
  315.6 1.1 copy.52
  316.7 1.0 fusion.15
  317.6 46.9 %custom-call.8 = f32[4,128,128]{2,1,0:T(8,128)S(1)} custom-call(f32[4,128,128]{2,1,0:T(8,128)S(1)} %fusion.15), custom_call_target="Cholesky" | custom-call | tf_op jit(solution)/shard_map/jit(cholesky)/cholesky | solution.py:157
  364.8 39.3 %custom-call.9 = f32[4,1,128,128]{2,3,1,0:T(8,128)S(1)} custom-call(f32[4,1,128,128]{3,2,1,0:T(8,128)S(1)} %get-tuple-element.349), custom_call_target="InvertDiagBlocksLowerTriangular" | custom-call | tf_op jit(solution)/shard_map/jit(_solve_triangular)/vmap()/triangular_solve | solution.py:159
  (83 shorter events, 16.8 us)
Async XLA Ops:
  7.2 85.1 %all-gather.2.cloned.1.call-start = ((), (), s32[]{:S(2)}) async-start(), calls=%async_computation.1 | async-start | bytes 2359296 | tf_op jit(solution)/shard_map/all_gather | solution.py:129
  92.3 6.4 %collective-permute-start = (bf16[8192,128]{1,0:T(8,128)(2,1)}, bf16[8192,128]{1,0:T(8,128)(2,1)}, u32[]{:S(2)}, u32[]{:S(2)}) collective-permute-start(bf16[8192,128]{1,0:T(8,128)(2,1)} %all-gather.2.cloned.1.call-done), channel_id=1, source_target_pairs={{0,1},{1,0},{2,3},{3,2},{4,5},{5,4},{6,7},{7,6},{8,9},{9,8},{10,11... | collective-permute-start | bytes 6291464 | tf_op jit(solution)/shard_map/ppermute | solution.py:130
  102.6 20.8 %copy-start = (bf16[128,512]{1,0:T(8,128)(2,1)S(1)}, bf16[128,512]{1,0:T(8,128)(2,1)}, u32[]{:S(2)}) copy-start(bf16[128,512]{1,0:T(8,128)(2,1)} %param.14) | copy-start | bytes 393220
  123.6 241.2 %copy-start.1 = (bf16[128,512]{1,0:T(8,128)(2,1)}, bf16[128,512]{1,0:T(8,128)(2,1)S(1)}, u32[]{:S(2)}) copy-start(bf16[128,512]{1,0:T(8,128)(2,1)S(1)} %get-tuple-element.344) | copy-start | bytes 393220
  124.3 15.9 %all-to-all-start = ((f32[16,1,128]{2,1,0:T(1,128)}), f32[16,1,128]{2,1,0:T(1,128)S(1)}, u32[]{:S(2)}, u32[]{:S(2)}) async-start(f32[16,1,128]{2,1,0:T(1,128)} %broadcast_in_dim.116), calls=%async_computation | async-start | bytes 16384 | tf_op jit(solution)/shard_map/all_to_all | solution.py:30
  132.6 97.0 %all-reduce.3.cloned.1.call-start = ((), (), s32[]{:S(2)}) async-start(), calls=%async_computation.2 | async-start | bytes 524288 | tf_op jit(solution)/shard_map/psum | solution.py:156
  141.8 173.8 %all-reduce.5.cloned.1.call-start = ((), (), s32[]{:S(2)}) async-start(), calls=%async_computation.3 | async-start | bytes 524288 | tf_op jit(solution)/shard_map/psum | solution.py:156
Sparse Core Ops, SparseCore 0:
  44.8 47.4 all-gather.1
  141.9 87.6 all-reduce.2
  231.9 83.6 all-reduce.4

commit v2 on v1

--- a/solution.py
+++ b/solution.py
@@ -35,6 +35,30 @@
 def over_copies(shard, axis):
     everything = copy_for_each(shard, axis)
     return jnp.sum(everything, axis=0)
+
+
+def exchange_sum(value, axis):
+    count = lax.axis_size(axis)
+    step = 1
+    while step < count:
+        partner = lax.ppermute(value, axis, [(i, i ^ step) for i in range(count)])
+        value = value + partner
+        step *= 2
+    return value
+
+
+def exchange_gather(value, axis):
+    count = lax.axis_size(axis)
+    me = lax.axis_index(axis)
+    step = 1
+    while step < count:
+        partner = lax.ppermute(value, axis, [(i, i ^ step) for i in range(count)])
+        low = (me & step) == 0
+        first = jnp.where(low, value, partner)
+        second = jnp.where(low, partner, value)
+        value = jnp.concatenate([first, second], axis=0)
+        step *= 2
+    return value
 
 
 def positions_and_docs(block_pos, doc_offset):
@@ -126,7 +150,7 @@
     )
     core = lax.axis_index("c")
     mine = jnp.where(core == 0, key_cols, value_cols)
-    gathered = lax.all_gather(lax.all_gather(mine, "x", axis=0, tiled=True), "y", axis=0, tiled=True)
+    gathered = lax.all_gather(exchange_gather(mine, "x"), "y", axis=0, tiled=True)
     other = lax.ppermute(gathered, "c", perm=[(0, 1), (1, 0)])
     key_piece = jnp.where(core == 0, gathered, other)
     value_piece = jnp.where(core == 0, other, gathered)
@@ -153,7 +177,7 @@
     normed = mixed * lax.rsqrt(square_sum[:, None] / WIDTH + EPSILON) * gain_cols[None, :]
     blocks = normed.reshape(row_count, head_count, HD)
     head_rows = jnp.transpose(blocks, (1, 0, 2))
-    gram_sum = lax.psum(lax.optimization_barrier(lax.psum(gram_of(head_rows), "x")), "y")
+    gram_sum = exchange_sum(exchange_sum(gram_of(head_rows), "x"), "y")
     lower_factor = jnp.linalg.cholesky(gram_sum)
     r_factor = jnp.transpose(lower_factor, (0, 2, 1)) / math.sqrt(total_rows)
     solved = jax.scipy.linalg.solve_triangular(

time: 414 us -> 332 us (0.80)
  waiting for transfers between devices: 228 us -> 134 us
  starting transfers between devices: 10.4 us -> 62.6 us
  blocking collectives: 36.6 us -> 0 us
    psum x2 -> x0, waiting for transfers between devices: 174 us -> none  [the longest x1 87.8 us: local(): lax.psum(gram_of(head_rows), 'x')]
    ppermute x0 -> x9, waiting for transfers between devices: none -> 72.9 us  [the longest x6 64.6 us: exchange_sum(): partner = lax.ppermute(value, axis, [(i, i ^ step) for i in range(count)])]
    ppermute x0 -> x9, starting transfers between devices: none -> 52.4 us  [the longest x6 29.4 us: exchange_sum(): partner = lax.ppermute(value, axis, [(i, i ^ step) for i in range(count)])]
    all_gather x1 -> x0, blocking collectives: 36.6 us -> none  [local(): lax.all_gather(mine, 'x', axis=0, tiled=True)]
  transfers between devices with their start and end apart: 5 -> 12, of which waited for: 4 -> 12; matrix products, arithmetic and copies ran while one was open for 1% -> 1% of each run, Pallas kernels for 0% -> 0%
where the time goes in v2:
time: 332 us; the launch traced here: 330 us
  waiting for transfers between devices  134 us (40%)
  other arithmetic  102 us (31%)
  starting transfers between devices  62.6 us (19%)
  between operations  14.5 us (4%)
  matrix products  7.18 us (2%)
  loops' own time  5.76 us (2%)
  local copies, waits for them, and re-layouts  4.06 us (1%)
    ppermute x6, waiting for transfers between devices, exchange_sum(): partner = lax.ppermute(value, axis, [(i, i ^ step) for i in range(count)])  64.6 us
    all_gather x1, waiting for transfers between devices, local(): lax.all_gather(exchange_gather(mine, 'x'), 'y', axis=0, tiled=True)  50.8 us
    another operation x4, other arithmetic, local(): lower_factor = jnp.linalg.cholesky(gram_sum)  47.1 us
    another operation x2, other arithmetic, local(): jax.scipy.linalg.solve_triangular(lower_factor, jnp.transpose(blocks, (1,...  39.4 us
    ppermute x6, starting transfers between devices, exchange_sum(): partner = lax.ppermute(value, axis, [(i, i ^ step) for i in range(count)])  29.4 us
    ppermute x3, starting transfers between devices, exchange_gather(): partner = lax.ppermute(value, axis, [(i, i ^ step) for i in range(count)])  23 us
    ppermute x3, waiting for transfers between devices, exchange_gather(): partner = lax.ppermute(value, axis, [(i, i ^ step) for i in range(count)])  8.31 us
    all_to_all x1, starting transfers between devices, copy_for_each(): lax.all_to_all(jnp.broadcast_to(shard[None], (count, *shard.shape)), axis...  8.21 us
  transfers between devices with their start and end apart: 12, of which 12 were waited for; matrix products, arithmetic and copies ran while one was open for 1% of the time, Pallas kernels for 0%

profile of v2, /device:TPU:14, one launch (start us, length us, event | category | flops | bytes accessed | tf_op | source)
XLA Modules:
  0.0 329.8 jit_solution(13982805818714320122)
XLA Ops:
  8.1 3.3 %collective-permute-start = (bf16[128,128]{1,0:T(8,128)(2,1)S(1)}, bf16[128,128]{1,0:T(8,128)(2,1)S(1)}, u32[]{:S(2)}, u32[]{:S(2)}) collective-permute-start(bf16[128,128]{1,0:T(8,128)(2,1)S(1)} %dynamic-slice_select_fusion), channel_id=1, source_target_pairs={{0,16},{16,0},{32,48},{48,32},{64,80},{80,64},{96,112},{112,96},{1... | collective-permute-start | bytes 98312 | tf_op jit(solution)/shard_map/ppermute | solution.py:55
  11.4 2.5 collective-permute-done
  13.9 4.2 %collective-permute-start.1 = (bf16[256,128]{1,0:T(8,128)(2,1)S(1)}, bf16[256,128]{1,0:T(8,128)(2,1)S(1)}, u32[]{:S(2)}, u32[]{:S(2)}) collective-permute-start(bf16[256,128]{1,0:T(8,128)(2,1)S(1)} %pad_maximum_fusion.2), channel_id=1, source_target_pairs={{0,32},{16,48},{32,0},{48,16},{64,96},{80,112},{96,64},{112,80},{1... | collective-permute-start | bytes 196616 | tf_op jit(solution)/shard_map/ppermute | solution.py:55
  18.2 2.8 collective-permute-done.1
  21.0 15.5 %collective-permute-start.2 = (bf16[512,128]{1,0:T(8,128)(2,1)S(1)}, bf16[512,128]{1,0:T(8,128)(2,1)S(1)}, u32[]{:S(2)}, u32[]{:S(2)}) collective-permute-start(bf16[512,128]{1,0:T(8,128)(2,1)S(1)} %pad_maximum_fusion.1), channel_id=1, source_target_pairs={{0,64},{16,80},{32,96},{48,112},{64,0},{80,16},{96,32},{112,48},{1... | collective-permute-start | bytes 393224 | tf_op jit(solution)/shard_map/ppermute | solution.py:55
  36.5 3.0 collective-permute-done.2
  40.3 50.8 %all-gather.2.cloned.1.call-done = bf16[8192,128]{1,0:T(8,128)(2,1)} async-done(((bf16[1024,128]{1,0:T(8,128)(2,1)}), bf16[8192,128]{1,0:T(8,128)(2,1)}) %all-gather.2.cloned.1.call-update) | async-done | bytes 2097168 | tf_op jit(solution)/shard_map/all_gather | solution.py:153
  94.1 3.5 %collective-permute-done.3 = bf16[8192,128]{1,0:T(8,128)(2,1)} collective-permute-done((bf16[8192,128]{1,0:T(8,128)(2,1)}, bf16[8192,128]{1,0:T(8,128)(2,1)}, u32[]{:S(2)}, u32[]{:S(2)}) %collective-permute-start.3) | collective-permute-done | bytes 2097184 | tf_op jit(solution)/shard_map/ppermute | solution.py:154
  97.6 3.8 %broadcast_select_fusion = (bf16[8192,128]{1,0:T(8,128)(2,1)S(1)}, bf16[8192,128]{1,0:T(8,128)(2,1)}) fusion(bf16[8192,128]{1,0:T(8,128)(2,1)} %collective-permute-done.3, bf16[8192,128]{1,0:T(8,128)(2,1)} %all-gather.2.cloned.1.call-done, pred[]{:T(512)S(6)} %eq.70), kind=kLoop, calls=%fused_computation.20 | loop fusion | flops 2097152 | bytes 8388609 | tf_op jit(solution)/shard_map/jit(_where)/select_n | solution.py:156
  101.5 20.6 %while.17 = (s32[]{:T(128)}, f32[1,4,128]{2,1,0:T(4,128)S(1)}, f32[1,4,128]{2,1,0:T(4,128)S(1)}, f32[1,4,128,128]{3,2,1,0:T(8,128)S(1)}, s32[8192]{0:T(1024)S(1)...) while((s32[]{:T(128)}, f32[1,4,128]{2,1,0:T(4,128)S(1)}, ...), condition=%wide.region_9.10_spmd, body=%wide.region_3.9_spmd.sunk | while | flops 272762368 | bytes 7792453 | solution.py:166
  123.1 8.2 %all-to-all-start = ((f32[16,1,128]{2,1,0:T(1,128)}), f32[16,1,128]{2,1,0:T(1,128)S(1)}, u32[]{:S(2)}, u32[]{:S(2)}) async-start(f32[16,1,128]{2,1,0:T(1,128)} %broadcast_in_dim.116), calls=%async_computation | async-start | bytes 16384 | tf_op jit(solution)/shard_map/all_to_all | solution.py:30
  132.1 6.7 %all-to-all-done = f32[16,1,128]{2,1,0:T(1,128)S(1)} async-done(((f32[16,1,128]{2,1,0:T(1,128)}), f32[16,1,128]{2,1,0:T(1,128)S(1)}, u32[]{:S(2)}, u32[]{:S(2)}) %all-to-all-start) | async-done | bytes 8224 | tf_op jit(solution)/shard_map/all_to_all | solution.py:30
  139.7 3.4 %collective-permute-start.4 = (f32[4,128,128]{1,2,0:T(8,128)S(1)}, f32[4,128,128]{1,2,0:T(8,128)S(1)}, u32[]{:S(2)}, u32[]{:S(2)}) collective-permute-start(f32[4,128,128]{1,2,0:T(8,128)S(1)} %fusion.19), channel_id=1, source_target_pairs={{0,16},{16,0},{32,48},{48,32},{64,80},{80,64},{96,112},{112,96},{1... | collective-permute-start | bytes 786440 | tf_op jit(solution)/shard_map/ppermute | solution.py:44
  143.1 6.6 %collective-permute-done.4 = f32[4,128,128]{1,2,0:T(8,128)S(1)} collective-permute-done((f32[4,128,128]{1,2,0:T(8,128)S(1)}, f32[4,128,128]{1,2,0:T(8,128)S(1)}, u32[]{:S(2)}, u32[]{:S(2)}) %collective-permute-start.4) | collective-permute-done | bytes 262176 | tf_op jit(solution)/shard_map/ppermute | solution.py:44
  149.7 13.5 %collective-permute-start.5 = (f32[4,128,128]{1,2,0:T(8,128)S(1)}, f32[4,128,128]{1,2,0:T(8,128)S(1)}, u32[]{:S(2)}, u32[]{:S(2)}) collective-permute-start(f32[4,128,128]{1,2,0:T(8,128)S(1)} %add.160), channel_id=1, source_target_pairs={{0,32},{16,48},{32,0},{48,16},{64,96},{80,112},{96,64},{112,80},{1... | collective-permute-start | bytes 786440 | tf_op jit(solution)/shard_map/ppermute | solution.py:44
  163.3 11.1 %collective-permute-done.5 = f32[4,128,128]{1,2,0:T(8,128)S(1)} collective-permute-done((f32[4,128,128]{1,2,0:T(8,128)S(1)}, f32[4,128,128]{1,2,0:T(8,128)S(1)}, u32[]{:S(2)}, u32[]{:S(2)}) %collective-permute-start.5) | collective-permute-done | bytes 262176 | tf_op jit(solution)/shard_map/ppermute | solution.py:44
  174.4 5.4 %collective-permute-start.6 = (f32[4,128,128]{1,2,0:T(8,128)S(1)}, f32[4,128,128]{1,2,0:T(8,128)S(1)}, u32[]{:S(2)}, u32[]{:S(2)}) collective-permute-start(f32[4,128,128]{1,2,0:T(8,128)S(1)} %add.161), channel_id=1, source_target_pairs={{0,64},{16,80},{32,96},{48,112},{64,0},{80,16},{96,32},{112,48},{1... | collective-permute-start | bytes 786440 | tf_op jit(solution)/shard_map/ppermute | solution.py:44
  179.8 13.4 %collective-permute-done.6 = f32[4,128,128]{1,2,0:T(8,128)S(1)} collective-permute-done((f32[4,128,128]{1,2,0:T(8,128)S(1)}, f32[4,128,128]{1,2,0:T(8,128)S(1)}, u32[]{:S(2)}, u32[]{:S(2)}) %collective-permute-start.6) | collective-permute-done | bytes 262176 | tf_op jit(solution)/shard_map/ppermute | solution.py:44
  195.2 7.1 %collective-permute-done.7 = f32[4,128,128]{1,2,0:T(8,128)S(1)} collective-permute-done((f32[4,128,128]{1,2,0:T(8,128)S(1)}, f32[4,128,128]{1,2,0:T(8,128)S(1)}, u32[]{:S(2)}, u32[]{:S(2)}) %collective-permute-start.7) | collective-permute-done | bytes 262176 | tf_op jit(solution)/shard_map/ppermute | solution.py:44
  204.3 12.8 %collective-permute-done.8 = f32[4,128,128]{1,2,0:T(8,128)S(1)} collective-permute-done((f32[4,128,128]{1,2,0:T(8,128)S(1)}, f32[4,128,128]{1,2,0:T(8,128)S(1)}, u32[]{:S(2)}, u32[]{:S(2)}) %collective-permute-start.8) | collective-permute-done | bytes 262176 | tf_op jit(solution)/shard_map/ppermute | solution.py:44
  217.1 3.2 collective-permute-start.9
  220.3 13.7 %collective-permute-done.9 = f32[4,128,128]{1,2,0:T(8,128)S(1)} collective-permute-done((f32[4,128,128]{1,2,0:T(8,128)S(1)}, f32[4,128,128]{1,2,0:T(8,128)S(1)}, u32[]{:S(2)}, u32[]{:S(2)}) %collective-permute-start.9) | collective-permute-done | bytes 262176 | tf_op jit(solution)/shard_map/ppermute | solution.py:44
  234.2 46.9 %custom-call.8 = f32[4,128,128]{2,1,0:T(8,128)S(1)} custom-call(f32[4,128,128]{2,1,0:T(8,128)S(1)} %fusion.15), custom_call_target="Cholesky" | custom-call | tf_op jit(solution)/shard_map/jit(cholesky)/cholesky | solution.py:181
  281.4 39.3 %custom-call.9 = f32[4,1,128,128]{2,3,1,0:T(8,128)S(1)} custom-call(f32[4,1,128,128]{3,2,1,0:T(8,128)S(1)} %get-tuple-element.349), custom_call_target="InvertDiagBlocksLowerTriangular" | custom-call | tf_op jit(solution)/shard_map/jit(_solve_triangular)/vmap()/triangular_solve | solution.py:183
  (112 shorter events, 35.9 us)
Async XLA Ops:
  7.2 85.9 %copy-start.3 = (s32[1,64]{1,0:T(1,128)S(1)}, s32[1,64]{1,0:T(1,128)}, u32[]{:S(2)}) copy-start(s32[1,64]{1,0:T(1,128)} %param.17) | copy-start | bytes 772
  7.2 86.2 %copy-start.4 = (s32[1,64]{1,0:T(1,128)S(1)}, s32[1,64]{1,0:T(1,128)}, u32[]{:S(2)}) copy-start(s32[1,64]{1,0:T(1,128)} %param.16) | copy-start | bytes 772
  7.2 86.6 %copy-start.2 = (bf16[128,512]{1,0:T(8,128)(2,1)S(1)}, bf16[128,512]{1,0:T(8,128)(2,1)}, u32[]{:S(2)}) copy-start(bf16[128,512]{1,0:T(8,128)(2,1)} %param.11) | copy-start | bytes 393220
  7.2 84.0 %all-gather.2.cloned.1.call-start = ((), (), s32[]{:S(2)}) async-start(), calls=%async_computation.1 | async-start | bytes 2359296 | tf_op jit(solution)/shard_map/all_gather | solution.py:153
  8.1 5.8 %collective-permute-start = (bf16[128,128]{1,0:T(8,128)(2,1)S(1)}, bf16[128,128]{1,0:T(8,128)(2,1)S(1)}, u32[]{:S(2)}, u32[]{:S(2)}) collective-permute-start(bf16[128,128]{1,0:T(8,128)(2,1)S(1)} %dynamic-slice_select_fusion), channel_id=1, source_target_pairs={{0,16},{16,0},{32,48},{48,32},{64,80},{80,64},{96,112},{112,96},{1... | collective-permute-start | bytes 98312 | tf_op jit(solution)/shard_map/ppermute | solution.py:55
  13.9 7.1 %collective-permute-start.1 = (bf16[256,128]{1,0:T(8,128)(2,1)S(1)}, bf16[256,128]{1,0:T(8,128)(2,1)S(1)}, u32[]{:S(2)}, u32[]{:S(2)}) collective-permute-start(bf16[256,128]{1,0:T(8,128)(2,1)S(1)} %pad_maximum_fusion.2), channel_id=1, source_target_pairs={{0,32},{16,48},{32,0},{48,16},{64,96},{80,112},{96,64},{112,80},{1... | collective-permute-start | bytes 196616 | tf_op jit(solution)/shard_map/ppermute | solution.py:55
  21.0 18.5 %collective-permute-start.2 = (bf16[512,128]{1,0:T(8,128)(2,1)S(1)}, bf16[512,128]{1,0:T(8,128)(2,1)S(1)}, u32[]{:S(2)}, u32[]{:S(2)}) collective-permute-start(bf16[512,128]{1,0:T(8,128)(2,1)S(1)} %pad_maximum_fusion.1), channel_id=1, source_target_pairs={{0,64},{16,80},{32,96},{48,112},{64,0},{80,16},{96,32},{112,48},{1... | collective-permute-start | bytes 393224 | tf_op jit(solution)/shard_map/ppermute | solution.py:55
  91.2 6.4 %collective-permute-start.3 = (bf16[8192,128]{1,0:T(8,128)(2,1)}, bf16[8192,128]{1,0:T(8,128)(2,1)}, u32[]{:S(2)}, u32[]{:S(2)}) collective-permute-start(bf16[8192,128]{1,0:T(8,128)(2,1)} %all-gather.2.cloned.1.call-done), channel_id=1, source_target_pairs={{0,1},{1,0},{2,3},{3,2},{4,5},{5,4},{6,7},{7,6},{8,9},{9,8},{10,11... | collective-permute-start | bytes 6291464 | tf_op jit(solution)/shard_map/ppermute | solution.py:154
  101.4 20.9 %copy-start = (bf16[128,512]{1,0:T(8,128)(2,1)S(1)}, bf16[128,512]{1,0:T(8,128)(2,1)}, u32[]{:S(2)}) copy-start(bf16[128,512]{1,0:T(8,128)(2,1)} %param.14) | copy-start | bytes 393220
  122.4 70.8 %copy-start.1 = (bf16[128,512]{1,0:T(8,128)(2,1)}, bf16[128,512]{1,0:T(8,128)(2,1)S(1)}, u32[]{:S(2)}) copy-start(bf16[128,512]{1,0:T(8,128)(2,1)S(1)} %get-tuple-element.344) | copy-start | bytes 393220
  123.1 15.7 %all-to-all-start = ((f32[16,1,128]{2,1,0:T(1,128)}), f32[16,1,128]{2,1,0:T(1,128)S(1)}, u32[]{:S(2)}, u32[]{:S(2)}) async-start(f32[16,1,128]{2,1,0:T(1,128)} %broadcast_in_dim.116), calls=%async_computation | async-start | bytes 16384 | tf_op jit(solution)/shard_map/all_to_all | solution.py:30
  139.7 10.0 %collective-permute-start.4 = (f32[4,128,128]{1,2,0:T(8,128)S(1)}, f32[4,128,128]{1,2,0:T(8,128)S(1)}, u32[]{:S(2)}, u32[]{:S(2)}) collective-permute-start(f32[4,128,128]{1,2,0:T(8,128)S(1)} %fusion.19), channel_id=1, source_target_pairs={{0,16},{16,0},{32,48},{48,32},{64,80},{80,64},{96,112},{112,96},{1... | collective-permute-start | bytes 786440 | tf_op jit(solution)/shard_map/ppermute | solution.py:44
  149.7 24.6 %collective-permute-start.5 = (f32[4,128,128]{1,2,0:T(8,128)S(1)}, f32[4,128,128]{1,2,0:T(8,128)S(1)}, u32[]{:S(2)}, u32[]{:S(2)}) collective-permute-start(f32[4,128,128]{1,2,0:T(8,128)S(1)} %add.160), channel_id=1, source_target_pairs={{0,32},{16,48},{32,0},{48,16},{64,96},{80,112},{96,64},{112,80},{1... | collective-permute-start | bytes 786440 | tf_op jit(solution)/shard_map/ppermute | solution.py:44
  174.4 18.8 %collective-permute-start.6 = (f32[4,128,128]{1,2,0:T(8,128)S(1)}, f32[4,128,128]{1,2,0:T(8,128)S(1)}, u32[]{:S(2)}, u32[]{:S(2)}) collective-permute-start(f32[4,128,128]{1,2,0:T(8,128)S(1)} %add.161), channel_id=1, source_target_pairs={{0,64},{16,80},{32,96},{48,112},{64,0},{80,16},{96,32},{112,48},{1... | collective-permute-start | bytes 786440 | tf_op jit(solution)/shard_map/ppermute | solution.py:44
  193.3 9.0 %collective-permute-start.7 = (f32[4,128,128]{1,2,0:T(8,128)S(1)}, f32[4,128,128]{1,2,0:T(8,128)S(1)}, u32[]{:S(2)}, u32[]{:S(2)}) collective-permute-start(f32[4,128,128]{1,2,0:T(8,128)S(1)} %add.162), channel_id=1, source_target_pairs={{0,128},{128,0},{256,384},{384,256},{512,640},{640,512},{768,896},... | collective-permute-start | bytes 786440 | tf_op jit(solution)/shard_map/ppermute | solution.py:44
  202.4 14.7 %collective-permute-start.8 = (f32[4,128,128]{1,2,0:T(8,128)S(1)}, f32[4,128,128]{1,2,0:T(8,128)S(1)}, u32[]{:S(2)}, u32[]{:S(2)}) collective-permute-start(f32[4,128,128]{1,2,0:T(8,128)S(1)} %add.163), channel_id=1, source_target_pairs={{0,256},{128,384},{256,0},{384,128},{512,768},{640,896},{768,512},... | collective-permute-start | bytes 786440 | tf_op jit(solution)/shard_map/ppermute | solution.py:44
  217.1 16.9 %collective-permute-start.9 = (f32[4,128,128]{1,2,0:T(8,128)S(1)}, f32[4,128,128]{1,2,0:T(8,128)S(1)}, u32[]{:S(2)}, u32[]{:S(2)}) collective-permute-start(f32[4,128,128]{1,2,0:T(8,128)S(1)} %add.164), channel_id=1, source_target_pairs={{0,512},{128,640},{256,768},{384,896},{512,0},{640,128},{768,256},... | collective-permute-start | bytes 786440 | tf_op jit(solution)/shard_map/ppermute | solution.py:44
Sparse Core Ops, SparseCore 0:
  40.5 50.6 all-gather.1

commit v3 on v2

--- a/solution.py
+++ b/solution.py
@@ -3,6 +3,8 @@
 import jax
 import jax.numpy as jnp
 from jax import lax
+from jax.experimental import pallas as pl
+from jax.experimental.pallas import tpu as pltpu
 from jax.sharding import PartitionSpec as P
 
 HEADS = 64
@@ -35,6 +37,47 @@
 def over_copies(shard, axis):
     everything = copy_for_each(shard, axis)
     return jnp.sum(everything, axis=0)
+
+
+def factor_kernel(g_ref, u_ref, li_ref, m_ref):
+    heads, n, _ = g_ref.shape
+    row_ids = lax.broadcasted_iota(jnp.int32, (n, 1), 0)
+    lane_ids = lax.broadcasted_iota(jnp.int32, (1, n), 1)
+    eye = (lax.broadcasted_iota(jnp.int32, (n, n), 0) == lax.broadcasted_iota(jnp.int32, (n, n), 1)).astype(jnp.float32)
+    for h in range(heads):
+        m_ref[h, :, :n] = g_ref[h]
+        m_ref[h, :, n:] = eye
+
+    def step(j, carry):
+        pick = lane_ids == j
+        for h in range(heads):
+            row = m_ref[h, pl.ds(j, 1), :]
+            pivot = jnp.sum(jnp.where(pick, row[:, :n], 0.0), axis=1, keepdims=True)
+            scale = lax.rsqrt(pivot)
+            scaled = row * scale
+            column = jnp.sum(jnp.where(pick, m_ref[h, :, :n], 0.0), axis=1, keepdims=True)
+            column = jnp.where(row_ids > j, column * scale, 0.0)
+            m_ref[h] = m_ref[h] - column * scaled
+            m_ref[h, pl.ds(j, 1), :] = scaled
+        return carry
+
+    lax.fori_loop(0, n, step, 0)
+    upper = lax.broadcasted_iota(jnp.int32, (n, n), 0) <= lax.broadcasted_iota(jnp.int32, (n, n), 1)
+    for h in range(heads):
+        u_ref[h] = jnp.where(upper, m_ref[h, :, :n], 0.0)
+        li_ref[h] = m_ref[h, :, n:]
+
+
+def factor(gram):
+    heads, n, _ = gram.shape
+    shape = jax.ShapeDtypeStruct((heads, n, n), jnp.float32)
+    return pl.pallas_call(
+        factor_kernel,
+        out_shape=(shape, shape),
+        in_specs=[pl.BlockSpec(memory_space=pltpu.VMEM)],
+        out_specs=(pl.BlockSpec(memory_space=pltpu.VMEM), pl.BlockSpec(memory_space=pltpu.VMEM)),
+        scratch_shapes=[pltpu.VMEM((heads, n, 2 * n), jnp.float32)],
+    )(gram)
 
 
 def exchange_sum(value, axis):
@@ -178,14 +221,10 @@
     blocks = normed.reshape(row_count, head_count, HD)
     head_rows = jnp.transpose(blocks, (1, 0, 2))
     gram_sum = exchange_sum(exchange_sum(gram_of(head_rows), "x"), "y")
-    lower_factor = jnp.linalg.cholesky(gram_sum)
-    r_factor = jnp.transpose(lower_factor, (0, 2, 1)) / math.sqrt(total_rows)
-    solved = jax.scipy.linalg.solve_triangular(
-        lower_factor, jnp.transpose(blocks, (1, 2, 0)), lower=True
-    )
-    whitened = jnp.transpose(solved, (2, 0, 1)).reshape(row_count, head_count * HD) * math.sqrt(
-        total_rows
-    )
+    upper_factor, lower_inverse = factor(gram_sum)
+    r_factor = upper_factor / math.sqrt(total_rows)
+    solved = jnp.einsum("rhc,hdc->rhd", blocks, lower_inverse, precision=lax.Precision.HIGHEST)
+    whitened = solved.reshape(row_count, head_count * HD) * math.sqrt(total_rows)
     return (attn_out, r_factor, whitened)
 
 

time: 332 us -> 306 us (0.922)
  other arithmetic: 102 us -> 18.6 us
  Pallas kernels: 0 us -> 53.5 us
  matrix products: 7.18 us -> 13.8 us
    another operation x7 -> x1, other arithmetic: 86.8 us -> 0.24 us  [the longest x4 47.1 us: local(): lower_factor = jnp.linalg.cholesky(gram_sum)]
    pallas_call x0 -> x1, Pallas kernels: none -> 53.5 us  [factor(): pl.pallas_call(factor_kernel, out_shape=(shape, shape), in_specs=[pl.Bloc...]
    dot_general x3 -> x6, matrix products: 4.21 us -> 8.43 us  [accumulate(): jnp.einsum('rkgd,nkd->kgrn', query_heads, key_heads, preferred_element_ty...]
where the time goes in v3:
time: 306 us; the launch traced here: 304 us
  waiting for transfers between devices  135 us (44%)
  starting transfers between devices  59.7 us (20%)
  Pallas kernels  53.5 us (17%)
  other arithmetic  18.6 us (6%)
  between operations  14.4 us (5%)
  matrix products  13.8 us (5%)
  loops' own time  5.84 us (2%)
  local copies, waits for them, and re-layouts  3.11 us (1%)
    ppermute x6, waiting for transfers between devices, exchange_sum(): partner = lax.ppermute(value, axis, [(i, i ^ step) for i in range(count)])  65.3 us
    pallas_call x1, Pallas kernels, factor(): pl.pallas_call(factor_kernel, out_shape=(shape, shape), in_specs=[pl.Bloc...  53.5 us
    all_gather x1, waiting for transfers between devices, local(): lax.all_gather(exchange_gather(mine, 'x'), 'y', axis=0, tiled=True)  50.8 us
    ppermute x6, starting transfers between devices, exchange_sum(): partner = lax.ppermute(value, axis, [(i, i ^ step) for i in range(count)])  26.6 us
    ppermute x3, starting transfers between devices, exchange_gather(): partner = lax.ppermute(value, axis, [(i, i ^ step) for i in range(count)])  23 us
    dot_general x6, matrix products, accumulate(): jnp.einsum('rkgd,nkd->kgrn', query_heads, key_heads, preferred_element_ty...  8.43 us
    ppermute x3, waiting for transfers between devices, exchange_gather(): partner = lax.ppermute(value, axis, [(i, i ^ step) for i in range(count)])  8.31 us
    all_to_all x1, starting transfers between devices, copy_for_each(): lax.all_to_all(jnp.broadcast_to(shard[None], (count, *shard.shape)), axis...  8.21 us
  transfers between devices with their start and end apart: 12, of which 12 were waited for; matrix products, arithmetic and copies ran while one was open for 1% of the time, Pallas kernels for 0%

profile of v3, /device:TPU:14, one launch (start us, length us, event | category | flops | bytes accessed | tf_op | source)
XLA Modules:
  0.0 303.8 jit_solution(6953288043682567061)
XLA Ops:
  8.1 3.3 %collective-permute-start = (bf16[128,128]{1,0:T(8,128)(2,1)S(1)}, bf16[128,128]{1,0:T(8,128)(2,1)S(1)}, u32[]{:S(2)}, u32[]{:S(2)}) collective-permute-start(bf16[128,128]{1,0:T(8,128)(2,1)S(1)} %dynamic-slice_select_fusion), channel_id=1, source_target_pairs={{0,16},{16,0},{32,48},{48,32},{64,80},{80,64},{96,112},{112,96},{1... | collective-permute-start | bytes 98312 | tf_op jit(solution)/shard_map/ppermute | solution.py:98
  13.9 4.2 %collective-permute-start.1 = (bf16[256,128]{1,0:T(8,128)(2,1)S(1)}, bf16[256,128]{1,0:T(8,128)(2,1)S(1)}, u32[]{:S(2)}, u32[]{:S(2)}) collective-permute-start(bf16[256,128]{1,0:T(8,128)(2,1)S(1)} %pad_maximum_fusion.2), channel_id=1, source_target_pairs={{0,32},{16,48},{32,0},{48,16},{64,96},{80,112},{96,64},{112,80},{1... | collective-permute-start | bytes 196616 | tf_op jit(solution)/shard_map/ppermute | solution.py:98
  18.2 2.8 collective-permute-done.1
  21.0 15.5 %collective-permute-start.2 = (bf16[512,128]{1,0:T(8,128)(2,1)S(1)}, bf16[512,128]{1,0:T(8,128)(2,1)S(1)}, u32[]{:S(2)}, u32[]{:S(2)}) collective-permute-start(bf16[512,128]{1,0:T(8,128)(2,1)S(1)} %pad_maximum_fusion.1), channel_id=1, source_target_pairs={{0,64},{16,80},{32,96},{48,112},{64,0},{80,16},{96,32},{112,48},{1... | collective-permute-start | bytes 393224 | tf_op jit(solution)/shard_map/ppermute | solution.py:98
  36.5 3.0 collective-permute-done.2
  40.3 50.8 %all-gather.2.cloned.1.call-done = bf16[8192,128]{1,0:T(8,128)(2,1)} async-done(((bf16[1024,128]{1,0:T(8,128)(2,1)}), bf16[8192,128]{1,0:T(8,128)(2,1)}) %all-gather.2.cloned.1.call-update) | async-done | bytes 2097168 | tf_op jit(solution)/shard_map/all_gather | solution.py:196
  94.1 3.5 %collective-permute-done.3 = bf16[8192,128]{1,0:T(8,128)(2,1)} collective-permute-done((bf16[8192,128]{1,0:T(8,128)(2,1)}, bf16[8192,128]{1,0:T(8,128)(2,1)}, u32[]{:S(2)}, u32[]{:S(2)}) %collective-permute-start.3) | collective-permute-done | bytes 2097184 | tf_op jit(solution)/shard_map/ppermute | solution.py:197
  97.6 3.8 %broadcast_select_fusion = (bf16[8192,128]{1,0:T(8,128)(2,1)S(1)}, bf16[8192,128]{1,0:T(8,128)(2,1)}) fusion(bf16[8192,128]{1,0:T(8,128)(2,1)} %collective-permute-done.3, bf16[8192,128]{1,0:T(8,128)(2,1)} %all-gather.2.cloned.1.call-done, pred[]{:T(512)S(6)} %eq.70), kind=kLoop, calls=%fused_computation.20 | loop fusion | flops 2097152 | bytes 8388609 | tf_op jit(solution)/shard_map/jit(_where)/select_n | solution.py:199
  101.4 27.5 %while.17 = (s32[]{:T(128)}, f32[1,4,128]{2,1,0:T(4,128)S(1)}, f32[1,4,128]{2,1,0:T(4,128)S(1)}, f32[1,4,128,128]{3,2,1,0:T(8,128)S(1)}, s32[8192]{0:T(1024)S(1)...) while((s32[]{:T(128)}, f32[1,4,128]{2,1,0:T(4,128)S(1)}, ...), condition=%wide.region_9.10_spmd, body=%wide.region_3.9_spmd.sunk | while | flops 272762368 | bytes 7792453 | solution.py:209
  130.0 8.2 %all-to-all-start = ((f32[16,1,128]{2,1,0:T(1,128)}), f32[16,1,128]{2,1,0:T(1,128)S(1)}, u32[]{:S(2)}, u32[]{:S(2)}) async-start(f32[16,1,128]{2,1,0:T(1,128)} %broadcast_in_dim.107), calls=%async_computation | async-start | bytes 16384 | tf_op jit(solution)/shard_map/all_to_all | solution.py:32
  139.0 6.7 %all-to-all-done = f32[16,1,128]{2,1,0:T(1,128)S(1)} async-done(((f32[16,1,128]{2,1,0:T(1,128)}), f32[16,1,128]{2,1,0:T(1,128)S(1)}, u32[]{:S(2)}, u32[]{:S(2)}) %all-to-all-start) | async-done | bytes 8224 | tf_op jit(solution)/shard_map/all_to_all | solution.py:32
  146.7 8.0 %collective-permute-start.4 = (f32[4,128,128]{2,1,0:T(8,128)S(1)}, f32[4,128,128]{2,1,0:T(8,128)S(1)}, u32[]{:S(2)}, u32[]{:S(2)}) collective-permute-start(f32[4,128,128]{2,1,0:T(8,128)S(1)} %fusion.17), channel_id=1, source_target_pairs={{0,16},{16,0},{32,48},{48,32},{64,80},{80,64},{96,112},{112,96},{1... | collective-permute-start | bytes 786440 | tf_op jit(solution)/shard_map/ppermute | solution.py:87
  154.7 6.3 %collective-permute-done.4 = f32[4,128,128]{2,1,0:T(8,128)S(1)} collective-permute-done((f32[4,128,128]{2,1,0:T(8,128)S(1)}, f32[4,128,128]{2,1,0:T(8,128)S(1)}, u32[]{:S(2)}, u32[]{:S(2)}) %collective-permute-start.4) | collective-permute-done | bytes 262176 | tf_op jit(solution)/shard_map/ppermute | solution.py:87
  161.1 4.3 %collective-permute-start.5 = (f32[4,128,128]{2,1,0:T(8,128)S(1)}, f32[4,128,128]{2,1,0:T(8,128)S(1)}, u32[]{:S(2)}, u32[]{:S(2)}) collective-permute-start(f32[4,128,128]{2,1,0:T(8,128)S(1)} %add.148), channel_id=1, source_target_pairs={{0,32},{16,48},{32,0},{48,16},{64,96},{80,112},{96,64},{112,80},{1... | collective-permute-start | bytes 786440 | tf_op jit(solution)/shard_map/ppermute | solution.py:87
  165.3 11.6 %collective-permute-done.5 = f32[4,128,128]{2,1,0:T(8,128)S(1)} collective-permute-done((f32[4,128,128]{2,1,0:T(8,128)S(1)}, f32[4,128,128]{2,1,0:T(8,128)S(1)}, u32[]{:S(2)}, u32[]{:S(2)}) %collective-permute-start.5) | collective-permute-done | bytes 262176 | tf_op jit(solution)/shard_map/ppermute | solution.py:87
  177.0 4.2 %collective-permute-start.6 = (f32[4,128,128]{2,1,0:T(8,128)S(1)}, f32[4,128,128]{2,1,0:T(8,128)S(1)}, u32[]{:S(2)}, u32[]{:S(2)}) collective-permute-start(f32[4,128,128]{2,1,0:T(8,128)S(1)} %add.149), channel_id=1, source_target_pairs={{0,64},{16,80},{32,96},{48,112},{64,0},{80,16},{96,32},{112,48},{1... | collective-permute-start | bytes 786440 | tf_op jit(solution)/shard_map/ppermute | solution.py:87
  181.2 13.5 %collective-permute-done.6 = f32[4,128,128]{2,1,0:T(8,128)S(1)} collective-permute-done((f32[4,128,128]{2,1,0:T(8,128)S(1)}, f32[4,128,128]{2,1,0:T(8,128)S(1)}, u32[]{:S(2)}, u32[]{:S(2)}) %collective-permute-start.6) | collective-permute-done | bytes 262176 | tf_op jit(solution)/shard_map/ppermute | solution.py:87
  194.8 3.0 collective-permute-start.7
  197.8 7.1 %collective-permute-done.7 = f32[4,128,128]{2,1,0:T(8,128)S(1)} collective-permute-done((f32[4,128,128]{2,1,0:T(8,128)S(1)}, f32[4,128,128]{2,1,0:T(8,128)S(1)}, u32[]{:S(2)}, u32[]{:S(2)}) %collective-permute-start.7) | collective-permute-done | bytes 262176 | tf_op jit(solution)/shard_map/ppermute | solution.py:87
  204.9 3.3 %collective-permute-start.8 = (f32[4,128,128]{2,1,0:T(8,128)S(1)}, f32[4,128,128]{2,1,0:T(8,128)S(1)}, u32[]{:S(2)}, u32[]{:S(2)}) collective-permute-start(f32[4,128,128]{2,1,0:T(8,128)S(1)} %add.151), channel_id=1, source_target_pairs={{0,256},{128,384},{256,0},{384,128},{512,768},{640,896},{768,512},... | collective-permute-start | bytes 786440 | tf_op jit(solution)/shard_map/ppermute | solution.py:87
  208.2 12.5 %collective-permute-done.8 = f32[4,128,128]{2,1,0:T(8,128)S(1)} collective-permute-done((f32[4,128,128]{2,1,0:T(8,128)S(1)}, f32[4,128,128]{2,1,0:T(8,128)S(1)}, u32[]{:S(2)}, u32[]{:S(2)}) %collective-permute-start.8) | collective-permute-done | bytes 262176 | tf_op jit(solution)/shard_map/ppermute | solution.py:87
  220.7 3.8 %collective-permute-start.9 = (f32[4,128,128]{2,1,0:T(8,128)S(1)}, f32[4,128,128]{2,1,0:T(8,128)S(1)}, u32[]{:S(2)}, u32[]{:S(2)}) collective-permute-start(f32[4,128,128]{2,1,0:T(8,128)S(1)} %add.152), channel_id=1, source_target_pairs={{0,512},{128,640},{256,768},{384,896},{512,0},{640,128},{768,256},... | collective-permute-start | bytes 786440 | tf_op jit(solution)/shard_map/ppermute | solution.py:87
  224.5 14.3 %collective-permute-done.9 = f32[4,128,128]{2,1,0:T(8,128)S(1)} collective-permute-done((f32[4,128,128]{2,1,0:T(8,128)S(1)}, f32[4,128,128]{2,1,0:T(8,128)S(1)}, u32[]{:S(2)}, u32[]{:S(2)}) %collective-permute-start.9) | collective-permute-done | bytes 262176 | tf_op jit(solution)/shard_map/ppermute | solution.py:87
  239.6 53.5 %shard_map.94 = (f32[4,128,128]{2,1,0:T(8,128)}, f32[4,128,128]{2,1,0:T(8,128)}) custom-call(f32[4,128,128]{2,1,0:T(8,128)} %add.153.g_ref), custom_call_target="tpu_custom_call" | custom-call | tf_op jit(solution)/shard_map/pallas_call | solution.py:74
  (122 shorter events, 50.2 us)
Async XLA Ops:
  7.2 85.9 %copy-start.3 = (s32[1,64]{1,0:T(1,128)S(1)}, s32[1,64]{1,0:T(1,128)}, u32[]{:S(2)}) copy-start(s32[1,64]{1,0:T(1,128)} %param.17) | copy-start | bytes 772
  7.2 86.2 %copy-start.4 = (s32[1,64]{1,0:T(1,128)S(1)}, s32[1,64]{1,0:T(1,128)}, u32[]{:S(2)}) copy-start(s32[1,64]{1,0:T(1,128)} %param.16) | copy-start | bytes 772
  7.2 86.6 %copy-start.2 = (bf16[128,512]{1,0:T(8,128)(2,1)S(1)}, bf16[128,512]{1,0:T(8,128)(2,1)}, u32[]{:S(2)}) copy-start(bf16[128,512]{1,0:T(8,128)(2,1)} %param.11) | copy-start | bytes 393220
  7.2 84.0 %all-gather.2.cloned.1.call-start = ((), (), s32[]{:S(2)}) async-start(), calls=%async_computation.1 | async-start | bytes 2359296 | tf_op jit(solution)/shard_map/all_gather | solution.py:196
  8.1 5.8 %collective-permute-start = (bf16[128,128]{1,0:T(8,128)(2,1)S(1)}, bf16[128,128]{1,0:T(8,128)(2,1)S(1)}, u32[]{:S(2)}, u32[]{:S(2)}) collective-permute-start(bf16[128,128]{1,0:T(8,128)(2,1)S(1)} %dynamic-slice_select_fusion), channel_id=1, source_target_pairs={{0,16},{16,0},{32,48},{48,32},{64,80},{80,64},{96,112},{112,96},{1... | collective-permute-start | bytes 98312 | tf_op jit(solution)/shard_map/ppermute | solution.py:98
  13.9 7.1 %collective-permute-start.1 = (bf16[256,128]{1,0:T(8,128)(2,1)S(1)}, bf16[256,128]{1,0:T(8,128)(2,1)S(1)}, u32[]{:S(2)}, u32[]{:S(2)}) collective-permute-start(bf16[256,128]{1,0:T(8,128)(2,1)S(1)} %pad_maximum_fusion.2), channel_id=1, source_target_pairs={{0,32},{16,48},{32,0},{48,16},{64,96},{80,112},{96,64},{112,80},{1... | collective-permute-start | bytes 196616 | tf_op jit(solution)/shard_map/ppermute | solution.py:98
  21.0 18.5 %collective-permute-start.2 = (bf16[512,128]{1,0:T(8,128)(2,1)S(1)}, bf16[512,128]{1,0:T(8,128)(2,1)S(1)}, u32[]{:S(2)}, u32[]{:S(2)}) collective-permute-start(bf16[512,128]{1,0:T(8,128)(2,1)S(1)} %pad_maximum_fusion.1), channel_id=1, source_target_pairs={{0,64},{16,80},{32,96},{48,112},{64,0},{80,16},{96,32},{112,48},{1... | collective-permute-start | bytes 393224 | tf_op jit(solution)/shard_map/ppermute | solution.py:98
  91.2 6.4 %collective-permute-start.3 = (bf16[8192,128]{1,0:T(8,128)(2,1)}, bf16[8192,128]{1,0:T(8,128)(2,1)}, u32[]{:S(2)}, u32[]{:S(2)}) collective-permute-start(bf16[8192,128]{1,0:T(8,128)(2,1)} %all-gather.2.cloned.1.call-done), channel_id=1, source_target_pairs={{0,1},{1,0},{2,3},{3,2},{4,5},{5,4},{6,7},{7,6},{8,9},{9,8},{10,11... | collective-permute-start | bytes 6291464 | tf_op jit(solution)/shard_map/ppermute | solution.py:197
  101.4 27.8 %copy-start = (bf16[128,512]{1,0:T(8,128)(2,1)S(1)}, bf16[128,512]{1,0:T(8,128)(2,1)}, u32[]{:S(2)}) copy-start(bf16[128,512]{1,0:T(8,128)(2,1)} %param.14) | copy-start | bytes 393220
  129.4 65.4 %copy-start.1 = (bf16[128,512]{1,0:T(8,128)(2,1)}, bf16[128,512]{1,0:T(8,128)(2,1)S(1)}, u32[]{:S(2)}) copy-start(bf16[128,512]{1,0:T(8,128)(2,1)S(1)} %get-tuple-element.348) | copy-start | bytes 393220
  130.0 15.7 %all-to-all-start = ((f32[16,1,128]{2,1,0:T(1,128)}), f32[16,1,128]{2,1,0:T(1,128)S(1)}, u32[]{:S(2)}, u32[]{:S(2)}) async-start(f32[16,1,128]{2,1,0:T(1,128)} %broadcast_in_dim.107), calls=%async_computation | async-start | bytes 16384 | tf_op jit(solution)/shard_map/all_to_all | solution.py:32
  146.7 14.3 %collective-permute-start.4 = (f32[4,128,128]{2,1,0:T(8,128)S(1)}, f32[4,128,128]{2,1,0:T(8,128)S(1)}, u32[]{:S(2)}, u32[]{:S(2)}) collective-permute-start(f32[4,128,128]{2,1,0:T(8,128)S(1)} %fusion.17), channel_id=1, source_target_pairs={{0,16},{16,0},{32,48},{48,32},{64,80},{80,64},{96,112},{112,96},{1... | collective-permute-start | bytes 786440 | tf_op jit(solution)/shard_map/ppermute | solution.py:87
  161.1 15.9 %collective-permute-start.5 = (f32[4,128,128]{2,1,0:T(8,128)S(1)}, f32[4,128,128]{2,1,0:T(8,128)S(1)}, u32[]{:S(2)}, u32[]{:S(2)}) collective-permute-start(f32[4,128,128]{2,1,0:T(8,128)S(1)} %add.148), channel_id=1, source_target_pairs={{0,32},{16,48},{32,0},{48,16},{64,96},{80,112},{96,64},{112,80},{1... | collective-permute-start | bytes 786440 | tf_op jit(solution)/shard_map/ppermute | solution.py:87
  177.0 17.7 %collective-permute-start.6 = (f32[4,128,128]{2,1,0:T(8,128)S(1)}, f32[4,128,128]{2,1,0:T(8,128)S(1)}, u32[]{:S(2)}, u32[]{:S(2)}) collective-permute-start(f32[4,128,128]{2,1,0:T(8,128)S(1)} %add.149), channel_id=1, source_target_pairs={{0,64},{16,80},{32,96},{48,112},{64,0},{80,16},{96,32},{112,48},{1... | collective-permute-start | bytes 786440 | tf_op jit(solution)/shard_map/ppermute | solution.py:87
  194.8 10.1 %collective-permute-start.7 = (f32[4,128,128]{2,1,0:T(8,128)S(1)}, f32[4,128,128]{2,1,0:T(8,128)S(1)}, u32[]{:S(2)}, u32[]{:S(2)}) collective-permute-start(f32[4,128,128]{2,1,0:T(8,128)S(1)} %add.150), channel_id=1, source_target_pairs={{0,128},{128,0},{256,384},{384,256},{512,640},{640,512},{768,896},... | collective-permute-start | bytes 786440 | tf_op jit(solution)/shard_map/ppermute | solution.py:87
  204.9 15.8 %collective-permute-start.8 = (f32[4,128,128]{2,1,0:T(8,128)S(1)}, f32[4,128,128]{2,1,0:T(8,128)S(1)}, u32[]{:S(2)}, u32[]{:S(2)}) collective-permute-start(f32[4,128,128]{2,1,0:T(8,128)S(1)} %add.151), channel_id=1, source_target_pairs={{0,256},{128,384},{256,0},{384,128},{512,768},{640,896},{768,512},... | collective-permute-start | bytes 786440 | tf_op jit(solution)/shard_map/ppermute | solution.py:87
  220.7 18.1 %collective-permute-start.9 = (f32[4,128,128]{2,1,0:T(8,128)S(1)}, f32[4,128,128]{2,1,0:T(8,128)S(1)}, u32[]{:S(2)}, u32[]{:S(2)}) collective-permute-start(f32[4,128,128]{2,1,0:T(8,128)S(1)} %add.152), channel_id=1, source_target_pairs={{0,512},{128,640},{256,768},{384,896},{512,0},{640,128},{768,256},... | collective-permute-start | bytes 786440 | tf_op jit(solution)/shard_map/ppermute | solution.py:87
Sparse Core Ops, SparseCore 0:
  40.5 50.6 all-gather.1

commit v4 on v3

--- a/solution.py
+++ b/solution.py
@@ -39,10 +39,13 @@
     return jnp.sum(everything, axis=0)
 
 
+TILE = 16
+
+
 def factor_kernel(g_ref, u_ref, li_ref, m_ref):
     heads, n, _ = g_ref.shape
-    row_ids = lax.broadcasted_iota(jnp.int32, (n, 1), 0)
     lane_ids = lax.broadcasted_iota(jnp.int32, (1, n), 1)
+    tile_rows = lax.broadcasted_iota(jnp.int32, (TILE, 1), 0)
     eye = (lax.broadcasted_iota(jnp.int32, (n, n), 0) == lax.broadcasted_iota(jnp.int32, (n, n), 1)).astype(jnp.float32)
     for h in range(heads):
         m_ref[h, :, :n] = g_ref[h]
@@ -50,15 +53,27 @@
 
     def step(j, carry):
         pick = lane_ids == j
+        scales, rows = [], []
         for h in range(heads):
             row = m_ref[h, pl.ds(j, 1), :]
             pivot = jnp.sum(jnp.where(pick, row[:, :n], 0.0), axis=1, keepdims=True)
             scale = lax.rsqrt(pivot)
             scaled = row * scale
-            column = jnp.sum(jnp.where(pick, m_ref[h, :, :n], 0.0), axis=1, keepdims=True)
-            column = jnp.where(row_ids > j, column * scale, 0.0)
-            m_ref[h] = m_ref[h] - column * scaled
             m_ref[h, pl.ds(j, 1), :] = scaled
+            scales.append(scale)
+            rows.append(scaled)
+
+        def update(t, inner):
+            first = pl.multiple_of(t * TILE, TILE)
+            below = (tile_rows + first) > j
+            for h in range(heads):
+                block = m_ref[h, pl.ds(first, TILE), :]
+                column = jnp.sum(jnp.where(pick, block[:, :n], 0.0), axis=1, keepdims=True)
+                column = jnp.where(below, column * scales[h], 0.0)
+                m_ref[h, pl.ds(first, TILE), :] = block - column * rows[h]
+            return inner
+
+        lax.fori_loop((j + 1) // TILE, n // TILE, update, 0)
         return carry
 
     lax.fori_loop(0, n, step, 0)
@@ -78,6 +93,27 @@
         out_specs=(pl.BlockSpec(memory_space=pltpu.VMEM), pl.BlockSpec(memory_space=pltpu.VMEM)),
         scratch_shapes=[pltpu.VMEM((heads, n, 2 * n), jnp.float32)],
     )(gram)
+
+
+def fold_pairs(gram):
+    heads, n, _ = gram.shape
+    upper = lax.broadcasted_iota(jnp.int32, (n, n), 0) <= lax.broadcasted_iota(jnp.int32, (n, n), 1)
+    first, second = gram[0::2], gram[1::2]
+    square = jnp.where(upper[None], first, second)
+    diagonal = jnp.diagonal(second, axis1=1, axis2=2)[:, None, :]
+    return jnp.concatenate([square, diagonal], axis=1)
+
+
+def unfold_pairs(folded):
+    pairs, _, n = folded.shape
+    square, diagonal = folded[:, :n, :], folded[:, n, :]
+    rows = lax.broadcasted_iota(jnp.int32, (n, n), 0)
+    cols = lax.broadcasted_iota(jnp.int32, (n, n), 1)
+    upper_part = jnp.where((rows <= cols)[None], square, 0.0)
+    first = upper_part + jnp.swapaxes(jnp.where((rows < cols)[None], square, 0.0), 1, 2)
+    lower_part = jnp.where((rows > cols)[None], square, 0.0)
+    second = lower_part + jnp.swapaxes(lower_part, 1, 2) + jnp.where((rows == cols)[None], diagonal[:, None, :], 0.0)
+    return jnp.stack([first, second], axis=1).reshape(2 * pairs, n, n)
 
 
 def exchange_sum(value, axis):
@@ -220,7 +256,7 @@
     normed = mixed * lax.rsqrt(square_sum[:, None] / WIDTH + EPSILON) * gain_cols[None, :]
     blocks = normed.reshape(row_count, head_count, HD)
     head_rows = jnp.transpose(blocks, (1, 0, 2))
-    gram_sum = exchange_sum(exchange_sum(gram_of(head_rows), "x"), "y")
+    gram_sum = unfold_pairs(exchange_sum(exchange_sum(fold_pairs(gram_of(head_rows)), "x"), "y"))
     upper_factor, lower_inverse = factor(gram_sum)
     r_factor = upper_factor / math.sqrt(total_rows)
     solved = jnp.einsum("rhc,hdc->rhd", blocks, lower_inverse, precision=lax.Precision.HIGHEST)

time: 306 us -> 296 us (0.967)
  waiting for transfers between devices: 135 us -> 106 us
  Pallas kernels: 53.5 us -> 64.6 us
  local copies, waits for them, and re-layouts: 3.11 us -> 10.8 us
  starting transfers between devices: 59.7 us -> 64.2 us
    ppermute x6, waiting for transfers between devices: 65.3 us -> 36.7 us  [exchange_sum(): partner = lax.ppermute(value, axis, [(i, i ^ step) for i in range(count)])]
    pallas_call x1, Pallas kernels: 53.5 us -> 64.6 us  [factor(): pl.pallas_call(factor_kernel, out_shape=(shape, shape), in_specs=[pl.Bloc...]
    slice x0 -> x3, local copies, waits for them, and re-layouts: none -> 4.71 us  [the longest x1 4.62 us: fold_pairs(): first, second = (gram[0::2], gram[1::2])]
    ppermute x6, starting transfers between devices: 26.6 us -> 31 us  [exchange_sum(): partner = lax.ppermute(value, axis, [(i, i ^ step) for i in range(count)])]
    dot_general x6 -> x5, matrix products: 8.43 us -> 7.02 us  [accumulate(): jnp.einsum('rkgd,nkd->kgrn', query_heads, key_heads, preferred_element_ty...]
where the time goes in v4:
time: 296 us; the launch traced here: 295 us
  waiting for transfers between devices  106 us (36%)
  Pallas kernels  64.6 us (22%)
  starting transfers between devices  64.2 us (22%)
  other arithmetic  17.8 us (6%)
  between operations  14.6 us (5%)
  matrix products  11.9 us (4%)
  local copies, waits for them, and re-layouts  10.8 us (4%)
  loops' own time  5.82 us (2%)
    pallas_call x1, Pallas kernels, factor(): pl.pallas_call(factor_kernel, out_shape=(shape, shape), in_specs=[pl.Bloc...  64.6 us
    all_gather x1, waiting for transfers between devices, local(): lax.all_gather(exchange_gather(mine, 'x'), 'y', axis=0, tiled=True)  50.8 us
    ppermute x6, waiting for transfers between devices, exchange_sum(): partner = lax.ppermute(value, axis, [(i, i ^ step) for i in range(count)])  36.7 us
    ppermute x6, starting transfers between devices, exchange_sum(): partner = lax.ppermute(value, axis, [(i, i ^ step) for i in range(count)])  31 us
    ppermute x3, starting transfers between devices, exchange_gather(): partner = lax.ppermute(value, axis, [(i, i ^ step) for i in range(count)])  23 us
    ppermute x3, waiting for transfers between devices, exchange_gather(): partner = lax.ppermute(value, axis, [(i, i ^ step) for i in range(count)])  8.31 us
    all_to_all x1, starting transfers between devices, copy_for_each(): lax.all_to_all(jnp.broadcast_to(shard[None], (count, *shard.shape)), axis...  8.21 us
    reduce_or x8, other arithmetic, attend_block(): return lax.cond(jnp.any(seen), accumulate, unchanged, state_now)  7.76 us
  transfers between devices with their start and end apart: 12, of which 12 were waited for; matrix products, arithmetic and copies ran while one was open for 1% of the time, Pallas kernels for 0%

profile of v4, /device:TPU:14, one launch (start us, length us, event | category | flops | bytes accessed | tf_op | source)
XLA Modules:
  0.0 295.5 jit_solution(5990345808882226278)
XLA Ops:
  8.1 3.3 %collective-permute-start = (bf16[128,128]{1,0:T(8,128)(2,1)S(1)}, bf16[128,128]{1,0:T(8,128)(2,1)S(1)}, u32[]{:S(2)}, u32[]{:S(2)}) collective-permute-start(bf16[128,128]{1,0:T(8,128)(2,1)S(1)} %dynamic-slice_select_fusion), channel_id=1, source_target_pairs={{0,16},{16,0},{32,48},{48,32},{64,80},{80,64},{96,112},{112,96},{1... | collective-permute-start | bytes 98312 | tf_op jit(solution)/shard_map/ppermute | solution.py:134
  13.9 4.2 %collective-permute-start.1 = (bf16[256,128]{1,0:T(8,128)(2,1)S(1)}, bf16[256,128]{1,0:T(8,128)(2,1)S(1)}, u32[]{:S(2)}, u32[]{:S(2)}) collective-permute-start(bf16[256,128]{1,0:T(8,128)(2,1)S(1)} %pad_maximum_fusion.4), channel_id=1, source_target_pairs={{0,32},{16,48},{32,0},{48,16},{64,96},{80,112},{96,64},{112,80},{1... | collective-permute-start | bytes 196616 | tf_op jit(solution)/shard_map/ppermute | solution.py:134
  18.2 2.8 collective-permute-done.1
  21.0 15.5 %collective-permute-start.2 = (bf16[512,128]{1,0:T(8,128)(2,1)S(1)}, bf16[512,128]{1,0:T(8,128)(2,1)S(1)}, u32[]{:S(2)}, u32[]{:S(2)}) collective-permute-start(bf16[512,128]{1,0:T(8,128)(2,1)S(1)} %pad_maximum_fusion.3), channel_id=1, source_target_pairs={{0,64},{16,80},{32,96},{48,112},{64,0},{80,16},{96,32},{112,48},{1... | collective-permute-start | bytes 393224 | tf_op jit(solution)/shard_map/ppermute | solution.py:134
  36.5 3.0 %collective-permute-done.2 = bf16[512,128]{1,0:T(8,128)(2,1)S(1)} collective-permute-done((bf16[512,128]{1,0:T(8,128)(2,1)S(1)}, bf16[512,128]{1,0:T(8,128)(2,1)S(1)}, u32[]{:S(2)}, u32[]{:S(2)}) %collective-permute-start.2) | collective-permute-done | bytes 131104 | tf_op jit(solution)/shard_map/ppermute | solution.py:134
  40.3 50.8 %all-gather.2.cloned.1.call-done = bf16[8192,128]{1,0:T(8,128)(2,1)} async-done(((bf16[1024,128]{1,0:T(8,128)(2,1)}), bf16[8192,128]{1,0:T(8,128)(2,1)}) %all-gather.2.cloned.1.call-update) | async-done | bytes 2097168 | tf_op jit(solution)/shard_map/all_gather | solution.py:232
  94.1 3.4 %collective-permute-done.3 = bf16[8192,128]{1,0:T(8,128)(2,1)} collective-permute-done((bf16[8192,128]{1,0:T(8,128)(2,1)}, bf16[8192,128]{1,0:T(8,128)(2,1)}, u32[]{:S(2)}, u32[]{:S(2)}) %collective-permute-start.3) | collective-permute-done | bytes 2097184 | tf_op jit(solution)/shard_map/ppermute | solution.py:233
  97.6 3.8 %broadcast_select_fusion = (bf16[8192,128]{1,0:T(8,128)(2,1)S(1)}, bf16[8192,128]{1,0:T(8,128)(2,1)}) fusion(bf16[8192,128]{1,0:T(8,128)(2,1)} %collective-permute-done.3, bf16[8192,128]{1,0:T(8,128)(2,1)} %all-gather.2.cloned.1.call-done, pred[]{:T(512)S(6)} %eq.77), kind=kLoop, calls=%fused_computation.21 | loop fusion | flops 2097152 | bytes 8388609 | tf_op jit(solution)/shard_map/jit(_where)/select_n | solution.py:235
  101.4 25.2 %while.17 = (s32[]{:T(128)}, f32[1,4,128]{2,1,0:T(4,128)S(1)}, f32[1,4,128]{2,1,0:T(4,128)S(1)}, f32[1,4,128,128]{3,2,1,0:T(8,128)S(1)}, s32[8192]{0:T(1024)S(1)...) while((s32[]{:T(128)}, f32[1,4,128]{2,1,0:T(4,128)S(1)}, ...), condition=%wide.region_9.10_spmd, body=%wide.region_3.9_spmd.sunk | while | flops 272762368 | bytes 7792453 | solution.py:245
  127.7 8.2 %all-to-all-start = ((f32[16,1,128]{2,1,0:T(1,128)}), f32[16,1,128]{2,1,0:T(1,128)S(1)}, u32[]{:S(2)}, u32[]{:S(2)}) async-start(f32[16,1,128]{2,1,0:T(1,128)} %broadcast_in_dim.172), calls=%async_computation | async-start | bytes 16384 | tf_op jit(solution)/shard_map/all_to_all | solution.py:32
  136.8 6.6 %all-to-all-done = f32[16,1,128]{2,1,0:T(1,128)S(1)} async-done(((f32[16,1,128]{2,1,0:T(1,128)}), f32[16,1,128]{2,1,0:T(1,128)S(1)}, u32[]{:S(2)}, u32[]{:S(2)}) %all-to-all-start) | async-done | bytes 8224 | tf_op jit(solution)/shard_map/all_to_all | solution.py:32
  144.4 4.6 %copy.70 = f32[2,128,128]{0,2,1:T(8,128)} copy(f32[2,128,128]{2,1,0:T(8,128)S(1)} %get-tuple-element.354) | data formatting | bytes 262144 | tf_op jit(solution)/shard_map/slice | solution.py:101
  150.9 10.3 %collective-permute-start.4 = (f32[2,129,128]{2,1,0:T(8,128)S(1)}, f32[2,129,128]{2,1,0:T(8,128)S(1)}, u32[]{:S(2)}, u32[]{:S(2)}) collective-permute-start(f32[2,129,128]{2,1,0:T(8,128)S(1)} %pad_maximum_fusion.2), channel_id=1, source_target_pairs={{0,16},{16,0},{32,48},{48,32},{64,80},{80,64},{96,112},{112,96},{1... | collective-permute-start | bytes 396296 | tf_op jit(solution)/shard_map/ppermute | solution.py:123
  161.2 3.7 %collective-permute-done.4 = f32[2,129,128]{2,1,0:T(8,128)S(1)} collective-permute-done((f32[2,129,128]{2,1,0:T(8,128)S(1)}, f32[2,129,128]{2,1,0:T(8,128)S(1)}, u32[]{:S(2)}, u32[]{:S(2)}) %collective-permute-start.4) | collective-permute-done | bytes 132128 | tf_op jit(solution)/shard_map/ppermute | solution.py:123
  164.9 4.5 %collective-permute-start.5 = (f32[2,129,128]{2,1,0:T(8,128)S(1)}, f32[2,129,128]{2,1,0:T(8,128)S(1)}, u32[]{:S(2)}, u32[]{:S(2)}) collective-permute-start(f32[2,129,128]{2,1,0:T(8,128)S(1)} %fusion.18), channel_id=1, source_target_pairs={{0,32},{16,48},{32,0},{48,16},{64,96},{80,112},{96,64},{112,80},{1... | collective-permute-start | bytes 396296 | tf_op jit(solution)/shard_map/ppermute | solution.py:123
  169.5 6.1 %collective-permute-done.5 = f32[2,129,128]{2,1,0:T(8,128)S(1)} collective-permute-done((f32[2,129,128]{2,1,0:T(8,128)S(1)}, f32[2,129,128]{2,1,0:T(8,128)S(1)}, u32[]{:S(2)}, u32[]{:S(2)}) %collective-permute-start.5) | collective-permute-done | bytes 132128 | tf_op jit(solution)/shard_map/ppermute | solution.py:123
  175.6 5.1 %collective-permute-start.6 = (f32[2,129,128]{2,1,0:T(8,128)S(1)}, f32[2,129,128]{2,1,0:T(8,128)S(1)}, u32[]{:S(2)}, u32[]{:S(2)}) collective-permute-start(f32[2,129,128]{2,1,0:T(8,128)S(1)} %add.162), channel_id=1, source_target_pairs={{0,64},{16,80},{32,96},{48,112},{64,0},{80,16},{96,32},{112,48},{1... | collective-permute-start | bytes 396296 | tf_op jit(solution)/shard_map/ppermute | solution.py:123
  180.7 8.3 %collective-permute-done.6 = f32[2,129,128]{2,1,0:T(8,128)S(1)} collective-permute-done((f32[2,129,128]{2,1,0:T(8,128)S(1)}, f32[2,129,128]{2,1,0:T(8,128)S(1)}, u32[]{:S(2)}, u32[]{:S(2)}) %collective-permute-start.6) | collective-permute-done | bytes 132128 | tf_op jit(solution)/shard_map/ppermute | solution.py:123
  189.1 3.2 %collective-permute-start.7 = (f32[2,129,128]{2,1,0:T(8,128)S(1)}, f32[2,129,128]{2,1,0:T(8,128)S(1)}, u32[]{:S(2)}, u32[]{:S(2)}) collective-permute-start(f32[2,129,128]{2,1,0:T(8,128)S(1)} %add.163), channel_id=1, source_target_pairs={{0,128},{128,0},{256,384},{384,256},{512,640},{640,512},{768,896},... | collective-permute-start | bytes 396296 | tf_op jit(solution)/shard_map/ppermute | solution.py:123
  192.3 3.9 %collective-permute-done.7 = f32[2,129,128]{2,1,0:T(8,128)S(1)} collective-permute-done((f32[2,129,128]{2,1,0:T(8,128)S(1)}, f32[2,129,128]{2,1,0:T(8,128)S(1)}, u32[]{:S(2)}, u32[]{:S(2)}) %collective-permute-start.7) | collective-permute-done | bytes 132128 | tf_op jit(solution)/shard_map/ppermute | solution.py:123
  198.2 8.2 %collective-permute-done.8 = f32[2,129,128]{2,1,0:T(8,128)S(1)} collective-permute-done((f32[2,129,128]{2,1,0:T(8,128)S(1)}, f32[2,129,128]{2,1,0:T(8,128)S(1)}, u32[]{:S(2)}, u32[]{:S(2)}) %collective-permute-start.8) | collective-permute-done | bytes 132128 | tf_op jit(solution)/shard_map/ppermute | solution.py:123
  206.4 5.8 %collective-permute-start.9 = (f32[2,129,128]{2,1,0:T(8,128)S(1)}, f32[2,129,128]{2,1,0:T(8,128)S(1)}, u32[]{:S(2)}, u32[]{:S(2)}) collective-permute-start(f32[2,129,128]{2,1,0:T(8,128)S(1)} %add.165), channel_id=1, source_target_pairs={{0,512},{128,640},{256,768},{384,896},{512,0},{640,128},{768,256},... | collective-permute-start | bytes 396296 | tf_op jit(solution)/shard_map/ppermute | solution.py:123
  212.3 6.5 %collective-permute-done.9 = f32[2,129,128]{2,1,0:T(8,128)S(1)} collective-permute-done((f32[2,129,128]{2,1,0:T(8,128)S(1)}, f32[2,129,128]{2,1,0:T(8,128)S(1)}, u32[]{:S(2)}, u32[]{:S(2)}) %collective-permute-start.9) | collective-permute-done | bytes 132128 | tf_op jit(solution)/shard_map/ppermute | solution.py:123
  220.2 64.6 %shard_map.94 = (f32[4,128,128]{2,1,0:T(8,128)}, f32[4,128,128]{2,1,0:T(8,128)}) custom-call(f32[4,128,128]{2,1,0:T(8,128)} %bitcast.90), custom_call_target="tpu_custom_call" | custom-call | tf_op jit(solution)/shard_map/pallas_call | solution.py:89
  (139 shorter events, 50.1 us)
Async XLA Ops:
  7.2 85.9 %copy-start.3 = (s32[1,64]{1,0:T(1,128)S(1)}, s32[1,64]{1,0:T(1,128)}, u32[]{:S(2)}) copy-start(s32[1,64]{1,0:T(1,128)} %param.17) | copy-start | bytes 772
  7.2 86.2 %copy-start.4 = (s32[1,64]{1,0:T(1,128)S(1)}, s32[1,64]{1,0:T(1,128)}, u32[]{:S(2)}) copy-start(s32[1,64]{1,0:T(1,128)} %param.16) | copy-start | bytes 772
  7.2 86.6 %copy-start.2 = (bf16[128,512]{1,0:T(8,128)(2,1)S(1)}, bf16[128,512]{1,0:T(8,128)(2,1)}, u32[]{:S(2)}) copy-start(bf16[128,512]{1,0:T(8,128)(2,1)} %param.11) | copy-start | bytes 393220
  7.2 84.0 %all-gather.2.cloned.1.call-start = ((), (), s32[]{:S(2)}) async-start(), calls=%async_computation.1 | async-start | bytes 2359296 | tf_op jit(solution)/shard_map/all_gather | solution.py:232
  8.1 5.8 %collective-permute-start = (bf16[128,128]{1,0:T(8,128)(2,1)S(1)}, bf16[128,128]{1,0:T(8,128)(2,1)S(1)}, u32[]{:S(2)}, u32[]{:S(2)}) collective-permute-start(bf16[128,128]{1,0:T(8,128)(2,1)S(1)} %dynamic-slice_select_fusion), channel_id=1, source_target_pairs={{0,16},{16,0},{32,48},{48,32},{64,80},{80,64},{96,112},{112,96},{1... | collective-permute-start | bytes 98312 | tf_op jit(solution)/shard_map/ppermute | solution.py:134
  13.9 7.1 %collective-permute-start.1 = (bf16[256,128]{1,0:T(8,128)(2,1)S(1)}, bf16[256,128]{1,0:T(8,128)(2,1)S(1)}, u32[]{:S(2)}, u32[]{:S(2)}) collective-permute-start(bf16[256,128]{1,0:T(8,128)(2,1)S(1)} %pad_maximum_fusion.4), channel_id=1, source_target_pairs={{0,32},{16,48},{32,0},{48,16},{64,96},{80,112},{96,64},{112,80},{1... | collective-permute-start | bytes 196616 | tf_op jit(solution)/shard_map/ppermute | solution.py:134
  21.0 18.5 %collective-permute-start.2 = (bf16[512,128]{1,0:T(8,128)(2,1)S(1)}, bf16[512,128]{1,0:T(8,128)(2,1)S(1)}, u32[]{:S(2)}, u32[]{:S(2)}) collective-permute-start(bf16[512,128]{1,0:T(8,128)(2,1)S(1)} %pad_maximum_fusion.3), channel_id=1, source_target_pairs={{0,64},{16,80},{32,96},{48,112},{64,0},{80,16},{96,32},{112,48},{1... | collective-permute-start | bytes 393224 | tf_op jit(solution)/shard_map/ppermute | solution.py:134
  91.2 6.4 %collective-permute-start.3 = (bf16[8192,128]{1,0:T(8,128)(2,1)}, bf16[8192,128]{1,0:T(8,128)(2,1)}, u32[]{:S(2)}, u32[]{:S(2)}) collective-permute-start(bf16[8192,128]{1,0:T(8,128)(2,1)} %all-gather.2.cloned.1.call-done), channel_id=1, source_target_pairs={{0,1},{1,0},{2,3},{3,2},{4,5},{5,4},{6,7},{7,6},{8,9},{9,8},{10,11... | collective-permute-start | bytes 6291464 | tf_op jit(solution)/shard_map/ppermute | solution.py:233
  101.4 25.5 %copy-start = (bf16[128,512]{1,0:T(8,128)(2,1)S(1)}, bf16[128,512]{1,0:T(8,128)(2,1)}, u32[]{:S(2)}) copy-start(bf16[128,512]{1,0:T(8,128)(2,1)} %param.14) | copy-start | bytes 393220
  127.1 22.0 %copy-start.1 = (bf16[128,512]{1,0:T(8,128)(2,1)}, bf16[128,512]{1,0:T(8,128)(2,1)S(1)}, u32[]{:S(2)}) copy-start(bf16[128,512]{1,0:T(8,128)(2,1)S(1)} %get-tuple-element.348) | copy-start | bytes 393220
  127.7 15.7 %all-to-all-start = ((f32[16,1,128]{2,1,0:T(1,128)}), f32[16,1,128]{2,1,0:T(1,128)S(1)}, u32[]{:S(2)}, u32[]{:S(2)}) async-start(f32[16,1,128]{2,1,0:T(1,128)} %broadcast_in_dim.172), calls=%async_computation | async-start | bytes 16384 | tf_op jit(solution)/shard_map/all_to_all | solution.py:32
  150.9 14.0 %collective-permute-start.4 = (f32[2,129,128]{2,1,0:T(8,128)S(1)}, f32[2,129,128]{2,1,0:T(8,128)S(1)}, u32[]{:S(2)}, u32[]{:S(2)}) collective-permute-start(f32[2,129,128]{2,1,0:T(8,128)S(1)} %pad_maximum_fusion.2), channel_id=1, source_target_pairs={{0,16},{16,0},{32,48},{48,32},{64,80},{80,64},{96,112},{112,96},{1... | collective-permute-start | bytes 396296 | tf_op jit(solution)/shard_map/ppermute | solution.py:123
  164.9 10.6 %collective-permute-start.5 = (f32[2,129,128]{2,1,0:T(8,128)S(1)}, f32[2,129,128]{2,1,0:T(8,128)S(1)}, u32[]{:S(2)}, u32[]{:S(2)}) collective-permute-start(f32[2,129,128]{2,1,0:T(8,128)S(1)} %fusion.18), channel_id=1, source_target_pairs={{0,32},{16,48},{32,0},{48,16},{64,96},{80,112},{96,64},{112,80},{1... | collective-permute-start | bytes 396296 | tf_op jit(solution)/shard_map/ppermute | solution.py:123
  175.6 13.5 %collective-permute-start.6 = (f32[2,129,128]{2,1,0:T(8,128)S(1)}, f32[2,129,128]{2,1,0:T(8,128)S(1)}, u32[]{:S(2)}, u32[]{:S(2)}) collective-permute-start(f32[2,129,128]{2,1,0:T(8,128)S(1)} %add.162), channel_id=1, source_target_pairs={{0,64},{16,80},{32,96},{48,112},{64,0},{80,16},{96,32},{112,48},{1... | collective-permute-start | bytes 396296 | tf_op jit(solution)/shard_map/ppermute | solution.py:123
  189.1 7.1 %collective-permute-start.7 = (f32[2,129,128]{2,1,0:T(8,128)S(1)}, f32[2,129,128]{2,1,0:T(8,128)S(1)}, u32[]{:S(2)}, u32[]{:S(2)}) collective-permute-start(f32[2,129,128]{2,1,0:T(8,128)S(1)} %add.163), channel_id=1, source_target_pairs={{0,128},{128,0},{256,384},{384,256},{512,640},{640,512},{768,896},... | collective-permute-start | bytes 396296 | tf_op jit(solution)/shard_map/ppermute | solution.py:123
  196.2 10.2 %collective-permute-start.8 = (f32[2,129,128]{2,1,0:T(8,128)S(1)}, f32[2,129,128]{2,1,0:T(8,128)S(1)}, u32[]{:S(2)}, u32[]{:S(2)}) collective-permute-start(f32[2,129,128]{2,1,0:T(8,128)S(1)} %add.164), channel_id=1, source_target_pairs={{0,256},{128,384},{256,0},{384,128},{512,768},{640,896},{768,512},... | collective-permute-start | bytes 396296 | tf_op jit(solution)/shard_map/ppermute | solution.py:123
  206.4 12.4 %collective-permute-start.9 = (f32[2,129,128]{2,1,0:T(8,128)S(1)}, f32[2,129,128]{2,1,0:T(8,128)S(1)}, u32[]{:S(2)}, u32[]{:S(2)}) collective-permute-start(f32[2,129,128]{2,1,0:T(8,128)S(1)} %add.165), channel_id=1, source_target_pairs={{0,512},{128,640},{256,768},{384,896},{512,0},{640,128},{768,256},... | collective-permute-start | bytes 396296 | tf_op jit(solution)/shard_map/ppermute | solution.py:123
Sparse Core Ops, SparseCore 0:
  40.5 50.6 all-gather.1

commit v5 on v4

--- a/solution.py
+++ b/solution.py
@@ -39,41 +39,28 @@
     return jnp.sum(everything, axis=0)
 
 
-TILE = 16
-
-
 def factor_kernel(g_ref, u_ref, li_ref, m_ref):
     heads, n, _ = g_ref.shape
+    row_ids = lax.broadcasted_iota(jnp.int32, (n, 1), 0)
     lane_ids = lax.broadcasted_iota(jnp.int32, (1, n), 1)
-    tile_rows = lax.broadcasted_iota(jnp.int32, (TILE, 1), 0)
     eye = (lax.broadcasted_iota(jnp.int32, (n, n), 0) == lax.broadcasted_iota(jnp.int32, (n, n), 1)).astype(jnp.float32)
     for h in range(heads):
         m_ref[h, :, :n] = g_ref[h]
         m_ref[h, :, n:] = eye
+    spare = jnp.zeros((8 - heads, n), jnp.float32)
 
     def step(j, carry):
         pick = lane_ids == j
-        scales, rows = [], []
+        below = row_ids > j
+        rows = [m_ref[h, pl.ds(j, 1), :] for h in range(heads)]
+        columns = jnp.transpose(jnp.concatenate([r[:, :n] for r in rows] + [spare], axis=0))
         for h in range(heads):
-            row = m_ref[h, pl.ds(j, 1), :]
-            pivot = jnp.sum(jnp.where(pick, row[:, :n], 0.0), axis=1, keepdims=True)
+            pivot = jnp.sum(jnp.where(pick, rows[h][:, :n], 0.0), axis=1, keepdims=True)
             scale = lax.rsqrt(pivot)
-            scaled = row * scale
+            scaled = rows[h] * scale
+            column = jnp.where(below, columns[:, h : h + 1] * scale, 0.0)
+            m_ref[h] = m_ref[h] - column * scaled
             m_ref[h, pl.ds(j, 1), :] = scaled
-            scales.append(scale)
-            rows.append(scaled)
-
-        def update(t, inner):
-            first = pl.multiple_of(t * TILE, TILE)
-            below = (tile_rows + first) > j
-            for h in range(heads):
-                block = m_ref[h, pl.ds(first, TILE), :]
-                column = jnp.sum(jnp.where(pick, block[:, :n], 0.0), axis=1, keepdims=True)
-                column = jnp.where(below, column * scales[h], 0.0)
-                m_ref[h, pl.ds(first, TILE), :] = block - column * rows[h]
-            return inner
-
-        lax.fori_loop((j + 1) // TILE, n // TILE, update, 0)
         return carry
 
     lax.fori_loop(0, n, step, 0)

time: 296 us -> 290 us (0.980)
  Pallas kernels: 64.6 us -> 57.9 us
  matrix products: 11.9 us -> 7.91 us
  starting transfers between devices: 64.2 us -> 67.6 us
    pallas_call x1, Pallas kernels: 64.6 us -> 57.9 us  [factor(): pl.pallas_call(factor_kernel, out_shape=(shape, shape), in_specs=[pl.Bloc...]
    ppermute x6, starting transfers between devices: 31 us -> 34.5 us  [exchange_sum(): partner = lax.ppermute(value, axis, [(i, i ^ step) for i in range(count)])]
    dot_general x5 -> x3, matrix products: 7.02 us -> 4.21 us  [accumulate(): jnp.einsum('rkgd,nkd->kgrn', query_heads, key_heads, preferred_element_ty...]
where the time goes in v5:
time: 290 us; the launch traced here: 287 us
  waiting for transfers between devices  105 us (36%)
  starting transfers between devices  67.6 us (23%)
  Pallas kernels  57.9 us (20%)
  other arithmetic  17.2 us (6%)
  between operations  14.6 us (5%)
  local copies, waits for them, and re-layouts  10.8 us (4%)
  matrix products  7.91 us (3%)
  loops' own time  5.76 us (2%)
    pallas_call x1, Pallas kernels, factor(): pl.pallas_call(factor_kernel, out_shape=(shape, shape), in_specs=[pl.Bloc...  57.9 us
    all_gather x1, waiting for transfers between devices, local(): lax.all_gather(exchange_gather(mine, 'x'), 'y', axis=0, tiled=True)  50.8 us
    ppermute x6, waiting for transfers between devices, exchange_sum(): partner = lax.ppermute(value, axis, [(i, i ^ step) for i in range(count)])  36.2 us
    ppermute x6, starting transfers between devices, exchange_sum(): partner = lax.ppermute(value, axis, [(i, i ^ step) for i in range(count)])  34.5 us
    ppermute x3, starting transfers between devices, exchange_gather(): partner = lax.ppermute(value, axis, [(i, i ^ step) for i in range(count)])  23 us
    ppermute x3, waiting for transfers between devices, exchange_gather(): partner = lax.ppermute(value, axis, [(i, i ^ step) for i in range(count)])  8.31 us
    all_to_all x1, starting transfers between devices, copy_for_each(): lax.all_to_all(jnp.broadcast_to(shard[None], (count, *shard.shape)), axis...  8.21 us
    reduce_or x8, other arithmetic, attend_block(): return lax.cond(jnp.any(seen), accumulate, unchanged, state_now)  7.76 us
  transfers between devices with their start and end apart: 12, of which 12 were waited for; matrix products, arithmetic and copies ran while one was open for 1% of the time, Pallas kernels for 0%

profile of v5, /device:TPU:14, one launch (start us, length us, event | category | flops | bytes accessed | tf_op | source)
XLA Modules:
  0.0 287.2 jit_solution(11149523901862021944)
XLA Ops:
  8.1 3.3 %collective-permute-start = (bf16[128,128]{1,0:T(8,128)(2,1)S(1)}, bf16[128,128]{1,0:T(8,128)(2,1)S(1)}, u32[]{:S(2)}, u32[]{:S(2)}) collective-permute-start(bf16[128,128]{1,0:T(8,128)(2,1)S(1)} %dynamic-slice_select_fusion), channel_id=1, source_target_pairs={{0,16},{16,0},{32,48},{48,32},{64,80},{80,64},{96,112},{112,96},{1... | collective-permute-start | bytes 98312 | tf_op jit(solution)/shard_map/ppermute | solution.py:121
  13.9 4.2 %collective-permute-start.1 = (bf16[256,128]{1,0:T(8,128)(2,1)S(1)}, bf16[256,128]{1,0:T(8,128)(2,1)S(1)}, u32[]{:S(2)}, u32[]{:S(2)}) collective-permute-start(bf16[256,128]{1,0:T(8,128)(2,1)S(1)} %pad_maximum_fusion.4), channel_id=1, source_target_pairs={{0,32},{16,48},{32,0},{48,16},{64,96},{80,112},{96,64},{112,80},{1... | collective-permute-start | bytes 196616 | tf_op jit(solution)/shard_map/ppermute | solution.py:121
  18.2 2.8 collective-permute-done.1
  21.0 15.5 %collective-permute-start.2 = (bf16[512,128]{1,0:T(8,128)(2,1)S(1)}, bf16[512,128]{1,0:T(8,128)(2,1)S(1)}, u32[]{:S(2)}, u32[]{:S(2)}) collective-permute-start(bf16[512,128]{1,0:T(8,128)(2,1)S(1)} %pad_maximum_fusion.3), channel_id=1, source_target_pairs={{0,64},{16,80},{32,96},{48,112},{64,0},{80,16},{96,32},{112,48},{1... | collective-permute-start | bytes 393224 | tf_op jit(solution)/shard_map/ppermute | solution.py:121
  36.5 3.0 %collective-permute-done.2 = bf16[512,128]{1,0:T(8,128)(2,1)S(1)} collective-permute-done((bf16[512,128]{1,0:T(8,128)(2,1)S(1)}, bf16[512,128]{1,0:T(8,128)(2,1)S(1)}, u32[]{:S(2)}, u32[]{:S(2)}) %collective-permute-start.2) | collective-permute-done | bytes 131104 | tf_op jit(solution)/shard_map/ppermute | solution.py:121
  40.3 50.8 %all-gather.2.cloned.1.call-done = bf16[8192,128]{1,0:T(8,128)(2,1)} async-done(((bf16[1024,128]{1,0:T(8,128)(2,1)}), bf16[8192,128]{1,0:T(8,128)(2,1)}) %all-gather.2.cloned.1.call-update) | async-done | bytes 2097168 | tf_op jit(solution)/shard_map/all_gather | solution.py:219
  94.1 3.4 %collective-permute-done.3 = bf16[8192,128]{1,0:T(8,128)(2,1)} collective-permute-done((bf16[8192,128]{1,0:T(8,128)(2,1)}, bf16[8192,128]{1,0:T(8,128)(2,1)}, u32[]{:S(2)}, u32[]{:S(2)}) %collective-permute-start.3) | collective-permute-done | bytes 2097184 | tf_op jit(solution)/shard_map/ppermute | solution.py:220
  97.6 3.8 %broadcast_select_fusion = (bf16[8192,128]{1,0:T(8,128)(2,1)S(1)}, bf16[8192,128]{1,0:T(8,128)(2,1)}) fusion(bf16[8192,128]{1,0:T(8,128)(2,1)} %collective-permute-done.3, bf16[8192,128]{1,0:T(8,128)(2,1)} %all-gather.2.cloned.1.call-done, pred[]{:T(512)S(6)} %eq.77), kind=kLoop, calls=%fused_computation.21 | loop fusion | flops 2097152 | bytes 8388609 | tf_op jit(solution)/shard_map/jit(_where)/select_n | solution.py:222
  101.4 20.6 %while.17 = (s32[]{:T(128)}, f32[1,4,128]{2,1,0:T(4,128)S(1)}, f32[1,4,128]{2,1,0:T(4,128)S(1)}, f32[1,4,128,128]{3,2,1,0:T(8,128)S(1)}, s32[8192]{0:T(1024)S(1)...) while((s32[]{:T(128)}, f32[1,4,128]{2,1,0:T(4,128)S(1)}, ...), condition=%wide.region_9.10_spmd, body=%wide.region_3.9_spmd.sunk | while | flops 272762368 | bytes 7792453 | solution.py:232
  123.1 8.2 %all-to-all-start = ((f32[16,1,128]{2,1,0:T(1,128)}), f32[16,1,128]{2,1,0:T(1,128)S(1)}, u32[]{:S(2)}, u32[]{:S(2)}) async-start(f32[16,1,128]{2,1,0:T(1,128)} %broadcast_in_dim.172), calls=%async_computation | async-start | bytes 16384 | tf_op jit(solution)/shard_map/all_to_all | solution.py:32
  132.2 6.6 %all-to-all-done = f32[16,1,128]{2,1,0:T(1,128)S(1)} async-done(((f32[16,1,128]{2,1,0:T(1,128)}), f32[16,1,128]{2,1,0:T(1,128)S(1)}, u32[]{:S(2)}, u32[]{:S(2)}) %all-to-all-start) | async-done | bytes 8224 | tf_op jit(solution)/shard_map/all_to_all | solution.py:32
  139.8 4.6 %copy.70 = f32[2,128,128]{0,2,1:T(8,128)} copy(f32[2,128,128]{2,1,0:T(8,128)S(1)} %get-tuple-element.354) | data formatting | bytes 262144 | tf_op jit(solution)/shard_map/slice | solution.py:88
  146.2 3.4 %collective-permute-start.4 = (f32[2,129,128]{2,1,0:T(8,128)S(1)}, f32[2,129,128]{2,1,0:T(8,128)S(1)}, u32[]{:S(2)}, u32[]{:S(2)}) collective-permute-start(f32[2,129,128]{2,1,0:T(8,128)S(1)} %pad_maximum_fusion.2), channel_id=1, source_target_pairs={{0,16},{16,0},{32,48},{48,32},{64,80},{80,64},{96,112},{112,96},{1... | collective-permute-start | bytes 396296 | tf_op jit(solution)/shard_map/ppermute | solution.py:110
  149.6 3.9 %collective-permute-done.4 = f32[2,129,128]{2,1,0:T(8,128)S(1)} collective-permute-done((f32[2,129,128]{2,1,0:T(8,128)S(1)}, f32[2,129,128]{2,1,0:T(8,128)S(1)}, u32[]{:S(2)}, u32[]{:S(2)}) %collective-permute-start.4) | collective-permute-done | bytes 132128 | tf_op jit(solution)/shard_map/ppermute | solution.py:110
  153.6 4.3 %collective-permute-start.5 = (f32[2,129,128]{2,1,0:T(8,128)S(1)}, f32[2,129,128]{2,1,0:T(8,128)S(1)}, u32[]{:S(2)}, u32[]{:S(2)}) collective-permute-start(f32[2,129,128]{2,1,0:T(8,128)S(1)} %fusion.18), channel_id=1, source_target_pairs={{0,32},{16,48},{32,0},{48,16},{64,96},{80,112},{96,64},{112,80},{1... | collective-permute-start | bytes 396296 | tf_op jit(solution)/shard_map/ppermute | solution.py:110
  157.9 6.1 %collective-permute-done.5 = f32[2,129,128]{2,1,0:T(8,128)S(1)} collective-permute-done((f32[2,129,128]{2,1,0:T(8,128)S(1)}, f32[2,129,128]{2,1,0:T(8,128)S(1)}, u32[]{:S(2)}, u32[]{:S(2)}) %collective-permute-start.5) | collective-permute-done | bytes 132128 | tf_op jit(solution)/shard_map/ppermute | solution.py:110
  164.0 16.8 %collective-permute-start.6 = (f32[2,129,128]{2,1,0:T(8,128)S(1)}, f32[2,129,128]{2,1,0:T(8,128)S(1)}, u32[]{:S(2)}, u32[]{:S(2)}) collective-permute-start(f32[2,129,128]{2,1,0:T(8,128)S(1)} %add.162), channel_id=1, source_target_pairs={{0,64},{16,80},{32,96},{48,112},{64,0},{80,16},{96,32},{112,48},{1... | collective-permute-start | bytes 396296 | tf_op jit(solution)/shard_map/ppermute | solution.py:110
  180.8 6.6 %collective-permute-done.6 = f32[2,129,128]{2,1,0:T(8,128)S(1)} collective-permute-done((f32[2,129,128]{2,1,0:T(8,128)S(1)}, f32[2,129,128]{2,1,0:T(8,128)S(1)}, u32[]{:S(2)}, u32[]{:S(2)}) %collective-permute-start.6) | collective-permute-done | bytes 132128 | tf_op jit(solution)/shard_map/ppermute | solution.py:110
  190.1 4.3 %collective-permute-done.7 = f32[2,129,128]{2,1,0:T(8,128)S(1)} collective-permute-done((f32[2,129,128]{2,1,0:T(8,128)S(1)}, f32[2,129,128]{2,1,0:T(8,128)S(1)}, u32[]{:S(2)}, u32[]{:S(2)}) %collective-permute-start.7) | collective-permute-done | bytes 132128 | tf_op jit(solution)/shard_map/ppermute | solution.py:110
  194.4 4.5 %collective-permute-start.8 = (f32[2,129,128]{2,1,0:T(8,128)S(1)}, f32[2,129,128]{2,1,0:T(8,128)S(1)}, u32[]{:S(2)}, u32[]{:S(2)}) collective-permute-start(f32[2,129,128]{2,1,0:T(8,128)S(1)} %add.164), channel_id=1, source_target_pairs={{0,256},{128,384},{256,0},{384,128},{512,768},{640,896},{768,512},... | collective-permute-start | bytes 396296 | tf_op jit(solution)/shard_map/ppermute | solution.py:110
  198.9 6.2 %collective-permute-done.8 = f32[2,129,128]{2,1,0:T(8,128)S(1)} collective-permute-done((f32[2,129,128]{2,1,0:T(8,128)S(1)}, f32[2,129,128]{2,1,0:T(8,128)S(1)}, u32[]{:S(2)}, u32[]{:S(2)}) %collective-permute-start.8) | collective-permute-done | bytes 132128 | tf_op jit(solution)/shard_map/ppermute | solution.py:110
  205.2 2.9 collective-permute-start.9
  208.1 9.1 %collective-permute-done.9 = f32[2,129,128]{2,1,0:T(8,128)S(1)} collective-permute-done((f32[2,129,128]{2,1,0:T(8,128)S(1)}, f32[2,129,128]{2,1,0:T(8,128)S(1)}, u32[]{:S(2)}, u32[]{:S(2)}) %collective-permute-start.9) | collective-permute-done | bytes 132128 | tf_op jit(solution)/shard_map/ppermute | solution.py:110
  218.6 57.9 %shard_map.94 = (f32[4,128,128]{2,1,0:T(8,128)}, f32[4,128,128]{2,1,0:T(8,128)}) custom-call(f32[4,128,128]{2,1,0:T(8,128)} %bitcast.90), custom_call_target="tpu_custom_call" | custom-call | tf_op jit(solution)/shard_map/pallas_call | solution.py:76
  (127 shorter events, 41.6 us)
Async XLA Ops:
  7.2 85.9 %copy-start.3 = (s32[1,64]{1,0:T(1,128)S(1)}, s32[1,64]{1,0:T(1,128)}, u32[]{:S(2)}) copy-start(s32[1,64]{1,0:T(1,128)} %param.17) | copy-start | bytes 772
  7.2 86.2 %copy-start.4 = (s32[1,64]{1,0:T(1,128)S(1)}, s32[1,64]{1,0:T(1,128)}, u32[]{:S(2)}) copy-start(s32[1,64]{1,0:T(1,128)} %param.16) | copy-start | bytes 772
  7.2 86.6 %copy-start.2 = (bf16[128,512]{1,0:T(8,128)(2,1)S(1)}, bf16[128,512]{1,0:T(8,128)(2,1)}, u32[]{:S(2)}) copy-start(bf16[128,512]{1,0:T(8,128)(2,1)} %param.11) | copy-start | bytes 393220
  7.2 84.0 %all-gather.2.cloned.1.call-start = ((), (), s32[]{:S(2)}) async-start(), calls=%async_computation.1 | async-start | bytes 2359296 | tf_op jit(solution)/shard_map/all_gather | solution.py:219
  8.1 5.8 %collective-permute-start = (bf16[128,128]{1,0:T(8,128)(2,1)S(1)}, bf16[128,128]{1,0:T(8,128)(2,1)S(1)}, u32[]{:S(2)}, u32[]{:S(2)}) collective-permute-start(bf16[128,128]{1,0:T(8,128)(2,1)S(1)} %dynamic-slice_select_fusion), channel_id=1, source_target_pairs={{0,16},{16,0},{32,48},{48,32},{64,80},{80,64},{96,112},{112,96},{1... | collective-permute-start | bytes 98312 | tf_op jit(solution)/shard_map/ppermute | solution.py:121
  13.9 7.1 %collective-permute-start.1 = (bf16[256,128]{1,0:T(8,128)(2,1)S(1)}, bf16[256,128]{1,0:T(8,128)(2,1)S(1)}, u32[]{:S(2)}, u32[]{:S(2)}) collective-permute-start(bf16[256,128]{1,0:T(8,128)(2,1)S(1)} %pad_maximum_fusion.4), channel_id=1, source_target_pairs={{0,32},{16,48},{32,0},{48,16},{64,96},{80,112},{96,64},{112,80},{1... | collective-permute-start | bytes 196616 | tf_op jit(solution)/shard_map/ppermute | solution.py:121
  21.0 18.5 %collective-permute-start.2 = (bf16[512,128]{1,0:T(8,128)(2,1)S(1)}, bf16[512,128]{1,0:T(8,128)(2,1)S(1)}, u32[]{:S(2)}, u32[]{:S(2)}) collective-permute-start(bf16[512,128]{1,0:T(8,128)(2,1)S(1)} %pad_maximum_fusion.3), channel_id=1, source_target_pairs={{0,64},{16,80},{32,96},{48,112},{64,0},{80,16},{96,32},{112,48},{1... | collective-permute-start | bytes 393224 | tf_op jit(solution)/shard_map/ppermute | solution.py:121
  91.2 6.4 %collective-permute-start.3 = (bf16[8192,128]{1,0:T(8,128)(2,1)}, bf16[8192,128]{1,0:T(8,128)(2,1)}, u32[]{:S(2)}, u32[]{:S(2)}) collective-permute-start(bf16[8192,128]{1,0:T(8,128)(2,1)} %all-gather.2.cloned.1.call-done), channel_id=1, source_target_pairs={{0,1},{1,0},{2,3},{3,2},{4,5},{5,4},{6,7},{7,6},{8,9},{9,8},{10,11... | collective-permute-start | bytes 6291464 | tf_op jit(solution)/shard_map/ppermute | solution.py:220
  101.4 20.9 %copy-start = (bf16[128,512]{1,0:T(8,128)(2,1)S(1)}, bf16[128,512]{1,0:T(8,128)(2,1)}, u32[]{:S(2)}) copy-start(bf16[128,512]{1,0:T(8,128)(2,1)} %param.14) | copy-start | bytes 393220
  122.4 22.0 %copy-start.1 = (bf16[128,512]{1,0:T(8,128)(2,1)}, bf16[128,512]{1,0:T(8,128)(2,1)S(1)}, u32[]{:S(2)}) copy-start(bf16[128,512]{1,0:T(8,128)(2,1)S(1)} %get-tuple-element.348) | copy-start | bytes 393220
  123.1 15.7 %all-to-all-start = ((f32[16,1,128]{2,1,0:T(1,128)}), f32[16,1,128]{2,1,0:T(1,128)S(1)}, u32[]{:S(2)}, u32[]{:S(2)}) async-start(f32[16,1,128]{2,1,0:T(1,128)} %broadcast_in_dim.172), calls=%async_computation | async-start | bytes 16384 | tf_op jit(solution)/shard_map/all_to_all | solution.py:32
  146.2 7.3 %collective-permute-start.4 = (f32[2,129,128]{2,1,0:T(8,128)S(1)}, f32[2,129,128]{2,1,0:T(8,128)S(1)}, u32[]{:S(2)}, u32[]{:S(2)}) collective-permute-start(f32[2,129,128]{2,1,0:T(8,128)S(1)} %pad_maximum_fusion.2), channel_id=1, source_target_pairs={{0,16},{16,0},{32,48},{48,32},{64,80},{80,64},{96,112},{112,96},{1... | collective-permute-start | bytes 396296 | tf_op jit(solution)/shard_map/ppermute | solution.py:110
  153.6 10.4 %collective-permute-start.5 = (f32[2,129,128]{2,1,0:T(8,128)S(1)}, f32[2,129,128]{2,1,0:T(8,128)S(1)}, u32[]{:S(2)}, u32[]{:S(2)}) collective-permute-start(f32[2,129,128]{2,1,0:T(8,128)S(1)} %fusion.18), channel_id=1, source_target_pairs={{0,32},{16,48},{32,0},{48,16},{64,96},{80,112},{96,64},{112,80},{1... | collective-permute-start | bytes 396296 | tf_op jit(solution)/shard_map/ppermute | solution.py:110
  164.0 23.4 %collective-permute-start.6 = (f32[2,129,128]{2,1,0:T(8,128)S(1)}, f32[2,129,128]{2,1,0:T(8,128)S(1)}, u32[]{:S(2)}, u32[]{:S(2)}) collective-permute-start(f32[2,129,128]{2,1,0:T(8,128)S(1)} %add.162), channel_id=1, source_target_pairs={{0,64},{16,80},{32,96},{48,112},{64,0},{80,16},{96,32},{112,48},{1... | collective-permute-start | bytes 396296 | tf_op jit(solution)/shard_map/ppermute | solution.py:110
  187.4 6.9 %collective-permute-start.7 = (f32[2,129,128]{2,1,0:T(8,128)S(1)}, f32[2,129,128]{2,1,0:T(8,128)S(1)}, u32[]{:S(2)}, u32[]{:S(2)}) collective-permute-start(f32[2,129,128]{2,1,0:T(8,128)S(1)} %add.163), channel_id=1, source_target_pairs={{0,128},{128,0},{256,384},{384,256},{512,640},{640,512},{768,896},... | collective-permute-start | bytes 396296 | tf_op jit(solution)/shard_map/ppermute | solution.py:110
  194.4 10.8 %collective-permute-start.8 = (f32[2,129,128]{2,1,0:T(8,128)S(1)}, f32[2,129,128]{2,1,0:T(8,128)S(1)}, u32[]{:S(2)}, u32[]{:S(2)}) collective-permute-start(f32[2,129,128]{2,1,0:T(8,128)S(1)} %add.164), channel_id=1, source_target_pairs={{0,256},{128,384},{256,0},{384,128},{512,768},{640,896},{768,512},... | collective-permute-start | bytes 396296 | tf_op jit(solution)/shard_map/ppermute | solution.py:110
  205.2 12.0 %collective-permute-start.9 = (f32[2,129,128]{2,1,0:T(8,128)S(1)}, f32[2,129,128]{2,1,0:T(8,128)S(1)}, u32[]{:S(2)}, u32[]{:S(2)}) collective-permute-start(f32[2,129,128]{2,1,0:T(8,128)S(1)} %add.165), channel_id=1, source_target_pairs={{0,512},{128,640},{256,768},{384,896},{512,0},{640,128},{768,256},... | collective-permute-start | bytes 396296 | tf_op jit(solution)/shard_map/ppermute | solution.py:110
Sparse Core Ops, SparseCore 0:
  40.5 50.6 all-gather.1

commit v6 on v5

--- a/solution.py
+++ b/solution.py
@@ -39,31 +39,47 @@
     return jnp.sum(everything, axis=0)
 
 
+PANEL = 16
+
+
 def factor_kernel(g_ref, u_ref, li_ref, m_ref):
     heads, n, _ = g_ref.shape
     row_ids = lax.broadcasted_iota(jnp.int32, (n, 1), 0)
     lane_ids = lax.broadcasted_iota(jnp.int32, (1, n), 1)
+    panel_rows = lax.broadcasted_iota(jnp.int32, (PANEL, 1), 0)
     eye = (lax.broadcasted_iota(jnp.int32, (n, n), 0) == lax.broadcasted_iota(jnp.int32, (n, n), 1)).astype(jnp.float32)
     for h in range(heads):
         m_ref[h, :, :n] = g_ref[h]
         m_ref[h, :, n:] = eye
     spare = jnp.zeros((8 - heads, n), jnp.float32)
 
-    def step(j, carry):
-        pick = lane_ids == j
-        below = row_ids > j
-        rows = [m_ref[h, pl.ds(j, 1), :] for h in range(heads)]
-        columns = jnp.transpose(jnp.concatenate([r[:, :n] for r in rows] + [spare], axis=0))
-        for h in range(heads):
-            pivot = jnp.sum(jnp.where(pick, rows[h][:, :n], 0.0), axis=1, keepdims=True)
-            scale = lax.rsqrt(pivot)
-            scaled = rows[h] * scale
-            column = jnp.where(below, columns[:, h : h + 1] * scale, 0.0)
-            m_ref[h] = m_ref[h] - column * scaled
-            m_ref[h, pl.ds(j, 1), :] = scaled
-        return carry
-
-    lax.fori_loop(0, n, step, 0)
+    for top in range(0, n, PANEL):
+
+        def step(offset, carry, top=top):
+            j = top + offset
+            pick = lane_ids == j
+            below = (panel_rows + top) > j
+            rows = [m_ref[h, pl.ds(j, 1), :] for h in range(heads)]
+            columns = jnp.transpose(jnp.concatenate([r[:, :n] for r in rows] + [spare], axis=0))
+            columns = columns[top : top + PANEL]
+            for h in range(heads):
+                pivot = jnp.sum(jnp.where(pick, rows[h][:, :n], 0.0), axis=1, keepdims=True)
+                scale = lax.rsqrt(pivot)
+                scaled = rows[h] * scale
+                column = jnp.where(below, columns[:, h : h + 1] * scale, 0.0)
+                block = m_ref[h, top : top + PANEL, :]
+                m_ref[h, top : top + PANEL, :] = block - column * scaled
+                m_ref[h, pl.ds(j, 1), :] = scaled
+            return carry
+
+        lax.fori_loop(0, PANEL, step, 0)
+        if top + PANEL < n:
+            for h in range(heads):
+                panel = m_ref[h, top : top + PANEL, :]
+                lead = jnp.where(row_ids >= top + PANEL, jnp.transpose(panel[:, :n]), 0.0)
+                m_ref[h] = m_ref[h] - jnp.dot(
+                    lead, panel, precision=lax.Precision.HIGHEST, preferred_element_type=jnp.float32
+                )
     upper = lax.broadcasted_iota(jnp.int32, (n, n), 0) <= lax.broadcasted_iota(jnp.int32, (n, n), 1)
     for h in range(heads):
         u_ref[h] = jnp.where(upper, m_ref[h, :, :n], 0.0)

time: 290 us -> 266 us (0.917)
  Pallas kernels: 57.9 us -> 35.9 us
    pallas_call x1, Pallas kernels: 57.9 us -> 35.9 us  [factor(): pl.pallas_call(factor_kernel, out_shape=(shape, shape), in_specs=[pl.Bloc...]
where the time goes in v6:
time: 266 us; the launch traced here: 264 us
  waiting for transfers between devices  105 us (39%)
  starting transfers between devices  67.2 us (25%)
  Pallas kernels  35.9 us (13%)
  other arithmetic  17.2 us (6%)
  between operations  14.6 us (5%)
  local copies, waits for them, and re-layouts  10.8 us (4%)
  matrix products  7.91 us (3%)
  loops' own time  5.76 us (2%)
    all_gather x1, waiting for transfers between devices, local(): lax.all_gather(exchange_gather(mine, 'x'), 'y', axis=0, tiled=True)  50.8 us
    ppermute x6, waiting for transfers between devices, exchange_sum(): partner = lax.ppermute(value, axis, [(i, i ^ step) for i in range(count)])  35.9 us
    pallas_call x1, Pallas kernels, factor(): pl.pallas_call(factor_kernel, out_shape=(shape, shape), in_specs=[pl.Bloc...  35.9 us
    ppermute x6, starting transfers between devices, exchange_sum(): partner = lax.ppermute(value, axis, [(i, i ^ step) for i in range(count)])  34 us
    ppermute x3, starting transfers between devices, exchange_gather(): partner = lax.ppermute(value, axis, [(i, i ^ step) for i in range(count)])  23 us
    ppermute x3, waiting for transfers between devices, exchange_gather(): partner = lax.ppermute(value, axis, [(i, i ^ step) for i in range(count)])  8.31 us
    all_to_all x1, starting transfers between devices, copy_for_each(): lax.all_to_all(jnp.broadcast_to(shard[None], (count, *shard.shape)), axis...  8.23 us
    reduce_or x8, other arithmetic, attend_block(): return lax.cond(jnp.any(seen), accumulate, unchanged, state_now)  7.76 us
  transfers between devices with their start and end apart: 12, of which 12 were waited for; matrix products, arithmetic and copies ran while one was open for 1% of the time, Pallas kernels for 0%

profile of v6, /device:TPU:14, one launch (start us, length us, event | category | flops | bytes accessed | tf_op | source)
XLA Modules:
  0.0 264.4 jit_solution(9627994631730155785)
XLA Ops:
  8.1 3.3 %collective-permute-start = (bf16[128,128]{1,0:T(8,128)(2,1)S(1)}, bf16[128,128]{1,0:T(8,128)(2,1)S(1)}, u32[]{:S(2)}, u32[]{:S(2)}) collective-permute-start(bf16[128,128]{1,0:T(8,128)(2,1)S(1)} %dynamic-slice_select_fusion), channel_id=1, source_target_pairs={{0,16},{16,0},{32,48},{48,32},{64,80},{80,64},{96,112},{112,96},{1... | collective-permute-start | bytes 98312 | tf_op jit(solution)/shard_map/ppermute | solution.py:137
  13.9 4.2 %collective-permute-start.1 = (bf16[256,128]{1,0:T(8,128)(2,1)S(1)}, bf16[256,128]{1,0:T(8,128)(2,1)S(1)}, u32[]{:S(2)}, u32[]{:S(2)}) collective-permute-start(bf16[256,128]{1,0:T(8,128)(2,1)S(1)} %pad_maximum_fusion.4), channel_id=1, source_target_pairs={{0,32},{16,48},{32,0},{48,16},{64,96},{80,112},{96,64},{112,80},{1... | collective-permute-start | bytes 196616 | tf_op jit(solution)/shard_map/ppermute | solution.py:137
  18.2 2.8 %collective-permute-done.1 = bf16[256,128]{1,0:T(8,128)(2,1)S(1)} collective-permute-done((bf16[256,128]{1,0:T(8,128)(2,1)S(1)}, bf16[256,128]{1,0:T(8,128)(2,1)S(1)}, u32[]{:S(2)}, u32[]{:S(2)}) %collective-permute-start.1) | collective-permute-done | bytes 65568 | tf_op jit(solution)/shard_map/ppermute | solution.py:137
  21.0 15.5 %collective-permute-start.2 = (bf16[512,128]{1,0:T(8,128)(2,1)S(1)}, bf16[512,128]{1,0:T(8,128)(2,1)S(1)}, u32[]{:S(2)}, u32[]{:S(2)}) collective-permute-start(bf16[512,128]{1,0:T(8,128)(2,1)S(1)} %pad_maximum_fusion.3), channel_id=1, source_target_pairs={{0,64},{16,80},{32,96},{48,112},{64,0},{80,16},{96,32},{112,48},{1... | collective-permute-start | bytes 393224 | tf_op jit(solution)/shard_map/ppermute | solution.py:137
  36.5 3.0 %collective-permute-done.2 = bf16[512,128]{1,0:T(8,128)(2,1)S(1)} collective-permute-done((bf16[512,128]{1,0:T(8,128)(2,1)S(1)}, bf16[512,128]{1,0:T(8,128)(2,1)S(1)}, u32[]{:S(2)}, u32[]{:S(2)}) %collective-permute-start.2) | collective-permute-done | bytes 131104 | tf_op jit(solution)/shard_map/ppermute | solution.py:137
  40.3 50.8 %all-gather.2.cloned.1.call-done = bf16[8192,128]{1,0:T(8,128)(2,1)} async-done(((bf16[1024,128]{1,0:T(8,128)(2,1)}), bf16[8192,128]{1,0:T(8,128)(2,1)}) %all-gather.2.cloned.1.call-update) | async-done | bytes 2097168 | tf_op jit(solution)/shard_map/all_gather | solution.py:235
  94.1 3.4 %collective-permute-done.3 = bf16[8192,128]{1,0:T(8,128)(2,1)} collective-permute-done((bf16[8192,128]{1,0:T(8,128)(2,1)}, bf16[8192,128]{1,0:T(8,128)(2,1)}, u32[]{:S(2)}, u32[]{:S(2)}) %collective-permute-start.3) | collective-permute-done | bytes 2097184 | tf_op jit(solution)/shard_map/ppermute | solution.py:236
  97.6 3.8 %broadcast_select_fusion = (bf16[8192,128]{1,0:T(8,128)(2,1)S(1)}, bf16[8192,128]{1,0:T(8,128)(2,1)}) fusion(bf16[8192,128]{1,0:T(8,128)(2,1)} %collective-permute-done.3, bf16[8192,128]{1,0:T(8,128)(2,1)} %all-gather.2.cloned.1.call-done, pred[]{:T(512)S(6)} %eq.77), kind=kLoop, calls=%fused_computation.21 | loop fusion | flops 2097152 | bytes 8388609 | tf_op jit(solution)/shard_map/jit(_where)/select_n | solution.py:238
  101.4 20.6 %while.17 = (s32[]{:T(128)}, f32[1,4,128]{2,1,0:T(4,128)S(1)}, f32[1,4,128]{2,1,0:T(4,128)S(1)}, f32[1,4,128,128]{3,2,1,0:T(8,128)S(1)}, s32[8192]{0:T(1024)S(1)...) while((s32[]{:T(128)}, f32[1,4,128]{2,1,0:T(4,128)S(1)}, ...), condition=%wide.region_9.10_spmd, body=%wide.region_3.9_spmd.sunk | while | flops 272762368 | bytes 7792453 | solution.py:248
  123.1 8.2 %all-to-all-start = ((f32[16,1,128]{2,1,0:T(1,128)}), f32[16,1,128]{2,1,0:T(1,128)S(1)}, u32[]{:S(2)}, u32[]{:S(2)}) async-start(f32[16,1,128]{2,1,0:T(1,128)} %broadcast_in_dim.172), calls=%async_computation | async-start | bytes 16384 | tf_op jit(solution)/shard_map/all_to_all | solution.py:32
  132.2 6.6 %all-to-all-done = f32[16,1,128]{2,1,0:T(1,128)S(1)} async-done(((f32[16,1,128]{2,1,0:T(1,128)}), f32[16,1,128]{2,1,0:T(1,128)S(1)}, u32[]{:S(2)}, u32[]{:S(2)}) %all-to-all-start) | async-done | bytes 8224 | tf_op jit(solution)/shard_map/all_to_all | solution.py:32
  139.8 4.6 %copy.70 = f32[2,128,128]{0,2,1:T(8,128)} copy(f32[2,128,128]{2,1,0:T(8,128)S(1)} %get-tuple-element.354) | data formatting | bytes 262144 | tf_op jit(solution)/shard_map/slice | solution.py:104
  146.3 8.0 %collective-permute-start.4 = (f32[2,129,128]{2,1,0:T(8,128)S(1)}, f32[2,129,128]{2,1,0:T(8,128)S(1)}, u32[]{:S(2)}, u32[]{:S(2)}) collective-permute-start(f32[2,129,128]{2,1,0:T(8,128)S(1)} %pad_maximum_fusion.2), channel_id=1, source_target_pairs={{0,16},{16,0},{32,48},{48,32},{64,80},{80,64},{96,112},{112,96},{1... | collective-permute-start | bytes 396296 | tf_op jit(solution)/shard_map/ppermute | solution.py:126
  154.3 3.7 %collective-permute-done.4 = f32[2,129,128]{2,1,0:T(8,128)S(1)} collective-permute-done((f32[2,129,128]{2,1,0:T(8,128)S(1)}, f32[2,129,128]{2,1,0:T(8,128)S(1)}, u32[]{:S(2)}, u32[]{:S(2)}) %collective-permute-start.4) | collective-permute-done | bytes 132128 | tf_op jit(solution)/shard_map/ppermute | solution.py:126
  158.0 6.6 %collective-permute-start.5 = (f32[2,129,128]{2,1,0:T(8,128)S(1)}, f32[2,129,128]{2,1,0:T(8,128)S(1)}, u32[]{:S(2)}, u32[]{:S(2)}) collective-permute-start(f32[2,129,128]{2,1,0:T(8,128)S(1)} %fusion.18), channel_id=1, source_target_pairs={{0,32},{16,48},{32,0},{48,16},{64,96},{80,112},{96,64},{112,80},{1... | collective-permute-start | bytes 396296 | tf_op jit(solution)/shard_map/ppermute | solution.py:126
  164.5 6.1 %collective-permute-done.5 = f32[2,129,128]{2,1,0:T(8,128)S(1)} collective-permute-done((f32[2,129,128]{2,1,0:T(8,128)S(1)}, f32[2,129,128]{2,1,0:T(8,128)S(1)}, u32[]{:S(2)}, u32[]{:S(2)}) %collective-permute-start.5) | collective-permute-done | bytes 132128 | tf_op jit(solution)/shard_map/ppermute | solution.py:126
  170.6 8.0 %collective-permute-start.6 = (f32[2,129,128]{2,1,0:T(8,128)S(1)}, f32[2,129,128]{2,1,0:T(8,128)S(1)}, u32[]{:S(2)}, u32[]{:S(2)}) collective-permute-start(f32[2,129,128]{2,1,0:T(8,128)S(1)} %add.162), channel_id=1, source_target_pairs={{0,64},{16,80},{32,96},{48,112},{64,0},{80,16},{96,32},{112,48},{1... | collective-permute-start | bytes 396296 | tf_op jit(solution)/shard_map/ppermute | solution.py:126
  178.6 6.7 %collective-permute-done.6 = f32[2,129,128]{2,1,0:T(8,128)S(1)} collective-permute-done((f32[2,129,128]{2,1,0:T(8,128)S(1)}, f32[2,129,128]{2,1,0:T(8,128)S(1)}, u32[]{:S(2)}, u32[]{:S(2)}) %collective-permute-start.6) | collective-permute-done | bytes 132128 | tf_op jit(solution)/shard_map/ppermute | solution.py:126
  187.3 5.0 %collective-permute-done.7 = f32[2,129,128]{2,1,0:T(8,128)S(1)} collective-permute-done((f32[2,129,128]{2,1,0:T(8,128)S(1)}, f32[2,129,128]{2,1,0:T(8,128)S(1)}, u32[]{:S(2)}, u32[]{:S(2)}) %collective-permute-start.7) | collective-permute-done | bytes 132128 | tf_op jit(solution)/shard_map/ppermute | solution.py:126
  192.4 5.5 %collective-permute-start.8 = (f32[2,129,128]{2,1,0:T(8,128)S(1)}, f32[2,129,128]{2,1,0:T(8,128)S(1)}, u32[]{:S(2)}, u32[]{:S(2)}) collective-permute-start(f32[2,129,128]{2,1,0:T(8,128)S(1)} %add.164), channel_id=1, source_target_pairs={{0,256},{128,384},{256,0},{384,128},{512,768},{640,896},{768,512},... | collective-permute-start | bytes 396296 | tf_op jit(solution)/shard_map/ppermute | solution.py:126
  197.9 5.6 %collective-permute-done.8 = f32[2,129,128]{2,1,0:T(8,128)S(1)} collective-permute-done((f32[2,129,128]{2,1,0:T(8,128)S(1)}, f32[2,129,128]{2,1,0:T(8,128)S(1)}, u32[]{:S(2)}, u32[]{:S(2)}) %collective-permute-start.8) | collective-permute-done | bytes 132128 | tf_op jit(solution)/shard_map/ppermute | solution.py:126
  203.5 4.0 %collective-permute-start.9 = (f32[2,129,128]{2,1,0:T(8,128)S(1)}, f32[2,129,128]{2,1,0:T(8,128)S(1)}, u32[]{:S(2)}, u32[]{:S(2)}) collective-permute-start(f32[2,129,128]{2,1,0:T(8,128)S(1)} %add.165), channel_id=1, source_target_pairs={{0,512},{128,640},{256,768},{384,896},{512,0},{640,128},{768,256},... | collective-permute-start | bytes 396296 | tf_op jit(solution)/shard_map/ppermute | solution.py:126
  207.6 8.8 %collective-permute-done.9 = f32[2,129,128]{2,1,0:T(8,128)S(1)} collective-permute-done((f32[2,129,128]{2,1,0:T(8,128)S(1)}, f32[2,129,128]{2,1,0:T(8,128)S(1)}, u32[]{:S(2)}, u32[]{:S(2)}) %collective-permute-start.9) | collective-permute-done | bytes 132128 | tf_op jit(solution)/shard_map/ppermute | solution.py:126
  217.8 35.9 %shard_map.94 = (f32[4,128,128]{2,1,0:T(8,128)}, f32[4,128,128]{2,1,0:T(8,128)}) custom-call(f32[4,128,128]{2,1,0:T(8,128)} %bitcast.90), custom_call_target="tpu_custom_call" | custom-call | tf_op jit(solution)/shard_map/pallas_call | solution.py:92
  (127 shorter events, 40.8 us)
Async XLA Ops:
  7.2 85.9 %copy-start.3 = (s32[1,64]{1,0:T(1,128)S(1)}, s32[1,64]{1,0:T(1,128)}, u32[]{:S(2)}) copy-start(s32[1,64]{1,0:T(1,128)} %param.17) | copy-start | bytes 772
  7.2 86.2 %copy-start.4 = (s32[1,64]{1,0:T(1,128)S(1)}, s32[1,64]{1,0:T(1,128)}, u32[]{:S(2)}) copy-start(s32[1,64]{1,0:T(1,128)} %param.16) | copy-start | bytes 772
  7.2 86.6 %copy-start.2 = (bf16[128,512]{1,0:T(8,128)(2,1)S(1)}, bf16[128,512]{1,0:T(8,128)(2,1)}, u32[]{:S(2)}) copy-start(bf16[128,512]{1,0:T(8,128)(2,1)} %param.11) | copy-start | bytes 393220
  7.2 84.0 %all-gather.2.cloned.1.call-start = ((), (), s32[]{:S(2)}) async-start(), calls=%async_computation.1 | async-start | bytes 2359296 | tf_op jit(solution)/shard_map/all_gather | solution.py:235
  8.1 5.8 %collective-permute-start = (bf16[128,128]{1,0:T(8,128)(2,1)S(1)}, bf16[128,128]{1,0:T(8,128)(2,1)S(1)}, u32[]{:S(2)}, u32[]{:S(2)}) collective-permute-start(bf16[128,128]{1,0:T(8,128)(2,1)S(1)} %dynamic-slice_select_fusion), channel_id=1, source_target_pairs={{0,16},{16,0},{32,48},{48,32},{64,80},{80,64},{96,112},{112,96},{1... | collective-permute-start | bytes 98312 | tf_op jit(solution)/shard_map/ppermute | solution.py:137
  13.9 7.1 %collective-permute-start.1 = (bf16[256,128]{1,0:T(8,128)(2,1)S(1)}, bf16[256,128]{1,0:T(8,128)(2,1)S(1)}, u32[]{:S(2)}, u32[]{:S(2)}) collective-permute-start(bf16[256,128]{1,0:T(8,128)(2,1)S(1)} %pad_maximum_fusion.4), channel_id=1, source_target_pairs={{0,32},{16,48},{32,0},{48,16},{64,96},{80,112},{96,64},{112,80},{1... | collective-permute-start | bytes 196616 | tf_op jit(solution)/shard_map/ppermute | solution.py:137
  21.0 18.5 %collective-permute-start.2 = (bf16[512,128]{1,0:T(8,128)(2,1)S(1)}, bf16[512,128]{1,0:T(8,128)(2,1)S(1)}, u32[]{:S(2)}, u32[]{:S(2)}) collective-permute-start(bf16[512,128]{1,0:T(8,128)(2,1)S(1)} %pad_maximum_fusion.3), channel_id=1, source_target_pairs={{0,64},{16,80},{32,96},{48,112},{64,0},{80,16},{96,32},{112,48},{1... | collective-permute-start | bytes 393224 | tf_op jit(solution)/shard_map/ppermute | solution.py:137
  91.2 6.4 %collective-permute-start.3 = (bf16[8192,128]{1,0:T(8,128)(2,1)}, bf16[8192,128]{1,0:T(8,128)(2,1)}, u32[]{:S(2)}, u32[]{:S(2)}) collective-permute-start(bf16[8192,128]{1,0:T(8,128)(2,1)} %all-gather.2.cloned.1.call-done), channel_id=1, source_target_pairs={{0,1},{1,0},{2,3},{3,2},{4,5},{5,4},{6,7},{7,6},{8,9},{9,8},{10,11... | collective-permute-start | bytes 6291464 | tf_op jit(solution)/shard_map/ppermute | solution.py:236
  101.4 20.9 %copy-start = (bf16[128,512]{1,0:T(8,128)(2,1)S(1)}, bf16[128,512]{1,0:T(8,128)(2,1)}, u32[]{:S(2)}) copy-start(bf16[128,512]{1,0:T(8,128)(2,1)} %param.14) | copy-start | bytes 393220
  122.4 22.0 %copy-start.1 = (bf16[128,512]{1,0:T(8,128)(2,1)}, bf16[128,512]{1,0:T(8,128)(2,1)S(1)}, u32[]{:S(2)}) copy-start(bf16[128,512]{1,0:T(8,128)(2,1)S(1)} %get-tuple-element.348) | copy-start | bytes 393220
  123.1 15.8 %all-to-all-start = ((f32[16,1,128]{2,1,0:T(1,128)}), f32[16,1,128]{2,1,0:T(1,128)S(1)}, u32[]{:S(2)}, u32[]{:S(2)}) async-start(f32[16,1,128]{2,1,0:T(1,128)} %broadcast_in_dim.172), calls=%async_computation | async-start | bytes 16384 | tf_op jit(solution)/shard_map/all_to_all | solution.py:32
  146.3 11.7 %collective-permute-start.4 = (f32[2,129,128]{2,1,0:T(8,128)S(1)}, f32[2,129,128]{2,1,0:T(8,128)S(1)}, u32[]{:S(2)}, u32[]{:S(2)}) collective-permute-start(f32[2,129,128]{2,1,0:T(8,128)S(1)} %pad_maximum_fusion.2), channel_id=1, source_target_pairs={{0,16},{16,0},{32,48},{48,32},{64,80},{80,64},{96,112},{112,96},{1... | collective-permute-start | bytes 396296 | tf_op jit(solution)/shard_map/ppermute | solution.py:126
  158.0 12.7 %collective-permute-start.5 = (f32[2,129,128]{2,1,0:T(8,128)S(1)}, f32[2,129,128]{2,1,0:T(8,128)S(1)}, u32[]{:S(2)}, u32[]{:S(2)}) collective-permute-start(f32[2,129,128]{2,1,0:T(8,128)S(1)} %fusion.18), channel_id=1, source_target_pairs={{0,32},{16,48},{32,0},{48,16},{64,96},{80,112},{96,64},{112,80},{1... | collective-permute-start | bytes 396296 | tf_op jit(solution)/shard_map/ppermute | solution.py:126
  170.6 14.7 %collective-permute-start.6 = (f32[2,129,128]{2,1,0:T(8,128)S(1)}, f32[2,129,128]{2,1,0:T(8,128)S(1)}, u32[]{:S(2)}, u32[]{:S(2)}) collective-permute-start(f32[2,129,128]{2,1,0:T(8,128)S(1)} %add.162), channel_id=1, source_target_pairs={{0,64},{16,80},{32,96},{48,112},{64,0},{80,16},{96,32},{112,48},{1... | collective-permute-start | bytes 396296 | tf_op jit(solution)/shard_map/ppermute | solution.py:126
  185.4 6.9 %collective-permute-start.7 = (f32[2,129,128]{2,1,0:T(8,128)S(1)}, f32[2,129,128]{2,1,0:T(8,128)S(1)}, u32[]{:S(2)}, u32[]{:S(2)}) collective-permute-start(f32[2,129,128]{2,1,0:T(8,128)S(1)} %add.163), channel_id=1, source_target_pairs={{0,128},{128,0},{256,384},{384,256},{512,640},{640,512},{768,896},... | collective-permute-start | bytes 396296 | tf_op jit(solution)/shard_map/ppermute | solution.py:126
  192.4 11.1 %collective-permute-start.8 = (f32[2,129,128]{2,1,0:T(8,128)S(1)}, f32[2,129,128]{2,1,0:T(8,128)S(1)}, u32[]{:S(2)}, u32[]{:S(2)}) collective-permute-start(f32[2,129,128]{2,1,0:T(8,128)S(1)} %add.164), channel_id=1, source_target_pairs={{0,256},{128,384},{256,0},{384,128},{512,768},{640,896},{768,512},... | collective-permute-start | bytes 396296 | tf_op jit(solution)/shard_map/ppermute | solution.py:126
  203.5 12.9 %collective-permute-start.9 = (f32[2,129,128]{2,1,0:T(8,128)S(1)}, f32[2,129,128]{2,1,0:T(8,128)S(1)}, u32[]{:S(2)}, u32[]{:S(2)}) collective-permute-start(f32[2,129,128]{2,1,0:T(8,128)S(1)} %add.165), channel_id=1, source_target_pairs={{0,512},{128,640},{256,768},{384,896},{512,0},{640,128},{768,256},... | collective-permute-start | bytes 396296 | tf_op jit(solution)/shard_map/ppermute | solution.py:126
Sparse Core Ops, SparseCore 0:
  40.5 50.6 all-gather.1

commit v7 on v6

--- a/solution.py
+++ b/solution.py
@@ -103,7 +103,8 @@
     upper = lax.broadcasted_iota(jnp.int32, (n, n), 0) <= lax.broadcasted_iota(jnp.int32, (n, n), 1)
     first, second = gram[0::2], gram[1::2]
     square = jnp.where(upper[None], first, second)
-    diagonal = jnp.diagonal(second, axis1=1, axis2=2)[:, None, :]
+    eye = lax.broadcasted_iota(jnp.int32, (n, n), 0) == lax.broadcasted_iota(jnp.int32, (n, n), 1)
+    diagonal = jnp.sum(jnp.where(eye[None], second, 0.0), axis=1, keepdims=True)
     return jnp.concatenate([square, diagonal], axis=1)
 
 

time: 266 us -> 286 us (1.075)
  waiting for transfers between devices: 105 us -> 130 us
  local copies, waits for them, and re-layouts: 10.8 us -> 4.53 us
  starting transfers between devices: 67.2 us -> 71.8 us
    ppermute x6, waiting for transfers between devices: 35.9 us -> 60.7 us  [exchange_sum(): partner = lax.ppermute(value, axis, [(i, i ^ step) for i in range(count)])]
    ppermute x6, starting transfers between devices: 34 us -> 38.6 us  [exchange_sum(): partner = lax.ppermute(value, axis, [(i, i ^ step) for i in range(count)])]
    slice x1, local copies, waits for them, and re-layouts: 4.62 us -> 0.09 us  [fold_pairs(): first, second = (gram[0::2], gram[1::2])]
where the time goes in v7:
time: 286 us; the launch traced here: 285 us
  waiting for transfers between devices  130 us (45%)
  starting transfers between devices  71.8 us (25%)
  Pallas kernels  35.9 us (13%)
  other arithmetic  16.9 us (6%)
  between operations  14.6 us (5%)
  matrix products  5.93 us (2%)
  loops' own time  5.74 us (2%)
  local copies, waits for them, and re-layouts  4.53 us (2%)
    ppermute x6, waiting for transfers between devices, exchange_sum(): partner = lax.ppermute(value, axis, [(i, i ^ step) for i in range(count)])  60.7 us
    all_gather x1, waiting for transfers between devices, local(): lax.all_gather(exchange_gather(mine, 'x'), 'y', axis=0, tiled=True)  50.8 us
    ppermute x6, starting transfers between devices, exchange_sum(): partner = lax.ppermute(value, axis, [(i, i ^ step) for i in range(count)])  38.6 us
    pallas_call x1, Pallas kernels, factor(): pl.pallas_call(factor_kernel, out_shape=(shape, shape), in_specs=[pl.Bloc...  35.9 us
    ppermute x3, starting transfers between devices, exchange_gather(): partner = lax.ppermute(value, axis, [(i, i ^ step) for i in range(count)])  23 us
    ppermute x3, waiting for transfers between devices, exchange_gather(): partner = lax.ppermute(value, axis, [(i, i ^ step) for i in range(count)])  8.31 us
    all_to_all x1, starting transfers between devices, copy_for_each(): lax.all_to_all(jnp.broadcast_to(shard[None], (count, *shard.shape)), axis...  8.22 us
    reduce_or x8, other arithmetic, attend_block(): return lax.cond(jnp.any(seen), accumulate, unchanged, state_now)  7.76 us
  transfers between devices with their start and end apart: 12, of which 12 were waited for; matrix products, arithmetic and copies ran while one was open for 1% of the time, Pallas kernels for 0%

profile of v7, /device:TPU:14, one launch (start us, length us, event | category | flops | bytes accessed | tf_op | source)
XLA Modules:
  0.0 285.5 jit_solution(6556656045336669287)
XLA Ops:
  8.1 3.3 %collective-permute-start = (bf16[128,128]{1,0:T(8,128)(2,1)S(1)}, bf16[128,128]{1,0:T(8,128)(2,1)S(1)}, u32[]{:S(2)}, u32[]{:S(2)}) collective-permute-start(bf16[128,128]{1,0:T(8,128)(2,1)S(1)} %dynamic-slice_select_fusion), channel_id=1, source_target_pairs={{0,16},{16,0},{32,48},{48,32},{64,80},{80,64},{96,112},{112,96},{1... | collective-permute-start | bytes 98312 | tf_op jit(solution)/shard_map/ppermute | solution.py:138
  11.4 2.5 collective-permute-done
  13.9 4.2 %collective-permute-start.1 = (bf16[256,128]{1,0:T(8,128)(2,1)S(1)}, bf16[256,128]{1,0:T(8,128)(2,1)S(1)}, u32[]{:S(2)}, u32[]{:S(2)}) collective-permute-start(bf16[256,128]{1,0:T(8,128)(2,1)S(1)} %pad_maximum_fusion.4), channel_id=1, source_target_pairs={{0,32},{16,48},{32,0},{48,16},{64,96},{80,112},{96,64},{112,80},{1... | collective-permute-start | bytes 196616 | tf_op jit(solution)/shard_map/ppermute | solution.py:138
  18.2 2.8 collective-permute-done.1
  21.0 15.5 %collective-permute-start.2 = (bf16[512,128]{1,0:T(8,128)(2,1)S(1)}, bf16[512,128]{1,0:T(8,128)(2,1)S(1)}, u32[]{:S(2)}, u32[]{:S(2)}) collective-permute-start(bf16[512,128]{1,0:T(8,128)(2,1)S(1)} %pad_maximum_fusion.3), channel_id=1, source_target_pairs={{0,64},{16,80},{32,96},{48,112},{64,0},{80,16},{96,32},{112,48},{1... | collective-permute-start | bytes 393224 | tf_op jit(solution)/shard_map/ppermute | solution.py:138
  36.5 3.0 %collective-permute-done.2 = bf16[512,128]{1,0:T(8,128)(2,1)S(1)} collective-permute-done((bf16[512,128]{1,0:T(8,128)(2,1)S(1)}, bf16[512,128]{1,0:T(8,128)(2,1)S(1)}, u32[]{:S(2)}, u32[]{:S(2)}) %collective-permute-start.2) | collective-permute-done | bytes 131104 | tf_op jit(solution)/shard_map/ppermute | solution.py:138
  40.3 50.8 %all-gather.2.cloned.1.call-done = bf16[8192,128]{1,0:T(8,128)(2,1)} async-done(((bf16[1024,128]{1,0:T(8,128)(2,1)}), bf16[8192,128]{1,0:T(8,128)(2,1)}) %all-gather.2.cloned.1.call-update) | async-done | bytes 2097168 | tf_op jit(solution)/shard_map/all_gather | solution.py:236
  94.1 3.4 %collective-permute-done.3 = bf16[8192,128]{1,0:T(8,128)(2,1)} collective-permute-done((bf16[8192,128]{1,0:T(8,128)(2,1)}, bf16[8192,128]{1,0:T(8,128)(2,1)}, u32[]{:S(2)}, u32[]{:S(2)}) %collective-permute-start.3) | collective-permute-done | bytes 2097184 | tf_op jit(solution)/shard_map/ppermute | solution.py:237
  97.6 3.8 %broadcast_select_fusion = (bf16[8192,128]{1,0:T(8,128)(2,1)S(1)}, bf16[8192,128]{1,0:T(8,128)(2,1)}) fusion(bf16[8192,128]{1,0:T(8,128)(2,1)} %collective-permute-done.3, bf16[8192,128]{1,0:T(8,128)(2,1)} %all-gather.2.cloned.1.call-done, pred[]{:T(512)S(6)} %eq.80), kind=kLoop, calls=%fused_computation.20 | loop fusion | flops 2097152 | bytes 8388609 | tf_op jit(solution)/shard_map/jit(_where)/select_n | solution.py:239
  101.5 18.2 %while.17 = (s32[]{:T(128)}, f32[1,4,128]{2,1,0:T(4,128)S(1)}, f32[1,4,128]{2,1,0:T(4,128)S(1)}, f32[1,4,128,128]{3,2,1,0:T(8,128)S(1)}, s32[8192]{0:T(1024)S(1)...) while((s32[]{:T(128)}, f32[1,4,128]{2,1,0:T(4,128)S(1)}, ...), condition=%wide.region_9.10_spmd, body=%wide.region_3.9_spmd.sunk | while | flops 272762368 | bytes 7792453 | solution.py:249
  110.6 2.3 conditional.2
  120.8 8.2 %all-to-all-start = ((f32[16,1,128]{2,1,0:T(1,128)}), f32[16,1,128]{2,1,0:T(1,128)S(1)}, u32[]{:S(2)}, u32[]{:S(2)}) async-start(f32[16,1,128]{2,1,0:T(1,128)} %broadcast_in_dim.175), calls=%async_computation | async-start | bytes 16384 | tf_op jit(solution)/shard_map/all_to_all | solution.py:32
  129.8 6.7 %all-to-all-done = f32[16,1,128]{2,1,0:T(1,128)S(1)} async-done(((f32[16,1,128]{2,1,0:T(1,128)}), f32[16,1,128]{2,1,0:T(1,128)S(1)}, u32[]{:S(2)}, u32[]{:S(2)}) %all-to-all-start) | async-done | bytes 8224 | tf_op jit(solution)/shard_map/all_to_all | solution.py:32
  137.9 17.3 %collective-permute-start.4 = (f32[2,129,128]{1,2,0:T(8,128)S(1)}, f32[2,129,128]{1,2,0:T(8,128)S(1)}, u32[]{:S(2)}, u32[]{:S(2)}) collective-permute-start(f32[2,129,128]{1,2,0:T(8,128)S(1)} %pad_maximum_fusion.1), channel_id=1, source_target_pairs={{0,16},{16,0},{32,48},{48,32},{64,80},{80,64},{96,112},{112,96},{1... | collective-permute-start | bytes 396296 | tf_op jit(solution)/shard_map/ppermute | solution.py:127
  155.2 6.3 %collective-permute-done.4 = f32[2,129,128]{1,2,0:T(8,128)S(1)} collective-permute-done((f32[2,129,128]{1,2,0:T(8,128)S(1)}, f32[2,129,128]{1,2,0:T(8,128)S(1)}, u32[]{:S(2)}, u32[]{:S(2)}) %collective-permute-start.4) | collective-permute-done | bytes 132128 | tf_op jit(solution)/shard_map/ppermute | solution.py:127
  161.5 4.5 %collective-permute-start.5 = (f32[2,129,128]{1,2,0:T(8,128)S(1)}, f32[2,129,128]{1,2,0:T(8,128)S(1)}, u32[]{:S(2)}, u32[]{:S(2)}) collective-permute-start(f32[2,129,128]{1,2,0:T(8,128)S(1)} %fusion.16), channel_id=1, source_target_pairs={{0,32},{16,48},{32,0},{48,16},{64,96},{80,112},{96,64},{112,80},{1... | collective-permute-start | bytes 396296 | tf_op jit(solution)/shard_map/ppermute | solution.py:127
  166.1 11.4 %collective-permute-done.5 = f32[2,129,128]{1,2,0:T(8,128)S(1)} collective-permute-done((f32[2,129,128]{1,2,0:T(8,128)S(1)}, f32[2,129,128]{1,2,0:T(8,128)S(1)}, u32[]{:S(2)}, u32[]{:S(2)}) %collective-permute-start.5) | collective-permute-done | bytes 132128 | tf_op jit(solution)/shard_map/ppermute | solution.py:127
  179.4 14.1 %collective-permute-done.6 = f32[2,129,128]{1,2,0:T(8,128)S(1)} collective-permute-done((f32[2,129,128]{1,2,0:T(8,128)S(1)}, f32[2,129,128]{1,2,0:T(8,128)S(1)}, u32[]{:S(2)}, u32[]{:S(2)}) %collective-permute-start.6) | collective-permute-done | bytes 132128 | tf_op jit(solution)/shard_map/ppermute | solution.py:127
  195.5 6.3 %collective-permute-done.7 = f32[2,129,128]{1,2,0:T(8,128)S(1)} collective-permute-done((f32[2,129,128]{1,2,0:T(8,128)S(1)}, f32[2,129,128]{1,2,0:T(8,128)S(1)}, u32[]{:S(2)}, u32[]{:S(2)}) %collective-permute-start.7) | collective-permute-done | bytes 132128 | tf_op jit(solution)/shard_map/ppermute | solution.py:127
  201.8 3.0 %collective-permute-start.8 = (f32[2,129,128]{1,2,0:T(8,128)S(1)}, f32[2,129,128]{1,2,0:T(8,128)S(1)}, u32[]{:S(2)}, u32[]{:S(2)}) collective-permute-start(f32[2,129,128]{1,2,0:T(8,128)S(1)} %add.160), channel_id=1, source_target_pairs={{0,256},{128,384},{256,0},{384,128},{512,768},{640,896},{768,512},... | collective-permute-start | bytes 396296 | tf_op jit(solution)/shard_map/ppermute | solution.py:127
  204.8 10.6 %collective-permute-done.8 = f32[2,129,128]{1,2,0:T(8,128)S(1)} collective-permute-done((f32[2,129,128]{1,2,0:T(8,128)S(1)}, f32[2,129,128]{1,2,0:T(8,128)S(1)}, u32[]{:S(2)}, u32[]{:S(2)}) %collective-permute-start.8) | collective-permute-done | bytes 132128 | tf_op jit(solution)/shard_map/ppermute | solution.py:127
  215.4 10.0 %collective-permute-start.9 = (f32[2,129,128]{1,2,0:T(8,128)S(1)}, f32[2,129,128]{1,2,0:T(8,128)S(1)}, u32[]{:S(2)}, u32[]{:S(2)}) collective-permute-start(f32[2,129,128]{1,2,0:T(8,128)S(1)} %add.161), channel_id=1, source_target_pairs={{0,512},{128,640},{256,768},{384,896},{512,0},{640,128},{768,256},... | collective-permute-start | bytes 396296 | tf_op jit(solution)/shard_map/ppermute | solution.py:127
  225.5 12.1 %collective-permute-done.9 = f32[2,129,128]{1,2,0:T(8,128)S(1)} collective-permute-done((f32[2,129,128]{1,2,0:T(8,128)S(1)}, f32[2,129,128]{1,2,0:T(8,128)S(1)}, u32[]{:S(2)}, u32[]{:S(2)}) %collective-permute-start.9) | collective-permute-done | bytes 132128 | tf_op jit(solution)/shard_map/ppermute | solution.py:127
  238.9 35.9 %shard_map.94 = (f32[4,128,128]{2,1,0:T(8,128)}, f32[4,128,128]{2,1,0:T(8,128)}) custom-call(f32[4,128,128]{2,1,0:T(8,128)} %bitcast.81), custom_call_target="tpu_custom_call" | custom-call | tf_op jit(solution)/shard_map/pallas_call | solution.py:92
  (118 shorter events, 31.7 us)
Async XLA Ops:
  7.2 85.9 %copy-start.3 = (s32[1,64]{1,0:T(1,128)S(1)}, s32[1,64]{1,0:T(1,128)}, u32[]{:S(2)}) copy-start(s32[1,64]{1,0:T(1,128)} %param.17) | copy-start | bytes 772
  7.2 86.2 %copy-start.4 = (s32[1,64]{1,0:T(1,128)S(1)}, s32[1,64]{1,0:T(1,128)}, u32[]{:S(2)}) copy-start(s32[1,64]{1,0:T(1,128)} %param.16) | copy-start | bytes 772
  7.2 86.6 %copy-start.2 = (bf16[128,512]{1,0:T(8,128)(2,1)S(1)}, bf16[128,512]{1,0:T(8,128)(2,1)}, u32[]{:S(2)}) copy-start(bf16[128,512]{1,0:T(8,128)(2,1)} %param.11) | copy-start | bytes 393220
  7.2 84.0 %all-gather.2.cloned.1.call-start = ((), (), s32[]{:S(2)}) async-start(), calls=%async_computation.1 | async-start | bytes 2359296 | tf_op jit(solution)/shard_map/all_gather | solution.py:236
  8.1 5.8 %collective-permute-start = (bf16[128,128]{1,0:T(8,128)(2,1)S(1)}, bf16[128,128]{1,0:T(8,128)(2,1)S(1)}, u32[]{:S(2)}, u32[]{:S(2)}) collective-permute-start(bf16[128,128]{1,0:T(8,128)(2,1)S(1)} %dynamic-slice_select_fusion), channel_id=1, source_target_pairs={{0,16},{16,0},{32,48},{48,32},{64,80},{80,64},{96,112},{112,96},{1... | collective-permute-start | bytes 98312 | tf_op jit(solution)/shard_map/ppermute | solution.py:138
  13.9 7.1 %collective-permute-start.1 = (bf16[256,128]{1,0:T(8,128)(2,1)S(1)}, bf16[256,128]{1,0:T(8,128)(2,1)S(1)}, u32[]{:S(2)}, u32[]{:S(2)}) collective-permute-start(bf16[256,128]{1,0:T(8,128)(2,1)S(1)} %pad_maximum_fusion.4), channel_id=1, source_target_pairs={{0,32},{16,48},{32,0},{48,16},{64,96},{80,112},{96,64},{112,80},{1... | collective-permute-start | bytes 196616 | tf_op jit(solution)/shard_map/ppermute | solution.py:138
  21.0 18.5 %collective-permute-start.2 = (bf16[512,128]{1,0:T(8,128)(2,1)S(1)}, bf16[512,128]{1,0:T(8,128)(2,1)S(1)}, u32[]{:S(2)}, u32[]{:S(2)}) collective-permute-start(bf16[512,128]{1,0:T(8,128)(2,1)S(1)} %pad_maximum_fusion.3), channel_id=1, source_target_pairs={{0,64},{16,80},{32,96},{48,112},{64,0},{80,16},{96,32},{112,48},{1... | collective-permute-start | bytes 393224 | tf_op jit(solution)/shard_map/ppermute | solution.py:138
  91.2 6.4 %collective-permute-start.3 = (bf16[8192,128]{1,0:T(8,128)(2,1)}, bf16[8192,128]{1,0:T(8,128)(2,1)}, u32[]{:S(2)}, u32[]{:S(2)}) collective-permute-start(bf16[8192,128]{1,0:T(8,128)(2,1)} %all-gather.2.cloned.1.call-done), channel_id=1, source_target_pairs={{0,1},{1,0},{2,3},{3,2},{4,5},{5,4},{6,7},{7,6},{8,9},{9,8},{10,11... | collective-permute-start | bytes 6291464 | tf_op jit(solution)/shard_map/ppermute | solution.py:237
  101.4 18.5 %copy-start = (bf16[128,512]{1,0:T(8,128)(2,1)S(1)}, bf16[128,512]{1,0:T(8,128)(2,1)}, u32[]{:S(2)}) copy-start(bf16[128,512]{1,0:T(8,128)(2,1)} %param.14) | copy-start | bytes 393220
  120.1 41.4 %copy-start.1 = (bf16[128,512]{1,0:T(8,128)(2,1)}, bf16[128,512]{1,0:T(8,128)(2,1)S(1)}, u32[]{:S(2)}) copy-start(bf16[128,512]{1,0:T(8,128)(2,1)S(1)} %get-tuple-element.348) | copy-start | bytes 393220
  120.8 15.8 %all-to-all-start = ((f32[16,1,128]{2,1,0:T(1,128)}), f32[16,1,128]{2,1,0:T(1,128)S(1)}, u32[]{:S(2)}, u32[]{:S(2)}) async-start(f32[16,1,128]{2,1,0:T(1,128)} %broadcast_in_dim.175), calls=%async_computation | async-start | bytes 16384 | tf_op jit(solution)/shard_map/all_to_all | solution.py:32
  137.9 23.6 %collective-permute-start.4 = (f32[2,129,128]{1,2,0:T(8,128)S(1)}, f32[2,129,128]{1,2,0:T(8,128)S(1)}, u32[]{:S(2)}, u32[]{:S(2)}) collective-permute-start(f32[2,129,128]{1,2,0:T(8,128)S(1)} %pad_maximum_fusion.1), channel_id=1, source_target_pairs={{0,16},{16,0},{32,48},{48,32},{64,80},{80,64},{96,112},{112,96},{1... | collective-permute-start | bytes 396296 | tf_op jit(solution)/shard_map/ppermute | solution.py:127
  161.5 15.9 %collective-permute-start.5 = (f32[2,129,128]{1,2,0:T(8,128)S(1)}, f32[2,129,128]{1,2,0:T(8,128)S(1)}, u32[]{:S(2)}, u32[]{:S(2)}) collective-permute-start(f32[2,129,128]{1,2,0:T(8,128)S(1)} %fusion.16), channel_id=1, source_target_pairs={{0,32},{16,48},{32,0},{48,16},{64,96},{80,112},{96,64},{112,80},{1... | collective-permute-start | bytes 396296 | tf_op jit(solution)/shard_map/ppermute | solution.py:127
  177.5 16.0 %collective-permute-start.6 = (f32[2,129,128]{1,2,0:T(8,128)S(1)}, f32[2,129,128]{1,2,0:T(8,128)S(1)}, u32[]{:S(2)}, u32[]{:S(2)}) collective-permute-start(f32[2,129,128]{1,2,0:T(8,128)S(1)} %add.158), channel_id=1, source_target_pairs={{0,64},{16,80},{32,96},{48,112},{64,0},{80,16},{96,32},{112,48},{1... | collective-permute-start | bytes 396296 | tf_op jit(solution)/shard_map/ppermute | solution.py:127
  193.5 8.3 %collective-permute-start.7 = (f32[2,129,128]{1,2,0:T(8,128)S(1)}, f32[2,129,128]{1,2,0:T(8,128)S(1)}, u32[]{:S(2)}, u32[]{:S(2)}) collective-permute-start(f32[2,129,128]{1,2,0:T(8,128)S(1)} %add.159), channel_id=1, source_target_pairs={{0,128},{128,0},{256,384},{384,256},{512,640},{640,512},{768,896},... | collective-permute-start | bytes 396296 | tf_op jit(solution)/shard_map/ppermute | solution.py:127
  201.8 13.5 %collective-permute-start.8 = (f32[2,129,128]{1,2,0:T(8,128)S(1)}, f32[2,129,128]{1,2,0:T(8,128)S(1)}, u32[]{:S(2)}, u32[]{:S(2)}) collective-permute-start(f32[2,129,128]{1,2,0:T(8,128)S(1)} %add.160), channel_id=1, source_target_pairs={{0,256},{128,384},{256,0},{384,128},{512,768},{640,896},{768,512},... | collective-permute-start | bytes 396296 | tf_op jit(solution)/shard_map/ppermute | solution.py:127
  215.4 22.1 %collective-permute-start.9 = (f32[2,129,128]{1,2,0:T(8,128)S(1)}, f32[2,129,128]{1,2,0:T(8,128)S(1)}, u32[]{:S(2)}, u32[]{:S(2)}) collective-permute-start(f32[2,129,128]{1,2,0:T(8,128)S(1)} %add.161), channel_id=1, source_target_pairs={{0,512},{128,640},{256,768},{384,896},{512,0},{640,128},{768,256},... | collective-permute-start | bytes 396296 | tf_op jit(solution)/shard_map/ppermute | solution.py:127
Sparse Core Ops, SparseCore 0:
  40.5 50.6 all-gather.1

commit v8 on v6

--- a/solution.py
+++ b/solution.py
@@ -39,7 +39,7 @@
     return jnp.sum(everything, axis=0)
 
 
-PANEL = 16
+PANEL = 32
 
 
 def factor_kernel(g_ref, u_ref, li_ref, m_ref):

time: 266 us -> 269 us (1.011)
    dot_general x3 -> x4, matrix products: 4.21 us -> 5.62 us  [accumulate(): jnp.einsum('rkgd,nkd->kgrn', query_heads, key_heads, preferred_element_ty...]
where the time goes in v8:
time: 269 us
  waiting for transfers between devices  106 us (39%)
  starting transfers between devices  67.6 us (25%)
  Pallas kernels  37.3 us (14%)
  other arithmetic  17.5 us (7%)
  between operations  14.6 us (5%)
  local copies, waits for them, and re-layouts  10.8 us (4%)
  matrix products  9.89 us (4%)
  loops' own time  5.79 us (2%)
    all_gather x1, waiting for transfers between devices, local(): lax.all_gather(exchange_gather(mine, 'x'), 'y', axis=0, tiled=True)  50.8 us
    pallas_call x1, Pallas kernels, factor(): pl.pallas_call(factor_kernel, out_shape=(shape, shape), in_specs=[pl.Bloc...  37.3 us
    ppermute x6, waiting for transfers between devices, exchange_sum(): partner = lax.ppermute(value, axis, [(i, i ^ step) for i in range(count)])  36.3 us
    ppermute x6, starting transfers between devices, exchange_sum(): partner = lax.ppermute(value, axis, [(i, i ^ step) for i in range(count)])  34.4 us
    ppermute x3, starting transfers between devices, exchange_gather(): partner = lax.ppermute(value, axis, [(i, i ^ step) for i in range(count)])  23 us
    ppermute x3, waiting for transfers between devices, exchange_gather(): partner = lax.ppermute(value, axis, [(i, i ^ step) for i in range(count)])  8.31 us
    all_to_all x1, starting transfers between devices, copy_for_each(): lax.all_to_all(jnp.broadcast_to(shard[None], (count, *shard.shape)), axis...  8.21 us
    reduce_or x8, other arithmetic, attend_block(): return lax.cond(jnp.any(seen), accumulate, unchanged, state_now)  7.76 us
  transfers between devices with their start and end apart: 12, of which 12 were waited for; matrix products, arithmetic and copies ran while one was open for 1% of the time, Pallas kernels for 0%

profile of v8, /device:TPU:14, one launch (start us, length us, event | category | flops | bytes accessed | tf_op | source)
XLA Modules:
  0.0 268.9 jit_solution(2129806309586953127)
XLA Ops:
  8.1 3.3 %collective-permute-start = (bf16[128,128]{1,0:T(8,128)(2,1)S(1)}, bf16[128,128]{1,0:T(8,128)(2,1)S(1)}, u32[]{:S(2)}, u32[]{:S(2)}) collective-permute-start(bf16[128,128]{1,0:T(8,128)(2,1)S(1)} %dynamic-slice_select_fusion), channel_id=1, source_target_pairs={{0,16},{16,0},{32,48},{48,32},{64,80},{80,64},{96,112},{112,96},{1... | collective-permute-start | bytes 98312 | tf_op jit(solution)/shard_map/ppermute | solution.py:137
  13.9 4.2 %collective-permute-start.1 = (bf16[256,128]{1,0:T(8,128)(2,1)S(1)}, bf16[256,128]{1,0:T(8,128)(2,1)S(1)}, u32[]{:S(2)}, u32[]{:S(2)}) collective-permute-start(bf16[256,128]{1,0:T(8,128)(2,1)S(1)} %pad_maximum_fusion.4), channel_id=1, source_target_pairs={{0,32},{16,48},{32,0},{48,16},{64,96},{80,112},{96,64},{112,80},{1... | collective-permute-start | bytes 196616 | tf_op jit(solution)/shard_map/ppermute | solution.py:137
  18.2 2.8 %collective-permute-done.1 = bf16[256,128]{1,0:T(8,128)(2,1)S(1)} collective-permute-done((bf16[256,128]{1,0:T(8,128)(2,1)S(1)}, bf16[256,128]{1,0:T(8,128)(2,1)S(1)}, u32[]{:S(2)}, u32[]{:S(2)}) %collective-permute-start.1) | collective-permute-done | bytes 65568 | tf_op jit(solution)/shard_map/ppermute | solution.py:137
  21.0 15.5 %collective-permute-start.2 = (bf16[512,128]{1,0:T(8,128)(2,1)S(1)}, bf16[512,128]{1,0:T(8,128)(2,1)S(1)}, u32[]{:S(2)}, u32[]{:S(2)}) collective-permute-start(bf16[512,128]{1,0:T(8,128)(2,1)S(1)} %pad_maximum_fusion.3), channel_id=1, source_target_pairs={{0,64},{16,80},{32,96},{48,112},{64,0},{80,16},{96,32},{112,48},{1... | collective-permute-start | bytes 393224 | tf_op jit(solution)/shard_map/ppermute | solution.py:137
  36.5 3.0 %collective-permute-done.2 = bf16[512,128]{1,0:T(8,128)(2,1)S(1)} collective-permute-done((bf16[512,128]{1,0:T(8,128)(2,1)S(1)}, bf16[512,128]{1,0:T(8,128)(2,1)S(1)}, u32[]{:S(2)}, u32[]{:S(2)}) %collective-permute-start.2) | collective-permute-done | bytes 131104 | tf_op jit(solution)/shard_map/ppermute | solution.py:137
  40.3 50.8 %all-gather.2.cloned.1.call-done = bf16[8192,128]{1,0:T(8,128)(2,1)} async-done(((bf16[1024,128]{1,0:T(8,128)(2,1)}), bf16[8192,128]{1,0:T(8,128)(2,1)}) %all-gather.2.cloned.1.call-update) | async-done | bytes 2097168 | tf_op jit(solution)/shard_map/all_gather | solution.py:235
  94.1 3.4 %collective-permute-done.3 = bf16[8192,128]{1,0:T(8,128)(2,1)} collective-permute-done((bf16[8192,128]{1,0:T(8,128)(2,1)}, bf16[8192,128]{1,0:T(8,128)(2,1)}, u32[]{:S(2)}, u32[]{:S(2)}) %collective-permute-start.3) | collective-permute-done | bytes 2097184 | tf_op jit(solution)/shard_map/ppermute | solution.py:236
  97.6 3.8 %broadcast_select_fusion = (bf16[8192,128]{1,0:T(8,128)(2,1)S(1)}, bf16[8192,128]{1,0:T(8,128)(2,1)}) fusion(bf16[8192,128]{1,0:T(8,128)(2,1)} %collective-permute-done.3, bf16[8192,128]{1,0:T(8,128)(2,1)} %all-gather.2.cloned.1.call-done, pred[]{:T(512)S(6)} %eq.77), kind=kLoop, calls=%fused_computation.21 | loop fusion | flops 2097152 | bytes 8388609 | tf_op jit(solution)/shard_map/jit(_where)/select_n | solution.py:238
  101.4 22.9 %while.17 = (s32[]{:T(128)}, f32[1,4,128]{2,1,0:T(4,128)S(1)}, f32[1,4,128]{2,1,0:T(4,128)S(1)}, f32[1,4,128,128]{3,2,1,0:T(8,128)S(1)}, s32[8192]{0:T(1024)S(1)...) while((s32[]{:T(128)}, f32[1,4,128]{2,1,0:T(4,128)S(1)}, ...), condition=%wide.region_9.10_spmd, body=%wide.region_3.9_spmd.sunk | while | flops 272762368 | bytes 7792453 | solution.py:248
  125.4 8.2 %all-to-all-start = ((f32[16,1,128]{2,1,0:T(1,128)}), f32[16,1,128]{2,1,0:T(1,128)S(1)}, u32[]{:S(2)}, u32[]{:S(2)}) async-start(f32[16,1,128]{2,1,0:T(1,128)} %broadcast_in_dim.172), calls=%async_computation | async-start | bytes 16384 | tf_op jit(solution)/shard_map/all_to_all | solution.py:32
  134.5 6.6 %all-to-all-done = f32[16,1,128]{2,1,0:T(1,128)S(1)} async-done(((f32[16,1,128]{2,1,0:T(1,128)}), f32[16,1,128]{2,1,0:T(1,128)S(1)}, u32[]{:S(2)}, u32[]{:S(2)}) %all-to-all-start) | async-done | bytes 8224 | tf_op jit(solution)/shard_map/all_to_all | solution.py:32
  142.1 4.6 %copy.70 = f32[2,128,128]{0,2,1:T(8,128)} copy(f32[2,128,128]{2,1,0:T(8,128)S(1)} %get-tuple-element.354) | data formatting | bytes 262144 | tf_op jit(solution)/shard_map/slice | solution.py:104
  148.6 3.4 %collective-permute-start.4 = (f32[2,129,128]{2,1,0:T(8,128)S(1)}, f32[2,129,128]{2,1,0:T(8,128)S(1)}, u32[]{:S(2)}, u32[]{:S(2)}) collective-permute-start(f32[2,129,128]{2,1,0:T(8,128)S(1)} %pad_maximum_fusion.2), channel_id=1, source_target_pairs={{0,16},{16,0},{32,48},{48,32},{64,80},{80,64},{96,112},{112,96},{1... | collective-permute-start | bytes 396296 | tf_op jit(solution)/shard_map/ppermute | solution.py:126
  152.0 3.9 %collective-permute-done.4 = f32[2,129,128]{2,1,0:T(8,128)S(1)} collective-permute-done((f32[2,129,128]{2,1,0:T(8,128)S(1)}, f32[2,129,128]{2,1,0:T(8,128)S(1)}, u32[]{:S(2)}, u32[]{:S(2)}) %collective-permute-start.4) | collective-permute-done | bytes 132128 | tf_op jit(solution)/shard_map/ppermute | solution.py:126
  155.9 13.5 %collective-permute-start.5 = (f32[2,129,128]{2,1,0:T(8,128)S(1)}, f32[2,129,128]{2,1,0:T(8,128)S(1)}, u32[]{:S(2)}, u32[]{:S(2)}) collective-permute-start(f32[2,129,128]{2,1,0:T(8,128)S(1)} %fusion.18), channel_id=1, source_target_pairs={{0,32},{16,48},{32,0},{48,16},{64,96},{80,112},{96,64},{112,80},{1... | collective-permute-start | bytes 396296 | tf_op jit(solution)/shard_map/ppermute | solution.py:126
  169.5 5.8 %collective-permute-done.5 = f32[2,129,128]{2,1,0:T(8,128)S(1)} collective-permute-done((f32[2,129,128]{2,1,0:T(8,128)S(1)}, f32[2,129,128]{2,1,0:T(8,128)S(1)}, u32[]{:S(2)}, u32[]{:S(2)}) %collective-permute-start.5) | collective-permute-done | bytes 132128 | tf_op jit(solution)/shard_map/ppermute | solution.py:126
  175.3 4.5 %collective-permute-start.6 = (f32[2,129,128]{2,1,0:T(8,128)S(1)}, f32[2,129,128]{2,1,0:T(8,128)S(1)}, u32[]{:S(2)}, u32[]{:S(2)}) collective-permute-start(f32[2,129,128]{2,1,0:T(8,128)S(1)} %add.162), channel_id=1, source_target_pairs={{0,64},{16,80},{32,96},{48,112},{64,0},{80,16},{96,32},{112,48},{1... | collective-permute-start | bytes 396296 | tf_op jit(solution)/shard_map/ppermute | solution.py:126
  179.8 8.3 %collective-permute-done.6 = f32[2,129,128]{2,1,0:T(8,128)S(1)} collective-permute-done((f32[2,129,128]{2,1,0:T(8,128)S(1)}, f32[2,129,128]{2,1,0:T(8,128)S(1)}, u32[]{:S(2)}, u32[]{:S(2)}) %collective-permute-start.6) | collective-permute-done | bytes 132128 | tf_op jit(solution)/shard_map/ppermute | solution.py:126
  188.2 4.1 %collective-permute-start.7 = (f32[2,129,128]{2,1,0:T(8,128)S(1)}, f32[2,129,128]{2,1,0:T(8,128)S(1)}, u32[]{:S(2)}, u32[]{:S(2)}) collective-permute-start(f32[2,129,128]{2,1,0:T(8,128)S(1)} %add.163), channel_id=1, source_target_pairs={{0,128},{128,0},{256,384},{384,256},{512,640},{640,512},{768,896},... | collective-permute-start | bytes 396296 | tf_op jit(solution)/shard_map/ppermute | solution.py:126
  192.3 3.2 %collective-permute-done.7 = f32[2,129,128]{2,1,0:T(8,128)S(1)} collective-permute-done((f32[2,129,128]{2,1,0:T(8,128)S(1)}, f32[2,129,128]{2,1,0:T(8,128)S(1)}, u32[]{:S(2)}, u32[]{:S(2)}) %collective-permute-start.7) | collective-permute-done | bytes 132128 | tf_op jit(solution)/shard_map/ppermute | solution.py:126
  197.5 8.2 %collective-permute-done.8 = f32[2,129,128]{2,1,0:T(8,128)S(1)} collective-permute-done((f32[2,129,128]{2,1,0:T(8,128)S(1)}, f32[2,129,128]{2,1,0:T(8,128)S(1)}, u32[]{:S(2)}, u32[]{:S(2)}) %collective-permute-start.8) | collective-permute-done | bytes 132128 | tf_op jit(solution)/shard_map/ppermute | solution.py:126
  205.7 6.9 %collective-permute-start.9 = (f32[2,129,128]{2,1,0:T(8,128)S(1)}, f32[2,129,128]{2,1,0:T(8,128)S(1)}, u32[]{:S(2)}, u32[]{:S(2)}) collective-permute-start(f32[2,129,128]{2,1,0:T(8,128)S(1)} %add.165), channel_id=1, source_target_pairs={{0,512},{128,640},{256,768},{384,896},{512,0},{640,128},{768,256},... | collective-permute-start | bytes 396296 | tf_op jit(solution)/shard_map/ppermute | solution.py:126
  212.7 6.8 %collective-permute-done.9 = f32[2,129,128]{2,1,0:T(8,128)S(1)} collective-permute-done((f32[2,129,128]{2,1,0:T(8,128)S(1)}, f32[2,129,128]{2,1,0:T(8,128)S(1)}, u32[]{:S(2)}, u32[]{:S(2)}) %collective-permute-start.9) | collective-permute-done | bytes 132128 | tf_op jit(solution)/shard_map/ppermute | solution.py:126
  220.9 37.3 %shard_map.94 = (f32[4,128,128]{2,1,0:T(8,128)}, f32[4,128,128]{2,1,0:T(8,128)}) custom-call(f32[4,128,128]{2,1,0:T(8,128)} %bitcast.90), custom_call_target="tpu_custom_call" | custom-call | tf_op jit(solution)/shard_map/pallas_call | solution.py:92
  (133 shorter events, 45.4 us)
Async XLA Ops:
  7.2 85.9 %copy-start.3 = (s32[1,64]{1,0:T(1,128)S(1)}, s32[1,64]{1,0:T(1,128)}, u32[]{:S(2)}) copy-start(s32[1,64]{1,0:T(1,128)} %param.17) | copy-start | bytes 772
  7.2 86.2 %copy-start.4 = (s32[1,64]{1,0:T(1,128)S(1)}, s32[1,64]{1,0:T(1,128)}, u32[]{:S(2)}) copy-start(s32[1,64]{1,0:T(1,128)} %param.16) | copy-start | bytes 772
  7.2 86.6 %copy-start.2 = (bf16[128,512]{1,0:T(8,128)(2,1)S(1)}, bf16[128,512]{1,0:T(8,128)(2,1)}, u32[]{:S(2)}) copy-start(bf16[128,512]{1,0:T(8,128)(2,1)} %param.11) | copy-start | bytes 393220
  7.2 84.0 %all-gather.2.cloned.1.call-start = ((), (), s32[]{:S(2)}) async-start(), calls=%async_computation.1 | async-start | bytes 2359296 | tf_op jit(solution)/shard_map/all_gather | solution.py:235
  8.1 5.8 %collective-permute-start = (bf16[128,128]{1,0:T(8,128)(2,1)S(1)}, bf16[128,128]{1,0:T(8,128)(2,1)S(1)}, u32[]{:S(2)}, u32[]{:S(2)}) collective-permute-start(bf16[128,128]{1,0:T(8,128)(2,1)S(1)} %dynamic-slice_select_fusion), channel_id=1, source_target_pairs={{0,16},{16,0},{32,48},{48,32},{64,80},{80,64},{96,112},{112,96},{1... | collective-permute-start | bytes 98312 | tf_op jit(solution)/shard_map/ppermute | solution.py:137
  13.9 7.1 %collective-permute-start.1 = (bf16[256,128]{1,0:T(8,128)(2,1)S(1)}, bf16[256,128]{1,0:T(8,128)(2,1)S(1)}, u32[]{:S(2)}, u32[]{:S(2)}) collective-permute-start(bf16[256,128]{1,0:T(8,128)(2,1)S(1)} %pad_maximum_fusion.4), channel_id=1, source_target_pairs={{0,32},{16,48},{32,0},{48,16},{64,96},{80,112},{96,64},{112,80},{1... | collective-permute-start | bytes 196616 | tf_op jit(solution)/shard_map/ppermute | solution.py:137
  21.0 18.5 %collective-permute-start.2 = (bf16[512,128]{1,0:T(8,128)(2,1)S(1)}, bf16[512,128]{1,0:T(8,128)(2,1)S(1)}, u32[]{:S(2)}, u32[]{:S(2)}) collective-permute-start(bf16[512,128]{1,0:T(8,128)(2,1)S(1)} %pad_maximum_fusion.3), channel_id=1, source_target_pairs={{0,64},{16,80},{32,96},{48,112},{64,0},{80,16},{96,32},{112,48},{1... | collective-permute-start | bytes 393224 | tf_op jit(solution)/shard_map/ppermute | solution.py:137
  91.2 6.4 %collective-permute-start.3 = (bf16[8192,128]{1,0:T(8,128)(2,1)}, bf16[8192,128]{1,0:T(8,128)(2,1)}, u32[]{:S(2)}, u32[]{:S(2)}) collective-permute-start(bf16[8192,128]{1,0:T(8,128)(2,1)} %all-gather.2.cloned.1.call-done), channel_id=1, source_target_pairs={{0,1},{1,0},{2,3},{3,2},{4,5},{5,4},{6,7},{7,6},{8,9},{9,8},{10,11... | collective-permute-start | bytes 6291464 | tf_op jit(solution)/shard_map/ppermute | solution.py:236
  101.4 23.2 %copy-start = (bf16[128,512]{1,0:T(8,128)(2,1)S(1)}, bf16[128,512]{1,0:T(8,128)(2,1)}, u32[]{:S(2)}) copy-start(bf16[128,512]{1,0:T(8,128)(2,1)} %param.14) | copy-start | bytes 393220
  124.7 22.0 %copy-start.1 = (bf16[128,512]{1,0:T(8,128)(2,1)}, bf16[128,512]{1,0:T(8,128)(2,1)S(1)}, u32[]{:S(2)}) copy-start(bf16[128,512]{1,0:T(8,128)(2,1)S(1)} %get-tuple-element.348) | copy-start | bytes 393220
  125.4 15.7 %all-to-all-start = ((f32[16,1,128]{2,1,0:T(1,128)}), f32[16,1,128]{2,1,0:T(1,128)S(1)}, u32[]{:S(2)}, u32[]{:S(2)}) async-start(f32[16,1,128]{2,1,0:T(1,128)} %broadcast_in_dim.172), calls=%async_computation | async-start | bytes 16384 | tf_op jit(solution)/shard_map/all_to_all | solution.py:32
  148.6 7.3 %collective-permute-start.4 = (f32[2,129,128]{2,1,0:T(8,128)S(1)}, f32[2,129,128]{2,1,0:T(8,128)S(1)}, u32[]{:S(2)}, u32[]{:S(2)}) collective-permute-start(f32[2,129,128]{2,1,0:T(8,128)S(1)} %pad_maximum_fusion.2), channel_id=1, source_target_pairs={{0,16},{16,0},{32,48},{48,32},{64,80},{80,64},{96,112},{112,96},{1... | collective-permute-start | bytes 396296 | tf_op jit(solution)/shard_map/ppermute | solution.py:126
  155.9 19.3 %collective-permute-start.5 = (f32[2,129,128]{2,1,0:T(8,128)S(1)}, f32[2,129,128]{2,1,0:T(8,128)S(1)}, u32[]{:S(2)}, u32[]{:S(2)}) collective-permute-start(f32[2,129,128]{2,1,0:T(8,128)S(1)} %fusion.18), channel_id=1, source_target_pairs={{0,32},{16,48},{32,0},{48,16},{64,96},{80,112},{96,64},{112,80},{1... | collective-permute-start | bytes 396296 | tf_op jit(solution)/shard_map/ppermute | solution.py:126
  175.3 12.9 %collective-permute-start.6 = (f32[2,129,128]{2,1,0:T(8,128)S(1)}, f32[2,129,128]{2,1,0:T(8,128)S(1)}, u32[]{:S(2)}, u32[]{:S(2)}) collective-permute-start(f32[2,129,128]{2,1,0:T(8,128)S(1)} %add.162), channel_id=1, source_target_pairs={{0,64},{16,80},{32,96},{48,112},{64,0},{80,16},{96,32},{112,48},{1... | collective-permute-start | bytes 396296 | tf_op jit(solution)/shard_map/ppermute | solution.py:126
  188.2 7.3 %collective-permute-start.7 = (f32[2,129,128]{2,1,0:T(8,128)S(1)}, f32[2,129,128]{2,1,0:T(8,128)S(1)}, u32[]{:S(2)}, u32[]{:S(2)}) collective-permute-start(f32[2,129,128]{2,1,0:T(8,128)S(1)} %add.163), channel_id=1, source_target_pairs={{0,128},{128,0},{256,384},{384,256},{512,640},{640,512},{768,896},... | collective-permute-start | bytes 396296 | tf_op jit(solution)/shard_map/ppermute | solution.py:126
  195.5 10.2 %collective-permute-start.8 = (f32[2,129,128]{2,1,0:T(8,128)S(1)}, f32[2,129,128]{2,1,0:T(8,128)S(1)}, u32[]{:S(2)}, u32[]{:S(2)}) collective-permute-start(f32[2,129,128]{2,1,0:T(8,128)S(1)} %add.164), channel_id=1, source_target_pairs={{0,256},{128,384},{256,0},{384,128},{512,768},{640,896},{768,512},... | collective-permute-start | bytes 396296 | tf_op jit(solution)/shard_map/ppermute | solution.py:126
  205.7 13.8 %collective-permute-start.9 = (f32[2,129,128]{2,1,0:T(8,128)S(1)}, f32[2,129,128]{2,1,0:T(8,128)S(1)}, u32[]{:S(2)}, u32[]{:S(2)}) collective-permute-start(f32[2,129,128]{2,1,0:T(8,128)S(1)} %add.165), channel_id=1, source_target_pairs={{0,512},{128,640},{256,768},{384,896},{512,0},{640,128},{768,256},... | collective-permute-start | bytes 396296 | tf_op jit(solution)/shard_map/ppermute | solution.py:126
Sparse Core Ops, SparseCore 0:
  40.5 50.6 all-gather.1
